TPU v7x, 256 devices: a whole 4x4x8 slice. The times are simulated.
256 devices in a mesh: grp: 16 (over y, x_lo, core), tm: 16 (over z, x_hi).
Axes of the slice: x: 4 (x_hi: 2, x_lo: 2; x = x_hi * 2 + x_lo), y: 4, z: 8, core: 2. Of those that a mesh axis runs over, the one named last changes fastest.
Arguments:
- motion: bfloat16 [1024, 128, 1024], P(('grp', 'tm')), may hold values from -30 to 30
- modulation: float32 [6, 1024], replicated, may hold values from -1.25 to 1.25
- w_temporal_qkv: bfloat16 [1024, 3072], replicated, may hold values from -1 to 1
- w_temporal_out: bfloat16 [1024, 1024], replicated, may hold values from -0.1875 to 0.1875
- w_inter_qkv: bfloat16 [1024, 3072], P('tm'), may hold values from -1 to 1
- w_inter_out: bfloat16 [1024, 1024], P('tm'), may hold values from -0.1875 to 0.1875
- links: int32 [16, 4], replicated, may hold values from 0 to 1, as said below
Outputs:
- motion_out: bfloat16 [1024, 128, 1024], P(('grp', 'tm'))
Inputs may be any that keep to these rules, and one draw needn't show every extreme that they name: Every group has between 1 and 4 links; one group has all of them and another exactly one.
All inputs are finite; a program needn't handle non-finite values.
Results may differ from a plain program's by a relative error of at most 0.008.
Values may be sent and summed in bfloat16 or wider, within the bound.
No kernel may reach another device: no remote copies, remote signals or barrier semaphores. Data moves between devices by JAX's collectives and lax.ppermute only.
A program may use at most 128 MiB of HBM per device.

v0:
```python
import jax
import jax.numpy as jnp
from jax import lax
from jax.sharding import PartitionSpec as P

HEAD = 64
REACH = 2


EPSILON = 1e-06


def from_behind(block, axis, distance):
    devices = range(lax.axis_size(axis))
    route = [((i - distance) % len(devices), i) for i in devices]
    return lax.ppermute(block, axis, route)


def modulate(field, modulation, first, second):
    values = field.astype(jnp.float32)
    mean_square = jnp.mean(values * values, axis=-1, keepdims=True)
    scaled = (
        values * lax.rsqrt(mean_square + EPSILON) * (1.0 + modulation[second]) + modulation[first]
    )
    return scaled.astype(jnp.bfloat16)


def softmax_rows(scores):
    row_top = jnp.max(scores, axis=-1, keepdims=True)
    weights = jnp.exp(scores - row_top)
    return (weights / jnp.sum(weights, axis=-1, keepdims=True)).astype(jnp.bfloat16)


def temporal_heads(char_items, qkv_weight):
    item_count, frame_count, feature_width = char_items.shape
    head_count = feature_width // HEAD
    packed = jnp.dot(
        char_items.reshape(item_count * frame_count, feature_width),
        qkv_weight,
        preferred_element_type=jnp.float32,
    )
    packed = packed.astype(jnp.bfloat16).reshape(item_count, frame_count, 3, head_count, HEAD)
    scores = jnp.einsum(
        "nfhd,nghd->nhfg", packed[:, :, 0], packed[:, :, 1], preferred_element_type=jnp.float32
    ) * HEAD ** (-0.5)
    weights = softmax_rows(scores)
    mixed_heads = jnp.einsum(
        "nhfg,nghd->nfhd", weights, packed[:, :, 2], preferred_element_type=jnp.float32
    )
    return mixed_heads.astype(jnp.bfloat16).reshape(item_count, frame_count, feature_width)


def per_device(motion, modulation, w_temporal_qkv, w_temporal_out, w_inter_qkv, w_inter_out, links):
    own_chars, all_frames, feature_width = motion.shape
    head_count = feature_width // HEAD
    inter_qkv, inter_out = (
        lax.all_gather(w_inter_qkv, "tm", axis=0, tiled=True),
        lax.all_gather(w_inter_out, "tm", axis=0, tiled=True),
    )
    normed = modulate(motion, modulation, 0, 1)
    t_mixed = temporal_heads(normed, w_temporal_qkv)
    t_projected = jnp.dot(
        t_mixed.reshape(own_chars * all_frames, feature_width),
        w_temporal_out,
        preferred_element_type=jnp.float32,
    )
    middle = (
        motion.astype(jnp.float32)
        + modulation[2] * t_projected.reshape(own_chars, all_frames, feature_width)
    ).astype(jnp.bfloat16)
    middle_frames = lax.all_to_all(middle, "tm", split_axis=1, concat_axis=0, tiled=True)
    char_count, frame_count, unused_width = middle_frames.shape
    token_count = char_count * frame_count
    normed_inter = modulate(middle_frames, modulation, 3, 4)
    packed = jnp.dot(
        normed_inter.reshape(token_count, feature_width),
        inter_qkv,
        preferred_element_type=jnp.float32,
    )
    packed = packed.astype(jnp.bfloat16).reshape(char_count, frame_count, 3 * feature_width)
    own_pairs = packed[:, :, feature_width:]
    neighbours = []
    current = own_pairs
    for step in range(REACH):
        current = from_behind(current, "grp", -1)
        neighbours.append(current)
    current = own_pairs
    for step in range(REACH):
        current = from_behind(current, "grp", 1)
        neighbours.append(current)
    stacked = jnp.concatenate([own_pairs] + neighbours, axis=0)
    queries = packed[:, :, :feature_width].reshape(char_count, frame_count, head_count, HEAD)
    key_part = stacked[:, :, :feature_width].reshape(-1, frame_count, head_count, HEAD)
    value_part = stacked[:, :, feature_width:].reshape(-1, frame_count, head_count, HEAD)
    scores = jnp.einsum(
        "cfhd,kfhd->fhck", queries, key_part, preferred_element_type=jnp.float32
    ) * HEAD ** (-0.5)
    group_ids = jnp.arange(links.shape[0], dtype=jnp.int32)
    own_links = jnp.sum(jnp.where(group_ids[:, None] == lax.axis_index("grp"), links, 0), axis=0)
    allowed = jnp.concatenate([jnp.ones((1,), jnp.int32), own_links])
    key_mask = jnp.repeat(allowed, char_count) > 0
    scores = jnp.where(key_mask, scores, -jnp.inf)
    weights = softmax_rows(scores)
    mixed_heads = jnp.einsum(
        "fhck,kfhd->cfhd", weights, value_part, preferred_element_type=jnp.float32
    ).astype(jnp.bfloat16)
    mixed_chars = lax.all_to_all(
        mixed_heads.reshape(char_count, frame_count, feature_width),
        "tm",
        split_axis=0,
        concat_axis=1,
        tiled=True,
    )
    result = jnp.dot(
        mixed_chars.reshape(own_chars * all_frames, feature_width),
        inter_out,
        preferred_element_type=jnp.float32,
    )
    total = middle.astype(jnp.float32) + modulation[5] * result.reshape(
        own_chars, all_frames, feature_width
    )
    return total.astype(jnp.bfloat16)


def solution(mesh):
    placed = (P(("grp", "tm"), None, None), P(), P(), P(), P("tm", None), P("tm", None), P())
    return jax.shard_map(
        per_device,
        mesh=mesh,
        in_specs=placed,
        out_specs=P(("grp", "tm"), None, None),
        check_vma=False,
    )
```

profile of v0, /device:TPU:8, one launch (start us, length us, event | category | flops | bytes accessed | tf_op | source)
XLA Modules:
  0.0 351.2 jit_solution(12227734614028227783)
XLA Ops:
  6.5 0.0 copy-start
  6.5 0.0 all-gather.3.cloned.1.call-start
  6.5 0.7 all-gather.3.cloned.1.call-update
  7.3 0.0 all-gather.5.cloned.1.call-start
  7.3 1.5 fusion.14
  8.8 1.0 fusion.53
  9.8 1.6 fusion.17
  11.4 7.6 %convolution_convert_fusion.1 = bf16[512,3072]{1,0:T(8,128)(2,1)} fusion(bf16[512,1024]{1,0:T(8,128)(2,1)S(1)} %bitcast.66, bf16[1024,3072]{1,0:T(8,128)(2,1)} %param.9), kind=kOutput, calls=%fused_computation.11 | convolution fusion | flops 3222798336 | bytes 10485760 | tf_op jit(solution)/shard_map/dot_general | solution.py:37
  19.0 8.6 %reshape.111 = bf16[4,128,3,16,64]{4,3,2,1,0:T(8,128)(2,1)} reshape(bf16[512,3072]{1,0:T(8,128)(2,1)} %convolution_convert_fusion.1) | data formatting | bytes 6291456 | tf_op jit(solution)/shard_map/reshape | solution.py:42
  27.6 6.1 %fusion.51 = (bf16[4,128,1,16,64]{4,3,2,1,0:T(8,128)(2,1)}, bf16[4,128,1,16,64]{4,3,2,1,0:T(8,128)(2,1)}, bf16[4,128,1,16,64]{4,3,2,1,0:T(8,128)(2,1)}) fusion(bf16[4,128,3,16,64]{4,3,2,1,0:T(8,128)(2,1)} %reshape.111), kind=kLoop, calls=%fused_computation.67 | loop fusion | bytes 6291456 | tf_op jit(solution)/shard_map/slice | solution.py:48
  33.7 2.8 copy.62
  36.5 3.5 %copy.63 = bf16[4,128,1,16,64]{1,4,3,0,2:T(8,128)(2,1)} copy(bf16[4,128,1,16,64]{4,3,2,1,0:T(8,128)(2,1)} %get-tuple-element.9) | data formatting | bytes 2097152
  40.1 3.5 %copy.61 = bf16[4,128,1,16,64]{1,4,3,0,2:T(8,128)(2,1)} copy(bf16[4,128,1,16,64]{4,3,2,1,0:T(8,128)(2,1)} %get-tuple-element.7) | data formatting | bytes 2097152
  43.6 2.0 fusion.42
  45.6 0.0 copy-start.5
  45.6 4.0 %fusion.54 = (f32[4,16,128]{2,1,0:T(8,128)S(1)}, f32[4,16,128,128]{2,3,1,0:T(8,128)S(1)}) fusion(f32[4,16,128,128]{2,3,1,0:T(8,128)S(1)} %fusion.42), kind=kOutput, calls=%fused_computation.70 | output fusion | flops 4194431 | bytes 8421376 | tf_op jit(solution)/shard_map/sub | solution.py:30
  49.6 0.0 copy-done.5
  49.6 0.0 copy-start.2
  49.7 0.7 fusion.40
  50.4 0.0 copy-done
  50.4 0.5 copy-done.2
  50.9 1.3 fusion.18
  52.2 0.8 copy.48
  53.0 48.1 %all_to_all.24 = bf16[4,128,1024]{2,0,1:T(4,128)(2,1)S(1)} all-to-all(bf16[4,128,1024]{2,0,1:T(4,128)(2,1)S(1)} %copy.48), channel_id=1, replica_groups=mesh['grp'=16,'tm'=16] {'tm'}, dimensions={1} | all-to-all | bytes 2097152 | tf_op jit(solution)/shard_map/all_to_all | solution.py:71
  101.1 0.4 convert_bitcast_fusion
  101.4 1.5 copy.50
  102.9 0.4 fusion.13
  103.3 0.1 reshape.107
  103.4 0.1 rsqrt.21
  103.5 1.9 fusion.23
  105.4 33.5 %all-gather.3.cloned.1.call-done = bf16[1024,3072]{1,0:T(8,128)(2,1)} async-done(((bf16[64,3072]{1,0:T(8,128)(2,1)}), bf16[1024,3072]{1,0:T(8,128)(2,1)}) %all-gather.3.cloned.1.call-update) | async-done | bytes 6291472 | tf_op jit(solution)/shard_map/all_gather | solution.py:57
  139.0 6.4 %fusion.7 = bf16[64,8,3072]{2,1,0:T(8,128)(2,1)S(1)} fusion(bf16[512,1024]{1,0:T(8,128)(2,1)S(1)} %fusion.23, bf16[1024,3072]{1,0:T(8,128)(2,1)} %all-gather.3.cloned.1.call-done), kind=kOutput, calls=%fused_computation.14 | convolution fusion | flops 3222798336 | bytes 10485760 | tf_op jit(solution)/shard_map/dot_general | solution.py:75
  145.4 1.7 copy-done.3
  147.1 1.9 fusion.52
  149.0 0.0 collective-permute-start
  149.0 0.5 collective-permute-start.2
  149.5 45.5 %collective-permute-done = bf16[64,8,2048]{2,1,0:T(8,128)(2,1)} collective-permute-done((bf16[64,8,2048]{2,1,0:T(8,128)(2,1)S(1)}, bf16[64,8,2048]{2,1,0:T(8,128)(2,1)}, u32[]{:S(2)}, u32[]{:S(2)}) %collective-permute-start) | collective-permute-done | bytes 2097184 | tf_op jit(solution)/shard_map/ppermute | solution.py:16
  195.0 2.9 collective-permute-start.1
  197.9 0.0 collective-permute-done.2
  197.9 0.0 collective-permute-start.3
  197.9 0.0 all-gather.5.cloned.1.call-update
  198.0 0.1 select_reduce_fusion
  198.1 0.1 add_compare_fusion
  198.2 0.1 broadcast_in_dim.34
  198.2 0.1 gt.12
  198.3 1.3 slice.57
  199.6 2.5 reshape.99
  202.2 3.1 constant_dynamic-update-slice_fusion.3
  205.3 39.4 %collective-permute-done.1 = bf16[64,8,2048]{2,1,0:T(8,128)(2,1)} collective-permute-done((bf16[64,8,2048]{2,1,0:T(8,128)(2,1)}, bf16[64,8,2048]{2,1,0:T(8,128)(2,1)}, u32[]{:S(2)}, u32[]{:S(2)}) %collective-permute-start.1) | collective-permute-done | bytes 2097184 | tf_op jit(solution)/shard_map/ppermute | solution.py:16
  244.8 3.2 constant_dynamic-update-slice_fusion.2
  247.9 3.2 constant_dynamic-update-slice_fusion.1
  251.1 0.0 collective-permute-done.3
  251.1 3.2 constant_dynamic-update-slice_fusion
  254.3 9.3 %fusion.50 = (bf16[320,8,1024]{2,1,0:T(8,128)(2,1)}, bf16[320,8,1024]{2,1,0:T(8,128)(2,1)}) fusion(bf16[320,8,2048]{2,1,0:T(8,128)(2,1)} %constant_dynamic-update-slice_fusion), kind=kLoop, calls=%fused_computation.66 | loop fusion | bytes 20971520 | tf_op jit(solution)/shard_map/slice | solution.py:93
  263.6 8.7 %copy.53 = bf16[320,8,1024]{0,2,1:T(8,128)(2,1)} copy(bf16[320,8,1024]{2,1,0:T(8,128)(2,1)} %get-tuple-element.5) | data formatting | bytes 10485760 | tf_op jit(solution)/shard_map/slice | solution.py:93
  272.3 12.4 %fusion.55 = (f32[8,16,64]{2,1,0:T(8,128)S(1)}, f32[8,16,64,320]{3,2,1,0:T(8,128)}) fusion(pred[320]{0:T(512)(128)(4,1)S(1)} %gt.12, bf16[320,8,16,64]{0,3,2,1:T(8,128)(2,1)} %bitcast.63, bf16[64,8,16,64]{3,2,1,0:T(8,128)(2,1)S(1)} %copy-done.4), kind=kOutput, calls=%fused_computation.71 | convolution fusion | flops 346030400 | bytes 16810304 | tf_op jit(solution)/shard_map/sub | solution.py:30
  284.7 8.5 %copy.52 = bf16[320,8,1024]{0,2,1:T(8,128)(2,1)} copy(bf16[320,8,1024]{2,1,0:T(8,128)(2,1)} %get-tuple-element.6) | data formatting | bytes 10485760 | tf_op jit(solution)/shard_map/slice | solution.py:94
  293.2 8.8 %fusion.28 = bf16[8,16,64,64]{3,2,1,0:T(8,128)(2,1)S(1)} fusion(bf16[320,8,16,64]{0,3,2,1:T(8,128)(2,1)} %bitcast.64, f32[8,16,64,320]{3,2,1,0:T(8,128)} %get-tuple-element.21, f32[8,16,64]{2,1,0:T(8,128)S(1)} %get-tuple-element.20), kind=kOutput, calls=%fused_computation.40 | convolution fusion | flops 341311488 | bytes 16809984 | tf_op jit(solution)/shard_map/fhck,kfhd->cfhd/dot_general | solution.py:104
  302.0 2.4 copy.55
  304.3 4.8 %all-to-all-start.1 = ((bf16[64,8,1024]{2,1,0:T(8,128)(2,1)}), bf16[64,8,1024]{2,1,0:T(8,128)(2,1)}, u32[]{:S(2)}, u32[]{:S(2)}) async-start(bf16[64,8,1024]{2,1,0:T(8,128)(2,1)} %copy.55), calls=%async_computation.1 | async-start | bytes 2097152 | tf_op jit(solution)/shard_map/all_to_all | solution.py:107
  309.2 0.0 copy-start.1
  309.2 0.0 all-gather.5.cloned.1.call-done
  309.2 31.0 %all-to-all-done.1 = bf16[64,8,1024]{2,1,0:T(8,128)(2,1)} async-done(((bf16[64,8,1024]{2,1,0:T(8,128)(2,1)}), bf16[64,8,1024]{2,1,0:T(8,128)(2,1)}, u32[]{:S(2)}, u32[]{:S(2)}) %all-to-all-start.1) | async-done | bytes 1048608 | tf_op jit(solution)/shard_map/all_to_all | solution.py:107
  340.2 4.1 %add_convert_fusion = bf16[4,128,1024]{2,1,0:T(8,128)(2,1)} fusion(bf16[4,128,1024]{2,1,0:T(8,128)(2,1)S(1)} %fusion.18, bf16[1024,1024]{1,0:T(8,128)(2,1)} %all-gather.5.cloned.1.call-done, bf16[4,16,8,1024]{3,2,0,1:T(8,128)(2,1)} %bitcast.23, f32[1024]{0:T(1024)S(1)} %bitcast.72), kind=kOutput, calls=%fused_computation.37 | convolution fusion | flops 1075838976 | bytes 5246976 | tf_op jit(solution)/shard_map/dot_general | solution.py:114
  (10 shorter events, 0.0 us)
Async XLA Ops:
  6.5 43.8 %copy-start = (bf16[1024,1024]{1,0:T(8,128)(2,1)S(1)}, bf16[1024,1024]{1,0:T(8,128)(2,1)}, u32[]{:S(2)}) copy-start(bf16[1024,1024]{1,0:T(8,128)(2,1)} %param.10) | copy-start | bytes 6291460
  6.5 132.4 %all-gather.3.cloned.1.call-start = ((), (), s32[]{:S(2)}) async-start(), calls=%async_computation.2 | async-start | bytes 6684672 | tf_op jit(solution)/shard_map/all_gather | solution.py:57
  7.3 302.0 %all-gather.5.cloned.1.call-start = ((), (), s32[]{:S(2)}) async-start(), calls=%async_computation.3 | async-start | bytes 2228224 | tf_op jit(solution)/shard_map/all_gather | solution.py:58
  45.6 4.0 %copy-start.5 = (bf16[4,128,1,16,64]{1,4,3,0,2:T(8,128)(2,1)S(1)}, bf16[4,128,1,16,64]{1,4,3,0,2:T(8,128)(2,1)}, u32[]{:S(2)}) copy-start(bf16[4,128,1,16,64]{1,4,3,0,2:T(8,128)(2,1)} %copy.61) | copy-start | bytes 3145732
  49.6 1.2 copy-start.2
  145.4 1.7 copy-start.3
  147.1 50.9 %copy-start.6 = (s32[16,4]{0,1:T(4,128)S(1)}, s32[16,4]{0,1:T(4,128)}, u32[]{:S(2)}) copy-start(s32[16,4]{0,1:T(4,128)} %param.13) | copy-start | bytes 772
  149.0 46.0 %collective-permute-start = (bf16[64,8,2048]{2,1,0:T(8,128)(2,1)S(1)}, bf16[64,8,2048]{2,1,0:T(8,128)(2,1)}, u32[]{:S(2)}, u32[]{:S(2)}) collective-permute-start(bf16[64,8,2048]{2,1,0:T(8,128)(2,1)S(1)} %get-tuple-element.10), channel_id=1, source_target_pairs={{16,0},{32,16},{48,32},{64,48},{80,64},{96,80},{112,96},{128,112},... | collective-permute-start | bytes 6291464 | tf_op jit(solution)/shard_map/ppermute | solution.py:16
  149.0 48.9 %collective-permute-start.2 = (bf16[64,8,2048]{2,1,0:T(8,128)(2,1)S(1)}, bf16[64,8,2048]{2,1,0:T(8,128)(2,1)}, u32[]{:S(2)}, u32[]{:S(2)}) collective-permute-start(bf16[64,8,2048]{2,1,0:T(8,128)(2,1)S(1)} %get-tuple-element.10), channel_id=1, source_target_pairs={{240,0},{0,16},{16,32},{32,48},{48,64},{64,80},{80,96},{96,112},{1... | collective-permute-start | bytes 6291464 | tf_op jit(solution)/shard_map/ppermute | solution.py:16
  195.0 49.8 %collective-permute-start.1 = (bf16[64,8,2048]{2,1,0:T(8,128)(2,1)}, bf16[64,8,2048]{2,1,0:T(8,128)(2,1)}, u32[]{:S(2)}, u32[]{:S(2)}) collective-permute-start(bf16[64,8,2048]{2,1,0:T(8,128)(2,1)} %collective-permute-done), channel_id=1, source_target_pairs={{16,0},{32,16},{48,32},{64,48},{80,64},{96,80},{112,96},{128,112},... | collective-permute-start | bytes 6291464 | tf_op jit(solution)/shard_map/ppermute | solution.py:16
  197.9 53.2 %collective-permute-start.3 = (bf16[64,8,2048]{2,1,0:T(8,128)(2,1)}, bf16[64,8,2048]{2,1,0:T(8,128)(2,1)}, u32[]{:S(2)}, u32[]{:S(2)}) collective-permute-start(bf16[64,8,2048]{2,1,0:T(8,128)(2,1)} %collective-permute-done.2), channel_id=1, source_target_pairs={{240,0},{0,16},{16,32},{32,48},{48,64},{64,80},{80,96},{96,112},{1... | collective-permute-start | bytes 6291464 | tf_op jit(solution)/shard_map/ppermute | solution.py:16
  263.6 8.7 %copy-start.4 = (bf16[64,8,16,64]{3,2,1,0:T(8,128)(2,1)S(1)}, bf16[64,8,16,64]{3,2,1,0:T(8,128)(2,1)}, u32[]{:S(2)}) copy-start(bf16[64,8,16,64]{3,2,1,0:T(8,128)(2,1)} %reshape.99) | copy-start | bytes 3145732
  304.3 35.9 %all-to-all-start.1 = ((bf16[64,8,1024]{2,1,0:T(8,128)(2,1)}), bf16[64,8,1024]{2,1,0:T(8,128)(2,1)}, u32[]{:S(2)}, u32[]{:S(2)}) async-start(bf16[64,8,1024]{2,1,0:T(8,128)(2,1)} %copy.55), calls=%async_computation.1 | async-start | bytes 2097152 | tf_op jit(solution)/shard_map/all_to_all | solution.py:107
  309.2 35.2 %copy-start.1 = (bf16[1024,1024]{1,0:T(8,128)(2,1)S(1)}, bf16[1024,1024]{1,0:T(8,128)(2,1)}, u32[]{:S(2)}) copy-start(bf16[1024,1024]{1,0:T(8,128)(2,1)} %param.10) | copy-start | bytes 6291460
Sparse Core Ops, SparseCore 0:
  9.9 128.9 all-gather.2
  198.1 83.9 all-gather.4
where the time goes:
time: 353 us; the launch traced here: 351 us
  waiting for transfers between devices  150 us (42%)
  local copies, waits for them, and re-layouts  76.8 us (22%)
  blocking collectives  48.1 us (14%)
  matrix products  43.2 us (12%)
  between operations  13.6 us (4%)
  other arithmetic  11 us (3%)
  starting transfers between devices  8.31 us (2%)
    ppermute x4, waiting for transfers between devices, from_behind(): return lax.ppermute(block, axis, route)  85 us
    all_to_all x1, blocking collectives, per_device(): lax.all_to_all(middle, 'tm', split_axis=1, concat_axis=0, tiled=True)  48.1 us
    all_gather x1, waiting for transfers between devices, per_device(): lax.all_gather(w_inter_qkv, 'tm', axis=0, tiled=True)  33.5 us
    all_to_all x1, waiting for transfers between devices, per_device(): lax.all_to_all(mixed_heads.reshape(char_count, frame_count, feature_width...  31 us
    unnamed x20, local copies, waits for them, and re-layouts  21.7 us
    slice x2, local copies, waits for them, and re-layouts, per_device(): stacked[:, :, :feature_width].reshape(-1, frame_count, head_count, HEAD)  18 us
    sub x1, matrix products, softmax_rows(): weights = jnp.exp(scores - row_top)  12.4 us
    dot_general x1, matrix products, per_device(): jnp.einsum('fhck,kfhd->cfhd', weights, value_part, preferred_element_type...  8.79 us
  transfers between devices with their start and end apart: 7, of which 4 were waited for; matrix products, arithmetic and copies ran while one was open for 33% of the time, Pallas kernels for 0%

commit v1 on v0

v1 whole, which is shorter than its diff:
```python
import jax
import jax.numpy as jnp
from jax import lax
from jax.sharding import PartitionSpec as P

HEAD = 64
REACH = 2


EPSILON = 1e-06


def from_group(block, axis, offset):
    count = lax.axis_size(axis)
    route = [((i + offset) % count, i) for i in range(count)]
    return lax.ppermute(block, axis, route)


def modulate(field, modulation, first, second):
    values = field.astype(jnp.float32)
    mean_square = jnp.mean(values * values, axis=-1, keepdims=True)
    scaled = (
        values * lax.rsqrt(mean_square + EPSILON) * (1.0 + modulation[second]) + modulation[first]
    )
    return scaled.astype(jnp.bfloat16)


def softmax_rows(scores):
    row_top = jnp.max(scores, axis=-1, keepdims=True)
    weights = jnp.exp(scores - row_top)
    return (weights / jnp.sum(weights, axis=-1, keepdims=True)).astype(jnp.bfloat16)


def gather_split_by_core(shard, axis_small, axis_pair):
    half = shard.shape[1] // 2
    pair_index = lax.axis_index(axis_pair) % 2
    mine = lax.dynamic_slice_in_dim(shard, pair_index * half, half, axis=1)
    gathered = lax.all_gather(mine, axis_small, axis=0, tiled=True)
    count = lax.axis_size(axis_pair)
    other = lax.ppermute(gathered, axis_pair, [(i, i ^ 1) for i in range(count)])
    return jnp.where(
        pair_index == 0,
        jnp.concatenate([gathered, other], axis=1),
        jnp.concatenate([other, gathered], axis=1),
    )


def per_device(motion, modulation, w_temporal_qkv, w_temporal_out, w_inter_qkv, w_inter_out, links):
    own_chars, all_frames, feature_width = motion.shape
    head_count = feature_width // HEAD
    scale = HEAD ** (-0.5)
    inter_qkv = gather_split_by_core(w_inter_qkv, "tm", "grp")
    inter_out = gather_split_by_core(w_inter_out, "tm", "grp")

    normed = modulate(motion, modulation, 0, 1)
    t_w = w_temporal_qkv.reshape(feature_width, 3, head_count, HEAD)
    t_packed = jnp.einsum(
        "nfk,kshd->snhfd", normed, t_w, preferred_element_type=jnp.float32
    ).astype(jnp.bfloat16)
    scores = jnp.einsum(
        "nhfd,nhgd->nhfg", t_packed[0], t_packed[1], preferred_element_type=jnp.float32
    ) * scale
    weights = softmax_rows(scores)
    t_mixed = jnp.einsum(
        "nhfg,nhgd->nhfd", weights, t_packed[2], preferred_element_type=jnp.float32
    ).astype(jnp.bfloat16)
    t_projected = jnp.einsum(
        "nhfd,hdo->nfo",
        t_mixed,
        w_temporal_out.reshape(head_count, HEAD, feature_width),
        preferred_element_type=jnp.float32,
    )
    middle = (motion.astype(jnp.float32) + modulation[2] * t_projected).astype(jnp.bfloat16)
    normed_inter = modulate(middle, modulation, 3, 4)

    frames_own = lax.all_to_all(normed_inter, "tm", split_axis=1, concat_axis=0, tiled=True)
    offsets = [j + 1 for j in range(REACH)] + [-(j + 1) for j in range(REACH)]
    others = [from_group(frames_own, "grp", offset) for offset in offsets]
    stacked = jnp.stack([frames_own] + others, axis=0)

    i_w = inter_qkv.reshape(feature_width, 3, head_count, HEAD)
    queries = jnp.einsum(
        "cfk,khd->fhcd", frames_own, i_w[:, 0], preferred_element_type=jnp.float32
    ).astype(jnp.bfloat16)
    pairs = jnp.einsum(
        "scfk,kthd->tfhscd", stacked, i_w[:, 1:], preferred_element_type=jnp.float32
    ).astype(jnp.bfloat16)
    scores = jnp.einsum(
        "fhcd,fhskd->fhcsk", queries, pairs[0], preferred_element_type=jnp.float32
    ) * scale
    own_links = lax.dynamic_index_in_dim(links, lax.axis_index("grp"), axis=0, keepdims=False)
    allowed = jnp.concatenate([jnp.ones((1,), jnp.int32), own_links]) > 0
    scores = jnp.where(allowed[:, None], scores, -jnp.inf)
    group_count, char_count = scores.shape[3], scores.shape[4]
    frame_count = scores.shape[0]
    weights = softmax_rows(
        scores.reshape(frame_count, head_count, char_count, group_count * char_count)
    ).reshape(scores.shape)
    mixed_heads = jnp.einsum(
        "fhcsk,fhskd->cfhd", weights, pairs[1], preferred_element_type=jnp.float32
    ).astype(jnp.bfloat16)
    mixed_chars = lax.all_to_all(
        mixed_heads.reshape(char_count, frame_count, feature_width),
        "tm",
        split_axis=0,
        concat_axis=1,
        tiled=True,
    )
    result = jnp.dot(
        mixed_chars.reshape(own_chars * all_frames, feature_width),
        inter_out,
        preferred_element_type=jnp.float32,
    )
    total = middle.astype(jnp.float32) + modulation[5] * result.reshape(
        own_chars, all_frames, feature_width
    )
    return total.astype(jnp.bfloat16)


def solution(mesh):
    placed = (P(("grp", "tm"), None, None), P(), P(), P(), P("tm", None), P("tm", None), P())
    return jax.shard_map(
        per_device,
        mesh=mesh,
        in_specs=placed,
        out_specs=P(("grp", "tm"), None, None),
        check_vma=False,
    )
```

time: 353 us -> 337 us (0.955)
  blocking collectives: 48.1 us -> 0 us
  local copies, waits for them, and re-layouts: 76.8 us -> 49.9 us
  matrix products: 43.2 us -> 68.6 us
  other arithmetic: 11 us -> 23 us
  starting transfers between devices: 8.31 us -> 20 us
  waiting for transfers between devices: 150 us -> 160 us
    all_to_all x1 -> x0, blocking collectives: 48.1 us -> none  [per_device(): lax.all_to_all(middle, 'tm', split_axis=1, concat_axis=0, tiled=True)]
    dot_general x6, matrix products: 26.7 us -> 63.7 us  [the longest x1 24.9 us: per_device(): jnp.einsum('scfk,kthd->tfhscd', stacked, i_w[:, 1:], preferred_element_ty...]
    slice x6 -> x0, local copies, waits for them, and re-layouts: 35.7 us -> none  [the longest x2 18 us: per_device(): stacked[:, :, :feature_width].reshape(-1, frame_count, head_count, HEAD)]
    all_gather x2, waiting for transfers between devices: 33.6 us -> 65.8 us  [gather_split_by_core(): gathered = lax.all_gather(mine, axis_small, axis=0, tiled=True)]
    ppermute x4 -> x6, waiting for transfers between devices: 85 us -> 66.8 us  [the longest x4 63.8 us: from_group(): return lax.ppermute(block, axis, route)]
    squeeze x0 -> x1, local copies, waits for them, and re-layouts: none -> 12.6 us  [per_device(): pairs[1]]
    sub x1 -> x0, matrix products: 12.4 us -> none  [softmax_rows(): weights = jnp.exp(scores - row_top)]
    reshape x2 -> x0, local copies, waits for them, and re-layouts: 11.2 us -> none  [the longest x1 8.63 us: temporal_heads(): packed.astype(jnp.bfloat16)]
  transfers between devices with their start and end apart: 7 -> 10, of which waited for: 4 -> 6; matrix products, arithmetic and copies ran while one was open for 33% -> 40% of each run, Pallas kernels for 0% -> 0%
where the time goes in v1:
time: 337 us; the launch traced here: 335 us
  waiting for transfers between devices  160 us (47%)
  matrix products  68.6 us (20%)
  local copies, waits for them, and re-layouts  49.9 us (15%)
  other arithmetic  23 us (7%)
  starting transfers between devices  20 us (6%)
  between operations  13.6 us (4%)
    all_gather x2, waiting for transfers between devices, gather_split_by_core(): gathered = lax.all_gather(mine, axis_small, axis=0, tiled=True)  65.8 us
    ppermute x4, waiting for transfers between devices, from_group(): return lax.ppermute(block, axis, route)  63.8 us
    all_to_all x1, waiting for transfers between devices, per_device(): lax.all_to_all(mixed_heads.reshape(char_count, frame_count, feature_width...  27.3 us
    dot_general x1, matrix products, per_device(): jnp.einsum('scfk,kthd->tfhscd', stacked, i_w[:, 1:], preferred_element_ty...  24.9 us
    unnamed x25, local copies, waits for them, and re-layouts  16.8 us
    dot_general x1, matrix products, per_device(): jnp.einsum('fhcsk,fhskd->cfhd', weights, pairs[1], preferred_element_type...  13.8 us
    dot_general x1, matrix products, per_device(): jnp.einsum('fhcd,fhskd->fhcsk', queries, pairs[0], preferred_element_type...  13.6 us
    squeeze x1, local copies, waits for them, and re-layouts, per_device(): pairs[1]  12.6 us
  transfers between devices with their start and end apart: 10, of which 6 were waited for; matrix products, arithmetic and copies ran while one was open for 40% of the time, Pallas kernels for 0%

profile of v1, /device:TPU:8, one launch (start us, length us, event | category | flops | bytes accessed | tf_op | source)
XLA Modules:
  0.0 335.0 jit_solution(16028606905051927640)
XLA Ops:
  6.5 0.0 copy-start
  6.5 0.0 all-gather.3.cloned.1.call-start
  6.5 1.8 constant_dynamic-slice_fusion.1
  8.3 0.0 all-gather.3.cloned.1.call-update
  8.3 0.0 copy-start.4
  8.3 0.0 copy-start.7
  8.3 8.7 %copy.25 = bf16[1024,3072]{0,1:T(8,128)(2,1)} copy(bf16[1024,3072]{1,0:T(8,128)(2,1)} %param.9) | data formatting | bytes 12582912 | tf_op args[2]
  17.1 0.0 copy-done.4
  17.1 0.3 fusion.14
  17.4 0.0 copy-done.7
  17.4 0.6 fusion.55
  18.0 5.9 %convert_bitcast_fusion.1 = bf16[3,4,16,128,64]{3,4,2,0,1:T(8,128)(2,1)S(1)} fusion(bf16[1024,3,16,64,1]{0,3,2,1,4:T(8,128)(2,1)} %bitcast.123, bf16[4,128,1024]{2,1,0:T(8,128)(2,1)S(1)} %copy-done.4, f32[1024]{0:T(1024)S(1)} %bitcast.132, f32[1024]{0:T(1024)S(1)} %bitcast.133, f32[4,128]{1,0:T(4,128)S(1)} %add_rsqrt_fusion.1), kind=kOutput, calls=%fused_computation.25 | convolution fusion | flops 3225419776 | bytes 10496000 | tf_op jit(solution)/shard_map/nfk,kshd->snhfd/dot_general | solution.py:57
  23.9 0.0 copy-start.3
  23.9 0.8 fusion.43
  24.7 2.9 fusion.56
  27.6 0.0 copy-done.3
  27.6 4.8 %fusion.19 = (f32[4,128]{1,0:T(4,128)S(1)}, bf16[4,128,1024]{2,1,0:T(8,128)(2,1)S(1)}) fusion(bf16[16,64,1024,1]{2,1,0,3:T(8,128)(2,1)S(1)} %bitcast.119, f32[4,16,128,128]{2,3,1,0:T(8,128)} %get-tuple-element.14, f32[4,16,128]{2,1,0:T(8,128)S(1)} %get-tuple-element.13, bf16[3,4,16,128,64]{3,4,2,0,1:T(8,128)(2,1)} %copy-done.3, f32[1024]{0:T(1024)S(1)} %bitcast.131, ...), kind=kOutput, calls=%fused_computation.34 | convolution fusion | flops 1214250496 | bytes 9476096 | tf_op jit(solution)/shard_map/nhfd,hdo->nfo/dot_general | solution.py:67
  32.4 0.0 copy-start.6
  32.4 0.0 copy-start.9
  32.5 0.4 fusion.22
  32.8 1.8 copy.28
  34.6 11.0 %all-to-all-start = ((bf16[4,128,1024]{2,0,1:T(4,128)(2,1)}), bf16[4,128,1024]{2,0,1:T(4,128)(2,1)S(1)}, u32[]{:S(2)}, u32[]{:S(2)}) async-start(bf16[4,128,1024]{2,0,1:T(4,128)(2,1)} %copy.28), calls=%async_computation | async-start | bytes 2097152 | tf_op jit(solution)/shard_map/all_to_all | solution.py:76
  45.7 0.0 all-gather.5.cloned.1.call-start
  45.7 65.8 %all-gather.3.cloned.1.call-done = bf16[1024,1536]{1,0:T(8,128)(2,1)} async-done(((bf16[64,1536]{1,0:T(8,128)(2,1)}), bf16[1024,1536]{1,0:T(8,128)(2,1)}) %all-gather.3.cloned.1.call-update) | async-done | bytes 3145744 | tf_op jit(solution)/shard_map/all_gather | solution.py:38
  111.5 0.0 collective-permute-start
  111.5 0.0 all-to-all-done
  111.5 0.4 copy.62
  111.9 1.1 all_to_all.27
  113.0 0.6 collective-permute-start.1
  113.6 1.5 collective-permute-start.2
  115.1 0.0 collective-permute-start.3
  115.1 0.0 copy-done.6
  115.1 0.6 constant_dynamic-slice_fusion
  115.7 0.0 all-gather.5.cloned.1.call-update
  115.7 0.2 dynamic-slice_reduce_fusion
  115.9 0.8 collective-permute-start.4
  116.7 0.1 add_compare_fusion
  116.8 0.3 stack.18
  117.1 1.2 reshape.70
  118.3 1.1 constant_dynamic-update-slice_fusion
  119.3 18.9 %collective-permute-done.1 = bf16[64,8,1024]{2,0,1:T(8,128)(2,1)} collective-permute-done((bf16[64,8,1024]{2,0,1:T(8,128)(2,1)}, bf16[64,8,1024]{2,0,1:T(8,128)(2,1)}, u32[]{:S(2)}, u32[]{:S(2)}) %collective-permute-start.1) | collective-permute-done | bytes 1048608 | tf_op jit(solution)/shard_map/ppermute | solution.py:16
  138.2 2.3 bitcast_dynamic-update-slice_fusion.3
  140.5 22.2 %collective-permute-done.2 = bf16[64,8,1024]{2,0,1:T(8,128)(2,1)} collective-permute-done((bf16[64,8,1024]{2,0,1:T(8,128)(2,1)}, bf16[64,8,1024]{2,0,1:T(8,128)(2,1)}, u32[]{:S(2)}, u32[]{:S(2)}) %collective-permute-start.2) | collective-permute-done | bytes 1048608 | tf_op jit(solution)/shard_map/ppermute | solution.py:16
  162.7 2.4 bitcast_dynamic-update-slice_fusion.2
  165.0 0.0 collective-permute-done.3
  165.0 2.2 bitcast_dynamic-update-slice_fusion.1
  167.3 22.8 %collective-permute-done.4 = bf16[64,8,1024]{2,0,1:T(8,128)(2,1)} collective-permute-done((bf16[64,8,1024]{2,0,1:T(8,128)(2,1)}, bf16[64,8,1024]{2,0,1:T(8,128)(2,1)}, u32[]{:S(2)}, u32[]{:S(2)}) %collective-permute-start.4) | collective-permute-done | bytes 1048608 | tf_op jit(solution)/shard_map/ppermute | solution.py:16
  190.1 2.3 bitcast_dynamic-update-slice_fusion
  192.4 0.0 collective-permute-done
  192.4 0.0 copy-done.2
  192.4 7.7 %maximum_select_fusion = bf16[1024,3072]{1,0:T(8,128)(2,1)} fusion(bf16[1024,1536]{1,0:T(8,128)(2,1)} %collective-permute-done, bf16[1024,1536]{1,0:T(8,128)(2,1)S(1)} %copy-done.2, pred[]{:T(512)S(6)} %eq.7), kind=kLoop, calls=%fused_computation.14 | loop fusion | flops 28311552 | bytes 12582913 | tf_op jit(solution)/shard_map/jit(_where)/select_n | solution.py:41
  200.1 8.6 %copy.27 = bf16[1024,3072]{0,1:T(8,128)(2,1)} copy(bf16[1024,3072]{1,0:T(8,128)(2,1)} %maximum_select_fusion) | data formatting | bytes 12582912 | tf_op jit(solution)/shard_map/jit(_where)/select_n | solution.py:41
  208.8 24.9 %convert_bitcast_fusion = bf16[2,8,16,5,64,64]{4,5,1,3,2,0:T(8,128)(2,1)S(1)} fusion(bf16[5,64,8,1024]{3,1,2,0:T(8,128)(2,1)} %bitcast_dynamic-update-slice_fusion, bf16[1024,3,16,64]{0,3,2,1:T(8,128)(2,1)} %bitcast.124), kind=kOutput, calls=%fused_computation.4 | convolution fusion | flops 10742661120 | bytes 19922944 | tf_op jit(solution)/shard_map/scfk,kthd->tfhscd/dot_general | solution.py:85
  233.6 12.6 %slice_bitcast_fusion.1 = (bf16[8,16,5,64,64]{3,4,0,2,1:T(8,128)(2,1)}, bf16[8,16,5,64,64]{3,4,0,2,1:T(8,128)(2,1)}) fusion(bf16[2,8,16,5,64,64]{4,5,1,3,2,0:T(8,128)(2,1)S(1)} %convert_bitcast_fusion), kind=kLoop, calls=%fused_computation.8 | loop fusion | bytes 20971520 | tf_op jit(solution)/shard_map/squeeze | solution.py:100
  246.2 13.6 %fusion.1 = (f32[8,16,64]{2,1,0:T(8,128)S(1)}, f32[8,16,64,5,64]{2,4,3,1,0:T(8,128)}) fusion(pred[5]{0:T(512)(128)(4,1)S(1)} %add_compare_fusion, bf16[8,16,5,64,64]{3,4,0,2,1:T(8,128)(2,1)} %get-tuple-element.6, bf16[1024,3,16,64]{0,3,2,1:T(8,128)(2,1)} %bitcast.125, bf16[64,8,1024,1]{2,0,1,3:T(8,128)(2,1)S(1)} %copy-done.5), kind=kOutput, calls=%fused_computation.5 | convolution fusion | flops 1417666560 | bytes 24150020 | tf_op jit(solution)/shard_map/fhcd,fhskd->fhcsk/dot_general | solution.py:88
  259.8 11.0 %fusion.2 = f32[8,16,64]{2,1,0:T(8,128)S(1)} fusion(f32[8,16,64,5,64]{2,4,3,1,0:T(8,128)} %get-tuple-element.18, f32[8,16,64]{2,1,0:T(8,128)S(1)} %get-tuple-element.17, pred[5]{0:T(512)(128)(4,1)S(1)} %add_compare_fusion), kind=kLoop, calls=%fused_computation.6 | loop fusion | flops 10477568 | bytes 10551301 | tf_op jit(solution)/shard_map/reduce_sum | solution.py:31
  270.7 13.8 %bitcast_convert_fusion = bf16[8,16,64,64]{3,2,1,0:T(8,128)(2,1)S(1)} fusion(f32[8,16,64,5,64]{2,4,3,1,0:T(8,128)} %get-tuple-element.18, f32[8,16,64]{2,1,0:T(8,128)S(1)} %fusion.2, f32[8,16,64]{2,1,0:T(8,128)S(1)} %get-tuple-element.17, pred[5]{0:T(512)(128)(4,1)S(1)} %add_compare_fusion, bf16[8,16,5,64,64]{3,4,0,2,1:T(8,128)(2,1)} %get-tuple-element.5), kind=kOutput, calls=%fused_computation.17 | convolution fusion | flops 349175808 | bytes 16842756 | tf_op jit(solution)/shard_map/fhcsk,fhskd->cfhd/dot_general | solution.py:99
  284.5 2.4 copy.34
  286.9 5.9 %all-to-all-start.1 = ((bf16[64,8,1024]{2,1,0:T(8,128)(2,1)}), bf16[64,8,1024]{2,1,0:T(8,128)(2,1)}, u32[]{:S(2)}, u32[]{:S(2)}) async-start(bf16[64,8,1024]{2,1,0:T(8,128)(2,1)} %copy.34), calls=%async_computation.1 | async-start | bytes 2097152 | tf_op jit(solution)/shard_map/all_to_all | solution.py:102
  292.8 0.0 all-gather.5.cloned.1.call-done
  292.9 0.1 collective-permute-start.5
  293.0 3.0 collective-permute-done.5
  296.0 27.3 %all-to-all-done.1 = bf16[64,8,1024]{2,1,0:T(8,128)(2,1)} async-done(((bf16[64,8,1024]{2,1,0:T(8,128)(2,1)}), bf16[64,8,1024]{2,1,0:T(8,128)(2,1)}, u32[]{:S(2)}, u32[]{:S(2)}) %all-to-all-start.1) | async-done | bytes 1048608 | tf_op jit(solution)/shard_map/all_to_all | solution.py:102
  323.2 4.9 %fusion.23 = bf16[4,128,1024]{2,1,0:T(8,128)(2,1)} fusion(bf16[4,128,1024]{2,1,0:T(8,128)(2,1)S(1)} %get-tuple-element.16, bf16[1024,512]{1,0:T(8,128)(2,1)} %collective-permute-done.5, bf16[1024,512]{1,0:T(8,128)(2,1)} %all-gather.5.cloned.1.call-done, pred[]{:T(512)S(6)} %eq.7, bf16[4,16,8,1024]{3,2,0,1:T(8,128)(2,1)} %bitcast.42, f32[1024]{0:T(1024)S(1)} %bitcast.130), kind=kOutput, calls=%fused_computation.38 | convolution fusion | flops 1085276160 | bytes 5246977 | tf_op jit(solution)/shard_map/dot_general | solution.py:109
  (11 shorter events, 0.0 us)
Async XLA Ops:
  6.5 21.1 %copy-start = (bf16[1024,1024]{1,0:T(8,128)(2,1)S(1)}, bf16[1024,1024]{1,0:T(8,128)(2,1)}, u32[]{:S(2)}) copy-start(bf16[1024,1024]{1,0:T(8,128)(2,1)} %param.10) | copy-start | bytes 6291460
  6.5 104.9 %all-gather.3.cloned.1.call-start = ((), (), s32[]{:S(2)}) async-start(), calls=%async_computation.2 | async-start | bytes 3342336 | tf_op jit(solution)/shard_map/all_gather | solution.py:38
  8.3 8.7 %copy-start.4 = (bf16[4,128,1024]{2,1,0:T(8,128)(2,1)S(1)}, bf16[4,128,1024]{2,1,0:T(8,128)(2,1)}, u32[]{:S(2)}) copy-start(bf16[4,128,1024]{2,1,0:T(8,128)(2,1)} %param.7) | copy-start | bytes 3145732
  8.3 9.0 %copy-start.7 = (f32[6,1024]{1,0:T(8,128)S(1)}, f32[6,1024]{1,0:T(8,128)}, u32[]{:S(2)}) copy-start(f32[6,1024]{1,0:T(8,128)} %param.8) | copy-start | bytes 73732
  23.9 3.7 %copy-start.3 = (bf16[3,4,16,128,64]{3,4,2,0,1:T(8,128)(2,1)}, bf16[3,4,16,128,64]{3,4,2,0,1:T(8,128)(2,1)S(1)}, u32[]{:S(2)}) copy-start(bf16[3,4,16,128,64]{3,4,2,0,1:T(8,128)(2,1)S(1)} %convert_bitcast_fusion.1) | copy-start | bytes 9437188
  32.4 82.6 %copy-start.6 = (bf16[64,1024]{1,0:T(8,128)(2,1)S(1)}, bf16[64,1024]{1,0:T(8,128)(2,1)}, u32[]{:S(2)}) copy-start(bf16[64,1024]{1,0:T(8,128)(2,1)} %param.12) | copy-start | bytes 393220
  32.4 83.3 %copy-start.9 = (s32[16,4]{0,1:T(4,128)S(1)}, s32[16,4]{0,1:T(4,128)}, u32[]{:S(2)}) copy-start(s32[16,4]{0,1:T(4,128)} %param.13) | copy-start | bytes 772
  34.6 76.9 %all-to-all-start = ((bf16[4,128,1024]{2,0,1:T(4,128)(2,1)}), bf16[4,128,1024]{2,0,1:T(4,128)(2,1)S(1)}, u32[]{:S(2)}, u32[]{:S(2)}) async-start(bf16[4,128,1024]{2,0,1:T(4,128)(2,1)} %copy.28), calls=%async_computation | async-start | bytes 2097152 | tf_op jit(solution)/shard_map/all_to_all | solution.py:76
  45.7 247.2 %all-gather.5.cloned.1.call-start = ((), (), s32[]{:S(2)}) async-start(), calls=%async_computation.3 | async-start | bytes 1114112 | tf_op jit(solution)/shard_map/all_gather | solution.py:38
  111.5 80.9 %collective-permute-start = (bf16[1024,1536]{1,0:T(8,128)(2,1)}, bf16[1024,1536]{1,0:T(8,128)(2,1)}, u32[]{:S(2)}, u32[]{:S(2)}) collective-permute-start(bf16[1024,1536]{1,0:T(8,128)(2,1)} %all-gather.3.cloned.1.call-done), channel_id=1, source_target_pairs={{0,16},{16,0},{32,48},{48,32},{64,80},{80,64},{96,112},{112,96},{1... | collective-permute-start | bytes 9437192 | tf_op jit(solution)/shard_map/ppermute | solution.py:40
  113.0 25.2 %collective-permute-start.1 = (bf16[64,8,1024]{2,0,1:T(8,128)(2,1)}, bf16[64,8,1024]{2,0,1:T(8,128)(2,1)}, u32[]{:S(2)}, u32[]{:S(2)}) collective-permute-start(bf16[64,8,1024]{2,0,1:T(8,128)(2,1)} %all_to_all.27), channel_id=1, source_target_pairs={{16,0},{32,16},{48,32},{64,48},{80,64},{96,80},{112,96},{128,112},... | collective-permute-start | bytes 3145736 | tf_op jit(solution)/shard_map/ppermute | solution.py:16
  113.6 49.0 %collective-permute-start.2 = (bf16[64,8,1024]{2,0,1:T(8,128)(2,1)}, bf16[64,8,1024]{2,0,1:T(8,128)(2,1)}, u32[]{:S(2)}, u32[]{:S(2)}) collective-permute-start(bf16[64,8,1024]{2,0,1:T(8,128)(2,1)} %all_to_all.27), channel_id=1, source_target_pairs={{32,0},{48,16},{64,32},{80,48},{96,64},{112,80},{128,96},{144,112}... | collective-permute-start | bytes 3145736 | tf_op jit(solution)/shard_map/ppermute | solution.py:16
  115.1 49.9 %collective-permute-start.3 = (bf16[64,8,1024]{2,0,1:T(8,128)(2,1)}, bf16[64,8,1024]{2,0,1:T(8,128)(2,1)}, u32[]{:S(2)}, u32[]{:S(2)}) collective-permute-start(bf16[64,8,1024]{2,0,1:T(8,128)(2,1)} %all_to_all.27), channel_id=1, source_target_pairs={{240,0},{0,16},{16,32},{32,48},{48,64},{64,80},{80,96},{96,112},{1... | collective-permute-start | bytes 3145736 | tf_op jit(solution)/shard_map/ppermute | solution.py:16
  115.9 74.2 %collective-permute-start.4 = (bf16[64,8,1024]{2,0,1:T(8,128)(2,1)}, bf16[64,8,1024]{2,0,1:T(8,128)(2,1)}, u32[]{:S(2)}, u32[]{:S(2)}) collective-permute-start(bf16[64,8,1024]{2,0,1:T(8,128)(2,1)} %all_to_all.27), channel_id=1, source_target_pairs={{224,0},{240,16},{0,32},{16,48},{32,64},{48,80},{64,96},{80,112},{... | collective-permute-start | bytes 3145736 | tf_op jit(solution)/shard_map/ppermute | solution.py:16
  118.3 74.1 %copy-start.2 = (bf16[1024,1536]{1,0:T(8,128)(2,1)S(1)}, bf16[1024,1536]{1,0:T(8,128)(2,1)}, u32[]{:S(2)}) copy-start(bf16[1024,1536]{1,0:T(8,128)(2,1)} %all-gather.3.cloned.1.call-done) | copy-start | bytes 9437188
  233.6 12.6 %copy-start.5 = (bf16[64,8,1024,1]{2,0,1,3:T(8,128)(2,1)S(1)}, bf16[64,8,1024,1]{2,0,1,3:T(8,128)(2,1)}, u32[]{:S(2)}) copy-start(bf16[64,8,1024,1]{2,0,1,3:T(8,128)(2,1)} %reshape.70) | copy-start | bytes 3145732
  284.5 38.7 %copy-start.8 = (f32[1,1024]{1,0:T(1,128)S(1)}, f32[1,1024]{1,0:T(1,128)}, u32[]{:S(2)}) copy-start(f32[1,1024]{1,0:T(1,128)} %get-tuple-element.7) | copy-start | bytes 12292
  286.9 36.3 %all-to-all-start.1 = ((bf16[64,8,1024]{2,1,0:T(8,128)(2,1)}), bf16[64,8,1024]{2,1,0:T(8,128)(2,1)}, u32[]{:S(2)}, u32[]{:S(2)}) async-start(bf16[64,8,1024]{2,1,0:T(8,128)(2,1)} %copy.34), calls=%async_computation.1 | async-start | bytes 2097152 | tf_op jit(solution)/shard_map/all_to_all | solution.py:102
  292.9 3.1 collective-permute-start.5
  323.2 4.9 %copy-start.1 = (bf16[1024,1024]{1,0:T(8,128)(2,1)S(1)}, bf16[1024,1024]{1,0:T(8,128)(2,1)}, u32[]{:S(2)}) copy-start(bf16[1024,1024]{1,0:T(8,128)(2,1)} %param.10) | copy-start | bytes 6291460
Sparse Core Ops, SparseCore 0:
  9.9 101.5 all-gather.2
  115.8 84.2 all-gather.4

commit v2 on v1

--- a/solution.py
+++ b/solution.py
@@ -31,26 +31,40 @@
     return (weights / jnp.sum(weights, axis=-1, keepdims=True)).astype(jnp.bfloat16)
 
 
-def gather_split_by_core(shard, axis_small, axis_pair):
-    half = shard.shape[1] // 2
+def gather_split_by_core(shards, axis_small, axis_pair):
     pair_index = lax.axis_index(axis_pair) % 2
-    mine = lax.dynamic_slice_in_dim(shard, pair_index * half, half, axis=1)
+    halves = [shard.shape[1] // 2 for shard in shards]
+    mine = jnp.concatenate(
+        [
+            lax.dynamic_slice_in_dim(shard, pair_index * half, half, axis=1)
+            for shard, half in zip(shards, halves)
+        ],
+        axis=1,
+    )
     gathered = lax.all_gather(mine, axis_small, axis=0, tiled=True)
     count = lax.axis_size(axis_pair)
     other = lax.ppermute(gathered, axis_pair, [(i, i ^ 1) for i in range(count)])
-    return jnp.where(
-        pair_index == 0,
-        jnp.concatenate([gathered, other], axis=1),
-        jnp.concatenate([other, gathered], axis=1),
-    )
+    results = []
+    start = 0
+    for half in halves:
+        own_part = gathered[:, start:start + half]
+        other_part = other[:, start:start + half]
+        start += half
+        results.append(
+            jnp.where(
+                pair_index == 0,
+                jnp.concatenate([own_part, other_part], axis=1),
+                jnp.concatenate([other_part, own_part], axis=1),
+            )
+        )
+    return results
 
 
 def per_device(motion, modulation, w_temporal_qkv, w_temporal_out, w_inter_qkv, w_inter_out, links):
     own_chars, all_frames, feature_width = motion.shape
     head_count = feature_width // HEAD
     scale = HEAD ** (-0.5)
-    inter_qkv = gather_split_by_core(w_inter_qkv, "tm", "grp")
-    inter_out = gather_split_by_core(w_inter_out, "tm", "grp")
+    inter_qkv, inter_out = gather_split_by_core((w_inter_qkv, w_inter_out), "tm", "grp")
 
     normed = modulate(motion, modulation, 0, 1)
     t_w = w_temporal_qkv.reshape(feature_width, 3, head_count, HEAD)
@@ -76,28 +90,26 @@
     frames_own = lax.all_to_all(normed_inter, "tm", split_axis=1, concat_axis=0, tiled=True)
     offsets = [j + 1 for j in range(REACH)] + [-(j + 1) for j in range(REACH)]
     others = [from_group(frames_own, "grp", offset) for offset in offsets]
-    stacked = jnp.stack([frames_own] + others, axis=0)
+    stacked = jnp.concatenate([frames_own] + others, axis=0)
+    char_count, frame_count, unused_width = frames_own.shape
 
     i_w = inter_qkv.reshape(feature_width, 3, head_count, HEAD)
     queries = jnp.einsum(
         "cfk,khd->fhcd", frames_own, i_w[:, 0], preferred_element_type=jnp.float32
     ).astype(jnp.bfloat16)
     pairs = jnp.einsum(
-        "scfk,kthd->tfhscd", stacked, i_w[:, 1:], preferred_element_type=jnp.float32
+        "mfk,kthd->tfhmd", stacked, i_w[:, 1:], preferred_element_type=jnp.float32
     ).astype(jnp.bfloat16)
     scores = jnp.einsum(
-        "fhcd,fhskd->fhcsk", queries, pairs[0], preferred_element_type=jnp.float32
+        "fhcd,fhmd->fhcm", queries, pairs[0], preferred_element_type=jnp.float32
     ) * scale
     own_links = lax.dynamic_index_in_dim(links, lax.axis_index("grp"), axis=0, keepdims=False)
-    allowed = jnp.concatenate([jnp.ones((1,), jnp.int32), own_links]) > 0
-    scores = jnp.where(allowed[:, None], scores, -jnp.inf)
-    group_count, char_count = scores.shape[3], scores.shape[4]
-    frame_count = scores.shape[0]
-    weights = softmax_rows(
-        scores.reshape(frame_count, head_count, char_count, group_count * char_count)
-    ).reshape(scores.shape)
+    allowed = jnp.concatenate([jnp.ones((1,), jnp.int32), own_links])
+    key_mask = jnp.repeat(allowed, char_count) > 0
+    scores = jnp.where(key_mask, scores, -jnp.inf)
+    weights = softmax_rows(scores)
     mixed_heads = jnp.einsum(
-        "fhcsk,fhskd->cfhd", weights, pairs[1], preferred_element_type=jnp.float32
+        "fhcm,fhmd->cfhd", weights, pairs[1], preferred_element_type=jnp.float32
     ).astype(jnp.bfloat16)
     mixed_chars = lax.all_to_all(
         mixed_heads.reshape(char_count, frame_count, feature_width),

time: 337 us -> 346 us (1.027)
  blocking collectives: 0 us -> 35.3 us
  matrix products: 68.6 us -> 48.1 us
  starting transfers between devices: 20 us -> 6.67 us
  waiting for transfers between devices: 160 us -> 169 us
    all_to_all x0 -> x1, blocking collectives: none -> 35.3 us  [per_device(): lax.all_to_all(normed_inter, 'tm', split_axis=1, concat_axis=0, tiled=True)]
    dot_general x3, matrix products: 52.2 us -> 31.7 us  [the longest x1 16.7 us: per_device(): jnp.einsum('mfk,kthd->tfhmd', stacked, i_w[:, 1:], preferred_element_type...]
    all_gather x2 -> x1, waiting for transfers between devices: 65.8 us -> 83.2 us  [gather_split_by_core(): gathered = lax.all_gather(mine, axis_small, axis=0, tiled=True)]
    sub x1 -> x2, other arithmetic: 2.95 us -> 17.4 us  [softmax_rows(): weights = jnp.exp(scores - row_top)]
    all_to_all x1 -> x0, starting transfers between devices: 11 us -> none  [per_device(): lax.all_to_all(normed_inter, 'tm', split_axis=1, concat_axis=0, tiled=True)]
    reduce_sum x1 -> x0, other arithmetic: 11 us -> none  [softmax_rows(): jnp.sum(weights, axis=-1, keepdims=True)]
    slice x0 -> x4, local copies, waits for them, and re-layouts: none -> 6.96 us  [the longest x2 4.37 us: gather_split_by_core(): other_part = other[:, start:start + half]]
    squeeze x1, local copies, waits for them, and re-layouts: 12.6 us -> 6.46 us  [per_device(): pairs[1]]
  transfers between devices with their start and end apart: 10 -> 7, of which waited for: 6 -> 5; matrix products, arithmetic and copies ran while one was open for 40% -> 12% of each run, Pallas kernels for 0% -> 0%
where the time goes in v2:
time: 346 us; the launch traced here: 345 us
  waiting for transfers between devices  169 us (49%)
  local copies, waits for them, and re-layouts  49.4 us (14%)
  matrix products  48.1 us (14%)
  blocking collectives  35.3 us (10%)
  other arithmetic  22.7 us (7%)
  between operations  13.6 us (4%)
  starting transfers between devices  6.67 us (2%)
    all_gather x1, waiting for transfers between devices, gather_split_by_core(): gathered = lax.all_gather(mine, axis_small, axis=0, tiled=True)  83.2 us
    ppermute x4, waiting for transfers between devices, from_group(): return lax.ppermute(block, axis, route)  59.5 us
    all_to_all x1, blocking collectives, per_device(): lax.all_to_all(normed_inter, 'tm', split_axis=1, concat_axis=0, tiled=True)  35.3 us
    all_to_all x1, waiting for transfers between devices, per_device(): lax.all_to_all(mixed_heads.reshape(char_count, frame_count, feature_width...  26.3 us
    unnamed x25, local copies, waits for them, and re-layouts  18.4 us
    sub x2, other arithmetic, softmax_rows(): weights = jnp.exp(scores - row_top)  17.4 us
    dot_general x1, matrix products, per_device(): jnp.einsum('mfk,kthd->tfhmd', stacked, i_w[:, 1:], preferred_element_type...  16.7 us
    dot_general x1, matrix products, per_device(): jnp.einsum('fhcd,fhmd->fhcm', queries, pairs[0], preferred_element_type=j...  9.05 us
  transfers between devices with their start and end apart: 7, of which 5 were waited for; matrix products, arithmetic and copies ran while one was open for 12% of the time, Pallas kernels for 0%

profile of v2, /device:TPU:8, one launch (start us, length us, event | category | flops | bytes accessed | tf_op | source)
XLA Modules:
  0.0 344.7 jit_solution(5347084905601416851)
XLA Ops:
  6.5 0.0 copy-start
  6.5 0.0 all-gather.2.cloned.1.call-start
  6.5 1.0 constant_dynamic-slice_fusion
  7.5 0.9 constant_dynamic-slice_fusion.1
  8.5 0.7 pad_maximum_fusion
  9.2 0.0 all-gather.2.cloned.1.call-update
  9.2 0.0 copy-start.7
  9.2 0.0 copy-start.8
  9.2 8.7 %copy.21 = bf16[1024,3072]{0,1:T(8,128)(2,1)} copy(bf16[1024,3072]{1,0:T(8,128)(2,1)} %param.9) | data formatting | bytes 12582912 | tf_op args[2]
  18.0 0.0 copy-done.7
  18.0 0.3 fusion.14
  18.3 0.0 copy-done.8
  18.3 5.9 %convert_bitcast_fusion.1 = bf16[3,4,16,128,64]{3,4,2,0,1:T(8,128)(2,1)S(1)} fusion(bf16[1024,3,16,64,1]{0,3,2,1,4:T(8,128)(2,1)} %bitcast.97, bf16[4,128,1024]{2,1,0:T(8,128)(2,1)S(1)} %copy-done.7, f32[1024]{0:T(1024)S(1)} %bitcast.104, f32[1024]{0:T(1024)S(1)} %bitcast.105, f32[4,128]{1,0:T(4,128)S(1)} %add_rsqrt_fusion.1), kind=kOutput, calls=%fused_computation.26 | convolution fusion | flops 3225419776 | bytes 10496000 | tf_op jit(solution)/shard_map/nfk,kshd->snhfd/dot_general | solution.py:71
  24.2 0.0 copy-start.4
  24.2 1.7 copy-done.4
  25.9 0.8 fusion.46
  26.7 2.9 fusion.59
  29.6 83.2 %all-gather.2.cloned.1.call-done = bf16[1024,2048]{1,0:T(8,128)(2,1)} async-done(((bf16[64,2048]{1,0:T(8,128)(2,1)}), bf16[1024,2048]{1,0:T(8,128)(2,1)}) %all-gather.2.cloned.1.call-update) | async-done | bytes 4194320 | tf_op jit(solution)/shard_map/all_gather | solution.py:44
  112.8 0.0 collective-permute-start
  112.8 0.0 copy-done
  112.8 4.8 %fusion.19 = (f32[4,128]{1,0:T(4,128)S(1)}, bf16[4,128,1024]{2,1,0:T(8,128)(2,1)S(1)}) fusion(bf16[16,64,1024,1]{2,1,0,3:T(8,128)(2,1)S(1)} %bitcast.92, f32[4,16,128,128]{2,3,1,0:T(8,128)} %get-tuple-element.14, f32[4,16,128]{2,1,0:T(8,128)S(1)} %get-tuple-element.13, bf16[3,4,16,128,64]{3,4,2,0,1:T(8,128)(2,1)} %copy-done.4, f32[1024]{0:T(1024)S(1)} %bitcast.103, ...), kind=kOutput, calls=%fused_computation.35 | convolution fusion | flops 1214250496 | bytes 9476096 | tf_op jit(solution)/shard_map/nhfd,hdo->nfo/dot_general | solution.py:81
  117.6 0.0 copy-start.5
  117.6 0.4 fusion.22
  118.0 0.0 copy-start.9
  118.0 0.8 copy.24
  118.8 35.3 %all_to_all.33 = bf16[4,128,1024]{2,0,1:T(4,128)(2,1)S(1)} all-to-all(bf16[4,128,1024]{2,0,1:T(4,128)(2,1)S(1)} %copy.24), channel_id=1, replica_groups=mesh['grp'=16,'tm'=16] {'tm'}, dimensions={1} | all-to-all | bytes 2097152 | tf_op jit(solution)/shard_map/all_to_all | solution.py:90
  154.1 0.4 copy.49
  154.5 0.0 copy-done.5
  154.5 0.3 all_to_all.27
  154.8 0.1 collective-permute-start.1
  154.9 1.5 collective-permute-start.2
  156.4 0.1 collective-permute-start.3
  156.6 0.6 collective-permute-start.4
  157.2 0.2 dynamic-slice_reduce_fusion
  157.4 0.1 add_compare_fusion
  157.4 0.1 broadcast_in_dim.8
  157.5 0.1 gt.12
  157.6 0.3 reshape.70
  157.9 1.1 constant_dynamic-update-slice_fusion.4
  159.0 18.5 %collective-permute-done.1 = bf16[64,8,1024]{2,0,1:T(8,128)(2,1)} collective-permute-done((bf16[64,8,1024]{2,0,1:T(8,128)(2,1)S(1)}, bf16[64,8,1024]{2,0,1:T(8,128)(2,1)}, u32[]{:S(2)}, u32[]{:S(2)}) %collective-permute-start.1) | collective-permute-done | bytes 1048608 | tf_op jit(solution)/shard_map/ppermute | solution.py:16
  177.5 2.3 constant_dynamic-update-slice_fusion.3
  179.8 23.1 %collective-permute-done.2 = bf16[64,8,1024]{2,0,1:T(8,128)(2,1)} collective-permute-done((bf16[64,8,1024]{2,0,1:T(8,128)(2,1)S(1)}, bf16[64,8,1024]{2,0,1:T(8,128)(2,1)}, u32[]{:S(2)}, u32[]{:S(2)}) %collective-permute-start.2) | collective-permute-done | bytes 1048608 | tf_op jit(solution)/shard_map/ppermute | solution.py:16
  202.9 2.3 constant_dynamic-update-slice_fusion.2
  205.2 0.0 collective-permute-done.3
  205.2 2.3 constant_dynamic-update-slice_fusion.1
  207.4 17.9 %collective-permute-done.4 = bf16[64,8,1024]{2,0,1:T(8,128)(2,1)} collective-permute-done((bf16[64,8,1024]{2,0,1:T(8,128)(2,1)S(1)}, bf16[64,8,1024]{2,0,1:T(8,128)(2,1)}, u32[]{:S(2)}, u32[]{:S(2)}) %collective-permute-start.4) | collective-permute-done | bytes 1048608 | tf_op jit(solution)/shard_map/ppermute | solution.py:16
  225.3 2.3 constant_dynamic-update-slice_fusion
  227.6 0.3 slice.71
  227.9 0.0 collective-permute-done
  227.9 2.1 slice.72
  230.0 3.8 %maximum_select_fusion = bf16[1024,3072]{1,0:T(8,128)(2,1)} fusion(bf16[1024,1536]{1,0:T(8,128)(2,1)S(1)} %slice.72, bf16[1024,1536]{1,0:T(8,128)(2,1)S(1)} %slice.71, pred[]{:T(512)S(6)} %eq.6), kind=kLoop, calls=%fused_computation.9 | loop fusion | flops 28311552 | bytes 12582913 | tf_op jit(solution)/shard_map/jit(_where)/select_n | solution.py:54
  233.8 8.7 %copy.23 = bf16[1024,3072]{0,1:T(8,128)(2,1)} copy(bf16[1024,3072]{1,0:T(8,128)(2,1)} %maximum_select_fusion) | data formatting | bytes 12582912 | tf_op jit(solution)/shard_map/jit(_where)/select_n | solution.py:54
  242.5 16.7 %convert_bitcast_fusion = bf16[2,8,16,320,64]{3,4,1,2,0:T(8,128)(2,1)S(1)} fusion(bf16[320,8,1024]{2,0,1:T(8,128)(2,1)} %constant_dynamic-update-slice_fusion, bf16[1024,3,16,64]{0,3,2,1:T(8,128)(2,1)} %bitcast.93), kind=kOutput, calls=%fused_computation.5 | convolution fusion | flops 10742661120 | bytes 19922944 | tf_op jit(solution)/shard_map/mfk,kthd->tfhmd/dot_general | solution.py:100
  259.2 6.5 %slice_bitcast_fusion.1 = (bf16[8,16,320,64]{2,3,0,1:T(8,128)(2,1)}, bf16[8,16,320,64]{2,3,0,1:T(8,128)(2,1)}) fusion(bf16[2,8,16,320,64]{3,4,1,2,0:T(8,128)(2,1)S(1)} %convert_bitcast_fusion), kind=kLoop, calls=%fused_computation.8 | loop fusion | bytes 20971520 | tf_op jit(solution)/shard_map/squeeze | solution.py:112
  265.6 9.1 %fusion.5 = f32[8,16,64,320]{3,2,1,0:T(8,128)} fusion(bf16[8,16,320,64]{2,3,0,1:T(8,128)(2,1)} %get-tuple-element.6, bf16[1024,3,16,64]{0,3,2,1:T(8,128)(2,1)} %bitcast.94, bf16[64,8,1024,1]{2,0,1,3:T(8,128)(2,1)S(1)} %reshape.70), kind=kOutput, calls=%fused_computation.12 | convolution fusion | flops 1409810432 | bytes 19922944 | tf_op jit(solution)/shard_map/fhcd,fhmd->fhcm/dot_general | solution.py:103
  274.7 14.4 %fusion.60 = (f32[8,16,64]{2,1,0:T(8,128)S(1)}, f32[8,16,64,320]{3,2,1,0:T(8,128)}) fusion(f32[8,16,64,320]{3,2,1,0:T(8,128)} %fusion.5, pred[320]{0:T(512)(128)(4,1)S(1)} %gt.12), kind=kOutput, calls=%fused_computation.90 | output fusion | flops 15728959 | bytes 21004608 | tf_op jit(solution)/shard_map/sub | solution.py:30
  289.1 6.0 %fusion.38 = bf16[8,16,64,64]{3,2,1,0:T(8,128)(2,1)S(1)} fusion(f32[8,16,64,320]{3,2,1,0:T(8,128)} %get-tuple-element.18, f32[8,16,64]{2,1,0:T(8,128)S(1)} %get-tuple-element.17, bf16[8,16,320,64]{2,3,0,1:T(8,128)(2,1)S(1)} %copy-done.2), kind=kOutput, calls=%fused_computation.56 | convolution fusion | flops 341311488 | bytes 16809984 | tf_op jit(solution)/shard_map/fhcm,fhmd->cfhd/dot_general | solution.py:111
  295.1 0.0 copy-start.6
  295.1 2.6 copy.29
  297.8 4.3 %all-to-all-start.1 = ((bf16[64,8,1024]{2,1,0:T(8,128)(2,1)}), bf16[64,8,1024]{2,1,0:T(8,128)(2,1)}, u32[]{:S(2)}, u32[]{:S(2)}) async-start(bf16[64,8,1024]{2,1,0:T(8,128)(2,1)} %copy.29), calls=%async_computation.1 | async-start | bytes 2097152 | tf_op jit(solution)/shard_map/all_to_all | solution.py:114
  302.1 2.3 slice.77
  304.4 2.3 slice.78
  306.7 26.3 %all-to-all-done.1 = bf16[64,8,1024]{2,1,0:T(8,128)(2,1)} async-done(((bf16[64,8,1024]{2,1,0:T(8,128)(2,1)}), bf16[64,8,1024]{2,1,0:T(8,128)(2,1)}, u32[]{:S(2)}, u32[]{:S(2)}) %all-to-all-start.1) | async-done | bytes 1048608 | tf_op jit(solution)/shard_map/all_to_all | solution.py:114
  333.0 4.9 %fusion.23 = bf16[4,128,1024]{2,1,0:T(8,128)(2,1)} fusion(bf16[4,128,1024]{2,1,0:T(8,128)(2,1)S(1)} %copy-done.6, bf16[1024,512]{1,0:T(8,128)(2,1)} %slice.78, bf16[1024,512]{1,0:T(8,128)(2,1)} %slice.77, pred[]{:T(512)S(6)} %eq.6, bf16[4,16,8,1024]{3,2,0,1:T(8,128)(2,1)} %bitcast.35, f32[1024]{0:T(1024)S(1)} %bitcast.102), kind=kOutput, calls=%fused_computation.39 | convolution fusion | flops 1085276160 | bytes 5246977 | tf_op jit(solution)/shard_map/dot_general | solution.py:121
  (11 shorter events, 0.1 us)
Async XLA Ops:
  6.5 106.3 %copy-start = (bf16[1024,1024]{1,0:T(8,128)(2,1)S(1)}, bf16[1024,1024]{1,0:T(8,128)(2,1)}, u32[]{:S(2)}) copy-start(bf16[1024,1024]{1,0:T(8,128)(2,1)} %param.10) | copy-start | bytes 6291460
  6.5 106.2 %all-gather.2.cloned.1.call-start = ((), (), s32[]{:S(2)}) async-start(), calls=%async_computation.2 | async-start | bytes 4456448 | tf_op jit(solution)/shard_map/all_gather | solution.py:44
  9.2 8.8 %copy-start.7 = (bf16[4,128,1024]{2,1,0:T(8,128)(2,1)S(1)}, bf16[4,128,1024]{2,1,0:T(8,128)(2,1)}, u32[]{:S(2)}) copy-start(bf16[4,128,1024]{2,1,0:T(8,128)(2,1)} %param.7) | copy-start | bytes 3145732
  9.2 9.0 %copy-start.8 = (f32[6,1024]{1,0:T(8,128)S(1)}, f32[6,1024]{1,0:T(8,128)}, u32[]{:S(2)}) copy-start(f32[6,1024]{1,0:T(8,128)} %param.8) | copy-start | bytes 73732
  24.2 1.7 copy-start.4
  112.8 115.1 %collective-permute-start = (bf16[1024,2048]{1,0:T(8,128)(2,1)}, bf16[1024,2048]{1,0:T(8,128)(2,1)}, u32[]{:S(2)}, u32[]{:S(2)}) collective-permute-start(bf16[1024,2048]{1,0:T(8,128)(2,1)} %all-gather.2.cloned.1.call-done), channel_id=1, source_target_pairs={{0,16},{16,0},{32,48},{48,32},{64,80},{80,64},{96,112},{112,96},{1... | collective-permute-start | bytes 12582920 | tf_op jit(solution)/shard_map/ppermute | solution.py:46
  117.6 36.9 %copy-start.5 = (bf16[4,128,1024]{2,1,0:T(8,128)(2,1)}, bf16[4,128,1024]{2,1,0:T(8,128)(2,1)S(1)}, u32[]{:S(2)}) copy-start(bf16[4,128,1024]{2,1,0:T(8,128)(2,1)S(1)} %get-tuple-element.16) | copy-start | bytes 3145732
  118.0 39.2 %copy-start.9 = (s32[16,4]{0,1:T(4,128)S(1)}, s32[16,4]{0,1:T(4,128)}, u32[]{:S(2)}) copy-start(s32[16,4]{0,1:T(4,128)} %param.13) | copy-start | bytes 772
  154.8 22.7 %collective-permute-start.1 = (bf16[64,8,1024]{2,0,1:T(8,128)(2,1)S(1)}, bf16[64,8,1024]{2,0,1:T(8,128)(2,1)}, u32[]{:S(2)}, u32[]{:S(2)}) collective-permute-start(bf16[64,8,1024]{2,0,1:T(8,128)(2,1)S(1)} %all_to_all.27), channel_id=1, source_target_pairs={{16,0},{32,16},{48,32},{64,48},{80,64},{96,80},{112,96},{128,112},... | collective-permute-start | bytes 3145736 | tf_op jit(solution)/shard_map/ppermute | solution.py:16
  154.9 47.9 %collective-permute-start.2 = (bf16[64,8,1024]{2,0,1:T(8,128)(2,1)S(1)}, bf16[64,8,1024]{2,0,1:T(8,128)(2,1)}, u32[]{:S(2)}, u32[]{:S(2)}) collective-permute-start(bf16[64,8,1024]{2,0,1:T(8,128)(2,1)S(1)} %all_to_all.27), channel_id=1, source_target_pairs={{32,0},{48,16},{64,32},{80,48},{96,64},{112,80},{128,96},{144,112}... | collective-permute-start | bytes 3145736 | tf_op jit(solution)/shard_map/ppermute | solution.py:16
  156.4 48.7 %collective-permute-start.3 = (bf16[64,8,1024]{2,0,1:T(8,128)(2,1)S(1)}, bf16[64,8,1024]{2,0,1:T(8,128)(2,1)}, u32[]{:S(2)}, u32[]{:S(2)}) collective-permute-start(bf16[64,8,1024]{2,0,1:T(8,128)(2,1)S(1)} %all_to_all.27), channel_id=1, source_target_pairs={{240,0},{0,16},{16,32},{32,48},{48,64},{64,80},{80,96},{96,112},{1... | collective-permute-start | bytes 3145736 | tf_op jit(solution)/shard_map/ppermute | solution.py:16
  156.6 68.7 %collective-permute-start.4 = (bf16[64,8,1024]{2,0,1:T(8,128)(2,1)S(1)}, bf16[64,8,1024]{2,0,1:T(8,128)(2,1)}, u32[]{:S(2)}, u32[]{:S(2)}) collective-permute-start(bf16[64,8,1024]{2,0,1:T(8,128)(2,1)S(1)} %all_to_all.27), channel_id=1, source_target_pairs={{224,0},{240,16},{0,32},{16,48},{32,64},{48,80},{64,96},{80,112},{... | collective-permute-start | bytes 3145736 | tf_op jit(solution)/shard_map/ppermute | solution.py:16
  159.0 68.6 %copy-start.3 = (bf16[1024,2048]{1,0:T(8,128)(2,1)S(1)}, bf16[1024,2048]{1,0:T(8,128)(2,1)}, u32[]{:S(2)}) copy-start(bf16[1024,2048]{1,0:T(8,128)(2,1)} %all-gather.2.cloned.1.call-done) | copy-start | bytes 12582916
  274.7 14.4 %copy-start.2 = (bf16[8,16,320,64]{2,3,0,1:T(8,128)(2,1)S(1)}, bf16[8,16,320,64]{2,3,0,1:T(8,128)(2,1)}, u32[]{:S(2)}) copy-start(bf16[8,16,320,64]{2,3,0,1:T(8,128)(2,1)} %get-tuple-element.5) | copy-start | bytes 15728644
  295.1 37.9 %copy-start.6 = (bf16[4,128,1024]{2,1,0:T(8,128)(2,1)S(1)}, bf16[4,128,1024]{2,1,0:T(8,128)(2,1)}, u32[]{:S(2)}) copy-start(bf16[4,128,1024]{2,1,0:T(8,128)(2,1)} %copy-done.5) | copy-start | bytes 3145732
  297.8 35.2 %all-to-all-start.1 = ((bf16[64,8,1024]{2,1,0:T(8,128)(2,1)}), bf16[64,8,1024]{2,1,0:T(8,128)(2,1)}, u32[]{:S(2)}, u32[]{:S(2)}) async-start(bf16[64,8,1024]{2,1,0:T(8,128)(2,1)} %copy.29), calls=%async_computation.1 | async-start | bytes 2097152 | tf_op jit(solution)/shard_map/all_to_all | solution.py:114
  333.0 4.9 %copy-start.1 = (bf16[1024,1024]{1,0:T(8,128)(2,1)S(1)}, bf16[1024,1024]{1,0:T(8,128)(2,1)}, u32[]{:S(2)}) copy-start(bf16[1024,1024]{1,0:T(8,128)(2,1)} %param.10) | copy-start | bytes 6291460
Sparse Core Ops, SparseCore 0:
  9.9 102.8 all-gather.1

commit v3 on v2

--- a/solution.py
+++ b/solution.py
@@ -31,7 +31,7 @@
     return (weights / jnp.sum(weights, axis=-1, keepdims=True)).astype(jnp.bfloat16)
 
 
-def gather_split_by_core(shards, axis_small, axis_pair):
+def gather_half_by_core(shards, axis_small, axis_pair):
     pair_index = lax.axis_index(axis_pair) % 2
     halves = [shard.shape[1] // 2 for shard in shards]
     mine = jnp.concatenate(
@@ -41,7 +41,11 @@
         ],
         axis=1,
     )
-    gathered = lax.all_gather(mine, axis_small, axis=0, tiled=True)
+    return lax.all_gather(mine, axis_small, axis=0, tiled=True), halves
+
+
+def swap_halves(gathered, halves, axis_pair):
+    pair_index = lax.axis_index(axis_pair) % 2
     count = lax.axis_size(axis_pair)
     other = lax.ppermute(gathered, axis_pair, [(i, i ^ 1) for i in range(count)])
     results = []
@@ -64,7 +68,7 @@
     own_chars, all_frames, feature_width = motion.shape
     head_count = feature_width // HEAD
     scale = HEAD ** (-0.5)
-    inter_qkv, inter_out = gather_split_by_core((w_inter_qkv, w_inter_out), "tm", "grp")
+    gathered, halves = gather_half_by_core((w_inter_qkv, w_inter_out), "tm", "grp")
 
     normed = modulate(motion, modulation, 0, 1)
     t_w = w_temporal_qkv.reshape(feature_width, 3, head_count, HEAD)
@@ -90,13 +94,15 @@
     frames_own = lax.all_to_all(normed_inter, "tm", split_axis=1, concat_axis=0, tiled=True)
     offsets = [j + 1 for j in range(REACH)] + [-(j + 1) for j in range(REACH)]
     others = [from_group(frames_own, "grp", offset) for offset in offsets]
-    stacked = jnp.concatenate([frames_own] + others, axis=0)
+    gathered, *others = lax.optimization_barrier((gathered, *others))
+    inter_qkv, inter_out = swap_halves(gathered, halves, "grp")
     char_count, frame_count, unused_width = frames_own.shape
 
     i_w = inter_qkv.reshape(feature_width, 3, head_count, HEAD)
     queries = jnp.einsum(
         "cfk,khd->fhcd", frames_own, i_w[:, 0], preferred_element_type=jnp.float32
     ).astype(jnp.bfloat16)
+    stacked = jnp.concatenate([frames_own] + others, axis=0)
     pairs = jnp.einsum(
         "mfk,kthd->tfhmd", stacked, i_w[:, 1:], preferred_element_type=jnp.float32
     ).astype(jnp.bfloat16)

time: 346 us -> 290 us (0.84)
  waiting for transfers between devices: 169 us -> 104 us
  starting transfers between devices: 6.67 us -> 14.1 us
  blocking collectives: 35.3 us -> 42.2 us
  local copies, waits for them, and re-layouts: 49.4 us -> 44.6 us
    all_gather x1, waiting for transfers between devices: 83.2 us -> 0.01 us  [gather_half_by_core(): return (lax.all_gather(mine, axis_small, axis=0, tiled=True), halves)]
    ppermute x4, waiting for transfers between devices: 59.5 us -> 78.1 us  [from_group(): return lax.ppermute(block, axis, route)]
    all_to_all x1, blocking collectives: 35.3 us -> 42.2 us  [per_device(): lax.all_to_all(normed_inter, 'tm', split_axis=1, concat_axis=0, tiled=True)]
    unnamed x25 -> x37, local copies, waits for them, and re-layouts: 18.4 us -> 13.8 us
    all_to_all x1, starting transfers between devices: 4.34 us -> 8.27 us  [per_device(): lax.all_to_all(mixed_heads.reshape(char_count, frame_count, feature_width...]
where the time goes in v3:
time: 290 us
  waiting for transfers between devices  104 us (36%)
  matrix products  48.1 us (17%)
  local copies, waits for them, and re-layouts  44.6 us (15%)
  blocking collectives  42.2 us (15%)
  other arithmetic  22.7 us (8%)
  starting transfers between devices  14.1 us (5%)
  between operations  13.7 us (5%)
    ppermute x4, waiting for transfers between devices, from_group(): return lax.ppermute(block, axis, route)  78.1 us
    all_to_all x1, blocking collectives, per_device(): lax.all_to_all(normed_inter, 'tm', split_axis=1, concat_axis=0, tiled=True)  42.2 us
    all_to_all x1, waiting for transfers between devices, per_device(): lax.all_to_all(mixed_heads.reshape(char_count, frame_count, feature_width...  26.2 us
    sub x2, other arithmetic, softmax_rows(): weights = jnp.exp(scores - row_top)  17.4 us
    dot_general x1, matrix products, per_device(): jnp.einsum('mfk,kthd->tfhmd', stacked, i_w[:, 1:], preferred_element_type...  16.7 us
    unnamed x37, local copies, waits for them, and re-layouts  13.8 us
    dot_general x1, matrix products, per_device(): jnp.einsum('fhcd,fhmd->fhcm', queries, pairs[0], preferred_element_type=j...  9.06 us
    select_n x1, local copies, waits for them, and re-layouts, swap_halves(): jnp.where(pair_index == 0, jnp.concatenate([own_part, other_part], axis=1...  8.65 us
  transfers between devices with their start and end apart: 7, of which 5 were waited for; matrix products, arithmetic and copies ran while one was open for 12% of the time, Pallas kernels for 0%

profile of v3, /device:TPU:8, one launch (start us, length us, event | category | flops | bytes accessed | tf_op | source)
XLA Modules:
  0.0 289.6 jit_solution(6086072957334108867)
XLA Ops:
  6.5 0.0 copy-start
  6.5 0.0 all-gather.2.cloned.1.call-start
  6.5 1.0 constant_dynamic-slice_fusion
  7.5 0.9 constant_dynamic-slice_fusion.1
  8.5 0.7 pad_maximum_fusion
  9.2 0.0 all-gather.2.cloned.1.call-update
  9.2 0.0 copy-start.6
  9.2 0.0 copy-start.14
  9.2 8.7 %copy.21 = bf16[1024,3072]{0,1:T(8,128)(2,1)} copy(bf16[1024,3072]{1,0:T(8,128)(2,1)} %param.9) | data formatting | bytes 12582912 | tf_op args[2]
  18.0 0.3 fusion.14
  18.2 0.0 copy-done.14
  18.3 5.9 %convert_bitcast_fusion.1 = bf16[3,4,16,128,64]{3,4,2,0,1:T(8,128)(2,1)S(1)} fusion(bf16[1024,3,16,64,1]{0,3,2,1,4:T(8,128)(2,1)} %bitcast.97, bf16[4,128,1024]{2,1,0:T(8,128)(2,1)S(1)} %copy-done.6, f32[1024]{0:T(1024)S(1)} %bitcast.104, f32[1024]{0:T(1024)S(1)} %bitcast.105, f32[4,128]{1,0:T(4,128)S(1)} %add_rsqrt_fusion.1), kind=kOutput, calls=%fused_computation.26 | convolution fusion | flops 3225419776 | bytes 10496000 | tf_op jit(solution)/shard_map/nfk,kshd->snhfd/dot_general | solution.py:75
  24.2 0.0 copy-start.3
  24.2 0.8 fusion.46
  25.0 2.9 %fusion.59 = (f32[4,16,128]{2,1,0:T(8,128)S(1)}, f32[4,16,128,128]{2,3,1,0:T(8,128)}) fusion(f32[4,16,128,128]{2,3,1,0:T(8,128)S(1)} %fusion.46), kind=kOutput, calls=%fused_computation.89 | output fusion | flops 4194431 | bytes 8421376 | tf_op jit(solution)/shard_map/sub | solution.py:30
  27.9 0.0 copy-done
  27.9 4.8 %fusion.19 = (f32[4,128]{1,0:T(4,128)S(1)}, bf16[4,128,1024]{2,1,0:T(8,128)(2,1)S(1)}) fusion(bf16[16,64,1024,1]{2,1,0,3:T(8,128)(2,1)S(1)} %bitcast.92, f32[4,16,128,128]{2,3,1,0:T(8,128)} %get-tuple-element.24, f32[4,16,128]{2,1,0:T(8,128)S(1)} %get-tuple-element.23, bf16[3,4,16,128,64]{3,4,2,0,1:T(8,128)(2,1)} %copy-done.3, f32[1024]{0:T(1024)S(1)} %bitcast.103, ...), kind=kOutput, calls=%fused_computation.35 | convolution fusion | flops 1214250496 | bytes 9476096 | tf_op jit(solution)/shard_map/nhfd,hdo->nfo/dot_general | solution.py:85
  32.7 0.0 copy-start.4
  32.8 0.4 fusion.22
  33.1 0.0 copy-start.15
  33.1 0.8 copy.23
  34.0 42.2 %all_to_all.33 = bf16[4,128,1024]{2,0,1:T(4,128)(2,1)S(1)} all-to-all(bf16[4,128,1024]{2,0,1:T(4,128)(2,1)S(1)} %copy.23), channel_id=1, replica_groups=mesh['grp'=16,'tm'=16] {'tm'}, dimensions={1} | all-to-all | bytes 2097152 | tf_op jit(solution)/shard_map/all_to_all | solution.py:94
  76.1 0.4 copy.49
  76.5 0.3 all_to_all.27
  76.8 1.5 collective-permute-start.3
  78.3 0.0 collective-permute-start.2
  78.3 1.5 collective-permute-start.1
  79.8 1.5 collective-permute-start
  81.3 36.3 %collective-permute-done.3 = bf16[64,8,1024]{2,0,1:T(8,128)(2,1)S(1)} collective-permute-done((bf16[64,8,1024]{2,0,1:T(8,128)(2,1)S(1)}, bf16[64,8,1024]{2,0,1:T(8,128)(2,1)S(1)}, u32[]{:S(2)}, u32[]{:S(2)}) %collective-permute-start.3) | collective-permute-done | bytes 1048608 | tf_op jit(solution)/shard_map/ppermute | solution.py:16
  117.6 21.1 %collective-permute-done.2 = bf16[64,8,1024]{2,0,1:T(8,128)(2,1)S(1)} collective-permute-done((bf16[64,8,1024]{2,0,1:T(8,128)(2,1)S(1)}, bf16[64,8,1024]{2,0,1:T(8,128)(2,1)S(1)}, u32[]{:S(2)}, u32[]{:S(2)}) %collective-permute-start.2) | collective-permute-done | bytes 1048608 | tf_op jit(solution)/shard_map/ppermute | solution.py:16
  138.7 1.5 collective-permute-done.1
  140.2 1.0 copy-done.11
  141.2 19.2 %collective-permute-done = bf16[64,8,1024]{2,0,1:T(8,128)(2,1)} collective-permute-done((bf16[64,8,1024]{2,0,1:T(8,128)(2,1)S(1)}, bf16[64,8,1024]{2,0,1:T(8,128)(2,1)}, u32[]{:S(2)}, u32[]{:S(2)}) %collective-permute-start) | collective-permute-done | bytes 1048608 | tf_op jit(solution)/shard_map/ppermute | solution.py:16
  160.4 1.3 collective-permute-start.4
  161.7 0.0 copy-done.15
  161.7 0.2 dynamic-slice_reduce_fusion
  161.9 0.1 add_compare_fusion
  162.0 0.1 broadcast_in_dim.8
  162.1 0.1 gt.12
  162.2 0.3 reshape.70
  162.4 0.1 constant_dynamic-update-slice_fusion.4
  162.5 2.2 slice.60
  164.8 1.4 constant_dynamic-update-slice_fusion.3
  166.2 0.0 copy-done.12
  166.2 0.1 constant_dynamic-update-slice_fusion.2
  166.3 0.1 constant_dynamic-update-slice_fusion.1
  166.4 0.1 constant_dynamic-update-slice_fusion
  166.5 2.4 copy-done.13
  168.9 0.0 collective-permute-done.4
  168.9 2.1 slice.71
  171.0 3.8 %maximum_select_fusion = bf16[1024,3072]{1,0:T(8,128)(2,1)} fusion(bf16[1024,1536]{1,0:T(8,128)(2,1)S(1)} %slice.71, bf16[1024,1536]{1,0:T(8,128)(2,1)S(1)} %slice.60, pred[]{:T(512)S(6)} %eq.7), kind=kLoop, calls=%fused_computation.9 | loop fusion | flops 28311552 | bytes 12582913 | tf_op jit(solution)/shard_map/jit(_where)/select_n | solution.py:58
  174.8 8.6 %copy.25 = bf16[1024,3072]{0,1:T(8,128)(2,1)} copy(bf16[1024,3072]{1,0:T(8,128)(2,1)} %maximum_select_fusion) | data formatting | bytes 12582912 | tf_op jit(solution)/shard_map/jit(_where)/select_n | solution.py:58
  183.4 16.7 %convert_bitcast_fusion = bf16[2,8,16,320,64]{3,4,1,2,0:T(8,128)(2,1)S(1)} fusion(bf16[320,8,1024]{2,0,1:T(8,128)(2,1)} %copy-done.13, bf16[1024,3,16,64]{0,3,2,1:T(8,128)(2,1)} %bitcast.93), kind=kOutput, calls=%fused_computation.5 | convolution fusion | flops 10742661120 | bytes 19922944 | tf_op jit(solution)/shard_map/mfk,kthd->tfhmd/dot_general | solution.py:106
  200.1 6.5 %slice_bitcast_fusion.1 = (bf16[8,16,320,64]{2,3,0,1:T(8,128)(2,1)}, bf16[8,16,320,64]{2,3,0,1:T(8,128)(2,1)}) fusion(bf16[2,8,16,320,64]{3,4,1,2,0:T(8,128)(2,1)S(1)} %convert_bitcast_fusion), kind=kLoop, calls=%fused_computation.8 | loop fusion | bytes 20971520 | tf_op jit(solution)/shard_map/squeeze | solution.py:118
  206.6 9.1 %fusion.5 = f32[8,16,64,320]{3,2,1,0:T(8,128)} fusion(bf16[8,16,320,64]{2,3,0,1:T(8,128)(2,1)} %get-tuple-element.16, bf16[1024,3,16,64]{0,3,2,1:T(8,128)(2,1)} %bitcast.94, bf16[64,8,1024,1]{2,0,1,3:T(8,128)(2,1)S(1)} %reshape.70), kind=kOutput, calls=%fused_computation.12 | convolution fusion | flops 1409810432 | bytes 19922944 | tf_op jit(solution)/shard_map/fhcd,fhmd->fhcm/dot_general | solution.py:109
  215.7 14.4 %fusion.60 = (f32[8,16,64]{2,1,0:T(8,128)S(1)}, f32[8,16,64,320]{3,2,1,0:T(8,128)}) fusion(f32[8,16,64,320]{3,2,1,0:T(8,128)} %fusion.5, pred[320]{0:T(512)(128)(4,1)S(1)} %gt.12), kind=kOutput, calls=%fused_computation.90 | output fusion | flops 15728959 | bytes 21004608 | tf_op jit(solution)/shard_map/sub | solution.py:30
  230.1 6.0 %fusion.38 = bf16[8,16,64,64]{3,2,1,0:T(8,128)(2,1)S(1)} fusion(f32[8,16,64,320]{3,2,1,0:T(8,128)} %get-tuple-element.28, f32[8,16,64]{2,1,0:T(8,128)S(1)} %get-tuple-element.27, bf16[8,16,320,64]{2,3,0,1:T(8,128)(2,1)S(1)} %copy-done.2), kind=kOutput, calls=%fused_computation.56 | convolution fusion | flops 341311488 | bytes 16809984 | tf_op jit(solution)/shard_map/fhcm,fhmd->cfhd/dot_general | solution.py:117
  236.1 0.0 copy-start.5
  236.1 2.7 copy.29
  238.8 8.3 %all-to-all-start.1 = ((bf16[64,8,1024]{2,1,0:T(8,128)(2,1)}), bf16[64,8,1024]{2,1,0:T(8,128)(2,1)}, u32[]{:S(2)}, u32[]{:S(2)}) async-start(bf16[64,8,1024]{2,1,0:T(8,128)(2,1)} %copy.29), calls=%async_computation.1 | async-start | bytes 2097152 | tf_op jit(solution)/shard_map/all_to_all | solution.py:120
  247.1 2.3 slice.66
  249.4 2.3 slice.76
  251.6 26.2 %all-to-all-done.1 = bf16[64,8,1024]{2,1,0:T(8,128)(2,1)} async-done(((bf16[64,8,1024]{2,1,0:T(8,128)(2,1)}), bf16[64,8,1024]{2,1,0:T(8,128)(2,1)}, u32[]{:S(2)}, u32[]{:S(2)}) %all-to-all-start.1) | async-done | bytes 1048608 | tf_op jit(solution)/shard_map/all_to_all | solution.py:120
  277.8 4.9 %fusion.23 = bf16[4,128,1024]{2,1,0:T(8,128)(2,1)} fusion(bf16[4,128,1024]{2,1,0:T(8,128)(2,1)S(1)} %copy-done.5, bf16[1024,512]{1,0:T(8,128)(2,1)} %slice.76, bf16[1024,512]{1,0:T(8,128)(2,1)} %slice.66, pred[]{:T(512)S(6)} %eq.7, bf16[4,16,8,1024]{3,2,0,1:T(8,128)(2,1)} %bitcast.35, f32[1024]{0:T(1024)S(1)} %bitcast.102), kind=kOutput, calls=%fused_computation.39 | convolution fusion | flops 1085276160 | bytes 5246977 | tf_op jit(solution)/shard_map/dot_general | solution.py:127
  (23 shorter events, 0.1 us)
Async XLA Ops:
  6.5 21.4 %copy-start = (bf16[1024,1024]{1,0:T(8,128)(2,1)S(1)}, bf16[1024,1024]{1,0:T(8,128)(2,1)}, u32[]{:S(2)}) copy-start(bf16[1024,1024]{1,0:T(8,128)(2,1)} %param.10) | copy-start | bytes 6291460
  6.5 153.9 %all-gather.2.cloned.1.call-start = ((), (), s32[]{:S(2)}) async-start(), calls=%async_computation.2 | async-start | bytes 4456448 | tf_op jit(solution)/shard_map/all_gather | solution.py:44
  9.2 8.7 %copy-start.6 = (bf16[4,128,1024]{2,1,0:T(8,128)(2,1)S(1)}, bf16[4,128,1024]{2,1,0:T(8,128)(2,1)}, u32[]{:S(2)}) copy-start(bf16[4,128,1024]{2,1,0:T(8,128)(2,1)} %param.7) | copy-start | bytes 3145732
  9.2 9.0 %copy-start.14 = (f32[6,1024]{1,0:T(8,128)S(1)}, f32[6,1024]{1,0:T(8,128)}, u32[]{:S(2)}) copy-start(f32[6,1024]{1,0:T(8,128)} %param.8) | copy-start | bytes 73732
  24.2 3.7 %copy-start.3 = (bf16[3,4,16,128,64]{3,4,2,0,1:T(8,128)(2,1)}, bf16[3,4,16,128,64]{3,4,2,0,1:T(8,128)(2,1)S(1)}, u32[]{:S(2)}) copy-start(bf16[3,4,16,128,64]{3,4,2,0,1:T(8,128)(2,1)S(1)} %convert_bitcast_fusion.1) | copy-start | bytes 9437188
  32.7 43.8 %copy-start.4 = (bf16[4,128,1024]{2,1,0:T(8,128)(2,1)}, bf16[4,128,1024]{2,1,0:T(8,128)(2,1)S(1)}, u32[]{:S(2)}) copy-start(bf16[4,128,1024]{2,1,0:T(8,128)(2,1)S(1)} %get-tuple-element.26) | copy-start | bytes 3145732
  33.1 128.6 %copy-start.15 = (s32[16,4]{0,1:T(4,128)S(1)}, s32[16,4]{0,1:T(4,128)}, u32[]{:S(2)}) copy-start(s32[16,4]{0,1:T(4,128)} %param.13) | copy-start | bytes 772
  76.8 40.8 %collective-permute-start.3 = (bf16[64,8,1024]{2,0,1:T(8,128)(2,1)S(1)}, bf16[64,8,1024]{2,0,1:T(8,128)(2,1)S(1)}, u32[]{:S(2)}, u32[]{:S(2)}) collective-permute-start(bf16[64,8,1024]{2,0,1:T(8,128)(2,1)S(1)} %all_to_all.27), channel_id=1, source_target_pairs={{224,0},{240,16},{0,32},{16,48},{32,64},{48,80},{64,96},{80,112},{... | collective-permute-start | bytes 3145736 | tf_op jit(solution)/shard_map/ppermute | solution.py:16
  78.3 60.3 %collective-permute-start.2 = (bf16[64,8,1024]{2,0,1:T(8,128)(2,1)S(1)}, bf16[64,8,1024]{2,0,1:T(8,128)(2,1)S(1)}, u32[]{:S(2)}, u32[]{:S(2)}) collective-permute-start(bf16[64,8,1024]{2,0,1:T(8,128)(2,1)S(1)} %all_to_all.27), channel_id=1, source_target_pairs={{240,0},{0,16},{16,32},{32,48},{48,64},{64,80},{80,96},{96,112},{1... | collective-permute-start | bytes 3145736 | tf_op jit(solution)/shard_map/ppermute | solution.py:16
  78.3 61.9 %collective-permute-start.1 = (bf16[64,8,1024]{2,0,1:T(8,128)(2,1)S(1)}, bf16[64,8,1024]{2,0,1:T(8,128)(2,1)S(1)}, u32[]{:S(2)}, u32[]{:S(2)}) collective-permute-start(bf16[64,8,1024]{2,0,1:T(8,128)(2,1)S(1)} %all_to_all.27), channel_id=1, source_target_pairs={{32,0},{48,16},{64,32},{80,48},{96,64},{112,80},{128,96},{144,112}... | collective-permute-start | bytes 3145736 | tf_op jit(solution)/shard_map/ppermute | solution.py:16
  79.8 80.6 %collective-permute-start = (bf16[64,8,1024]{2,0,1:T(8,128)(2,1)S(1)}, bf16[64,8,1024]{2,0,1:T(8,128)(2,1)}, u32[]{:S(2)}, u32[]{:S(2)}) collective-permute-start(bf16[64,8,1024]{2,0,1:T(8,128)(2,1)S(1)} %all_to_all.27), channel_id=1, source_target_pairs={{16,0},{32,16},{48,32},{64,48},{80,64},{96,80},{112,96},{128,112},... | collective-permute-start | bytes 3145736 | tf_op jit(solution)/shard_map/ppermute | solution.py:16
  117.6 22.6 %copy-start.7 = (bf16[64,8,1024]{2,0,1:T(8,128)(2,1)}, bf16[64,8,1024]{2,0,1:T(8,128)(2,1)S(1)}, u32[]{:S(2)}) copy-start(bf16[64,8,1024]{2,0,1:T(8,128)(2,1)S(1)} %collective-permute-done.3) | copy-start | bytes 3145732
  138.7 1.6 copy-start.9
  140.2 1.0 copy-start.11
  160.4 8.5 %collective-permute-start.4 = (bf16[1024,2048]{1,0:T(8,128)(2,1)}, bf16[1024,2048]{1,0:T(8,128)(2,1)}, u32[]{:S(2)}, u32[]{:S(2)}) collective-permute-start(bf16[1024,2048]{1,0:T(8,128)(2,1)} %all-gather.2.cloned.1.call-done), channel_id=1, source_target_pairs={{0,16},{16,0},{32,48},{48,32},{64,80},{80,64},{96,112},{112,96},{1... | collective-permute-start | bytes 12582920 | tf_op jit(solution)/shard_map/ppermute | solution.py:50
  162.5 3.7 %copy-start.12 = (bf16[64,8,1024]{2,0,1:T(8,128)(2,1)S(1)}, bf16[64,8,1024]{2,0,1:T(8,128)(2,1)}, u32[]{:S(2)}) copy-start(bf16[64,8,1024]{2,0,1:T(8,128)(2,1)} %copy-done.11) | copy-start | bytes 3145732
  162.5 3.8 %copy-start.10 = (bf16[64,8,1024]{2,0,1:T(8,128)(2,1)S(1)}, bf16[64,8,1024]{2,0,1:T(8,128)(2,1)}, u32[]{:S(2)}) copy-start(bf16[64,8,1024]{2,0,1:T(8,128)(2,1)} %copy-done.9) | copy-start | bytes 3145732
  164.8 1.6 copy-start.8
  166.5 2.4 copy-start.13
  215.7 14.4 %copy-start.2 = (bf16[8,16,320,64]{2,3,0,1:T(8,128)(2,1)S(1)}, bf16[8,16,320,64]{2,3,0,1:T(8,128)(2,1)}, u32[]{:S(2)}) copy-start(bf16[8,16,320,64]{2,3,0,1:T(8,128)(2,1)} %get-tuple-element.15) | copy-start | bytes 15728644
  236.1 41.7 %copy-start.5 = (bf16[4,128,1024]{2,1,0:T(8,128)(2,1)S(1)}, bf16[4,128,1024]{2,1,0:T(8,128)(2,1)}, u32[]{:S(2)}) copy-start(bf16[4,128,1024]{2,1,0:T(8,128)(2,1)} %copy-done.4) | copy-start | bytes 3145732
  238.8 39.1 %all-to-all-start.1 = ((bf16[64,8,1024]{2,1,0:T(8,128)(2,1)}), bf16[64,8,1024]{2,1,0:T(8,128)(2,1)}, u32[]{:S(2)}, u32[]{:S(2)}) async-start(bf16[64,8,1024]{2,1,0:T(8,128)(2,1)} %copy.29), calls=%async_computation.1 | async-start | bytes 2097152 | tf_op jit(solution)/shard_map/all_to_all | solution.py:120
  277.8 4.9 %copy-start.1 = (bf16[1024,1024]{1,0:T(8,128)(2,1)S(1)}, bf16[1024,1024]{1,0:T(8,128)(2,1)}, u32[]{:S(2)}) copy-start(bf16[1024,1024]{1,0:T(8,128)(2,1)} %param.10) | copy-start | bytes 6291460
Sparse Core Ops, SparseCore 0:
  9.9 126.2 all-gather.1

commit v4 on v3

--- a/solution.py
+++ b/solution.py
@@ -92,9 +92,19 @@
     normed_inter = modulate(middle, modulation, 3, 4)
 
     frames_own = lax.all_to_all(normed_inter, "tm", split_axis=1, concat_axis=0, tiled=True)
-    offsets = [j + 1 for j in range(REACH)] + [-(j + 1) for j in range(REACH)]
-    others = [from_group(frames_own, "grp", offset) for offset in offsets]
-    gathered, *others = lax.optimization_barrier((gathered, *others))
+    pair_index = lax.axis_index("grp") % 2
+    group_count = lax.axis_size("grp")
+    pair_route = [(i, i ^ 1) for i in range(group_count)]
+    ahead_two = from_group(frames_own, "grp", 2)
+    behind_two = from_group(frames_own, "grp", -2)
+    pair_own = lax.ppermute(frames_own, "grp", pair_route)
+    gathered, ahead_two, behind_two = lax.optimization_barrier((gathered, ahead_two, behind_two))
+    relayed = lax.ppermute(
+        jnp.where(pair_index == 0, ahead_two, behind_two), "grp", pair_route
+    )
+    ahead_one = jnp.where(pair_index == 0, pair_own, relayed)
+    behind_one = jnp.where(pair_index == 0, relayed, pair_own)
+    others = [ahead_one, ahead_two, behind_one, behind_two]
     inter_qkv, inter_out = swap_halves(gathered, halves, "grp")
     char_count, frame_count, unused_width = frames_own.shape
 

time: 290 us -> 276 us (0.952)
  waiting for transfers between devices: 104 us -> 89.3 us
  other arithmetic: 22.7 us -> 26.9 us
  starting transfers between devices: 14.1 us -> 11.1 us
    ppermute x4 -> x2, waiting for transfers between devices: 78.1 us -> 59.3 us  [from_group(): return lax.ppermute(block, axis, route)]
    ppermute x0 -> x2, waiting for transfers between devices: none -> 3.94 us  [the longest x1 2.44 us: per_device(): pair_own = lax.ppermute(frames_own, 'grp', pair_route)]
    unnamed x0 -> x2, other arithmetic: none -> 3.26 us
    unnamed x37 -> x25, local copies, waits for them, and re-layouts: 13.8 us -> 12.5 us
  transfers between devices with their start and end apart: 7 -> 7, of which waited for: 5 -> 5; matrix products, arithmetic and copies ran while one was open for 12% -> 14% of each run, Pallas kernels for 0% -> 0%
where the time goes in v4:
time: 276 us
  waiting for transfers between devices  89.3 us (32%)
  matrix products  48.1 us (17%)
  local copies, waits for them, and re-layouts  44.7 us (16%)
  blocking collectives  41.8 us (15%)
  other arithmetic  26.9 us (10%)
  between operations  13.6 us (5%)
  starting transfers between devices  11.1 us (4%)
    ppermute x2, waiting for transfers between devices, from_group(): return lax.ppermute(block, axis, route)  59.3 us
    all_to_all x1, blocking collectives, per_device(): lax.all_to_all(normed_inter, 'tm', split_axis=1, concat_axis=0, tiled=True)  41.8 us
    all_to_all x1, waiting for transfers between devices, per_device(): lax.all_to_all(mixed_heads.reshape(char_count, frame_count, feature_width...  26 us
    sub x2, other arithmetic, softmax_rows(): weights = jnp.exp(scores - row_top)  17.3 us
    dot_general x1, matrix products, per_device(): jnp.einsum('mfk,kthd->tfhmd', stacked, i_w[:, 1:], preferred_element_type...  16.7 us
    unnamed x25, local copies, waits for them, and re-layouts  12.5 us
    dot_general x1, matrix products, per_device(): jnp.einsum('fhcd,fhmd->fhcm', queries, pairs[0], preferred_element_type=j...  9.05 us
    select_n x1, local copies, waits for them, and re-layouts, swap_halves(): jnp.where(pair_index == 0, jnp.concatenate([own_part, other_part], axis=1...  8.62 us
  transfers between devices with their start and end apart: 7, of which 5 were waited for; matrix products, arithmetic and copies ran while one was open for 14% of the time, Pallas kernels for 0%

profile of v4, /device:TPU:8, one launch (start us, length us, event | category | flops | bytes accessed | tf_op | source)
XLA Modules:
  0.0 275.5 jit_solution(5627433274881251307)
XLA Ops:
  6.5 0.0 copy-start
  6.5 0.0 all-gather.2.cloned.1.call-start
  6.5 1.0 constant_dynamic-slice_fusion
  7.5 0.9 constant_dynamic-slice_fusion.1
  8.5 0.7 pad_maximum_fusion
  9.2 0.0 all-gather.2.cloned.1.call-update
  9.2 0.0 copy-start.7
  9.2 0.0 copy-start.9
  9.2 8.7 %copy.21 = bf16[1024,3072]{0,1:T(8,128)(2,1)} copy(bf16[1024,3072]{1,0:T(8,128)(2,1)} %param.9) | data formatting | bytes 12582912 | tf_op args[2]
  17.9 0.0 copy-done.7
  17.9 0.3 fusion.14
  18.2 0.0 copy-done.9
  18.3 5.9 %convert_bitcast_fusion.1 = bf16[3,4,16,128,64]{3,4,2,0,1:T(8,128)(2,1)S(1)} fusion(bf16[1024,3,16,64,1]{0,3,2,1,4:T(8,128)(2,1)} %bitcast.97, bf16[4,128,1024]{2,1,0:T(8,128)(2,1)S(1)} %copy-done.7, f32[1024]{0:T(1024)S(1)} %bitcast.104, f32[1024]{0:T(1024)S(1)} %bitcast.105, f32[4,128]{1,0:T(4,128)S(1)} %add_rsqrt_fusion.1), kind=kOutput, calls=%fused_computation.26 | convolution fusion | flops 3225419776 | bytes 10496000 | tf_op jit(solution)/shard_map/nfk,kshd->snhfd/dot_general | solution.py:75
  24.2 0.0 copy-start.4
  24.2 0.8 fusion.46
  25.0 2.9 %fusion.59 = (f32[4,16,128]{2,1,0:T(8,128)S(1)}, f32[4,16,128,128]{2,3,1,0:T(8,128)}) fusion(f32[4,16,128,128]{2,3,1,0:T(8,128)S(1)} %fusion.46), kind=kOutput, calls=%fused_computation.90 | output fusion | flops 4194431 | bytes 8421376 | tf_op jit(solution)/shard_map/sub | solution.py:30
  27.9 4.8 %fusion.19 = (f32[4,128]{1,0:T(4,128)S(1)}, bf16[4,128,1024]{2,1,0:T(8,128)(2,1)S(1)}) fusion(bf16[16,64,1024,1]{2,1,0,3:T(8,128)(2,1)S(1)} %bitcast.92, f32[4,16,128,128]{2,3,1,0:T(8,128)} %get-tuple-element.20, f32[4,16,128]{2,1,0:T(8,128)S(1)} %get-tuple-element.19, bf16[3,4,16,128,64]{3,4,2,0,1:T(8,128)(2,1)} %copy-done.4, f32[1024]{0:T(1024)S(1)} %bitcast.103, ...), kind=kOutput, calls=%fused_computation.35 | convolution fusion | flops 1214250496 | bytes 9476096 | tf_op jit(solution)/shard_map/nhfd,hdo->nfo/dot_general | solution.py:85
  32.7 0.0 copy-start.5
  32.7 0.4 fusion.22
  33.1 0.8 copy.23
  33.9 41.8 %all_to_all.33 = bf16[4,128,1024]{2,0,1:T(4,128)(2,1)S(1)} all-to-all(bf16[4,128,1024]{2,0,1:T(4,128)(2,1)S(1)} %copy.23), channel_id=1, replica_groups=mesh['grp'=16,'tm'=16] {'tm'}, dimensions={1} | all-to-all | bytes 2097152 | tf_op jit(solution)/shard_map/all_to_all | solution.py:94
  75.8 0.4 copy.49
  76.1 0.0 copy-done.5
  76.2 1.1 all_to_all.27
  77.3 1.2 collective-permute-start.1
  78.5 1.7 collective-permute-start
  80.2 37.4 %collective-permute-done.1 = bf16[64,8,1024]{2,0,1:T(8,128)(2,1)S(1)} collective-permute-done((bf16[64,8,1024]{2,0,1:T(8,128)(2,1)}, bf16[64,8,1024]{2,0,1:T(8,128)(2,1)S(1)}, u32[]{:S(2)}, u32[]{:S(2)}) %collective-permute-start.1) | collective-permute-done | bytes 1048608 | tf_op jit(solution)/shard_map/ppermute | solution.py:16
  117.6 22.0 %collective-permute-done = bf16[64,8,1024]{2,0,1:T(8,128)(2,1)S(1)} collective-permute-done((bf16[64,8,1024]{2,0,1:T(8,128)(2,1)}, bf16[64,8,1024]{2,0,1:T(8,128)(2,1)S(1)}, u32[]{:S(2)}, u32[]{:S(2)}) %collective-permute-start) | collective-permute-done | bytes 1048608 | tf_op jit(solution)/shard_map/ppermute | solution.py:16
  139.5 0.0 collective-permute-start.2
  139.5 0.5 collective-permute-start.3
  140.1 1.1 broadcast_select_fusion
  141.1 0.0 collective-permute-start.4
  141.1 0.0 copy-done.10
  141.1 0.2 dynamic-slice_reduce_fusion
  141.3 0.1 add_compare_fusion
  141.4 0.1 broadcast_in_dim.8
  141.5 0.1 gt.12
  141.6 1.1 reshape.70
  142.7 1.3 constant_dynamic-update-slice_fusion.2
  144.0 2.1 slice.60
  146.1 2.4 collective-permute-done.3
  148.5 1.5 collective-permute-done.4
  150.0 1.6 select_dynamic-update-slice_fusion.1
  151.7 0.1 constant_dynamic-update-slice_fusion.1
  151.8 1.6 select_dynamic-update-slice_fusion
  153.4 0.1 constant_dynamic-update-slice_fusion
  153.5 2.4 copy-done.8
  155.9 0.0 collective-permute-done.2
  155.9 2.1 slice.71
  158.0 3.8 %maximum_select_fusion = bf16[1024,3072]{1,0:T(8,128)(2,1)} fusion(bf16[1024,1536]{1,0:T(8,128)(2,1)S(1)} %slice.71, bf16[1024,1536]{1,0:T(8,128)(2,1)S(1)} %slice.60, pred[]{:T(512)S(6)} %eq.6), kind=kLoop, calls=%fused_computation.9 | loop fusion | flops 28311552 | bytes 12582913 | tf_op jit(solution)/shard_map/jit(_where)/select_n | solution.py:58
  161.8 8.6 %copy.25 = bf16[1024,3072]{0,1:T(8,128)(2,1)} copy(bf16[1024,3072]{1,0:T(8,128)(2,1)} %maximum_select_fusion) | data formatting | bytes 12582912 | tf_op jit(solution)/shard_map/jit(_where)/select_n | solution.py:58
  170.4 16.7 %convert_bitcast_fusion = bf16[2,8,16,320,64]{3,4,1,2,0:T(8,128)(2,1)S(1)} fusion(bf16[320,8,1024]{2,0,1:T(8,128)(2,1)} %copy-done.8, bf16[1024,3,16,64]{0,3,2,1:T(8,128)(2,1)} %bitcast.93), kind=kOutput, calls=%fused_computation.5 | convolution fusion | flops 10742661120 | bytes 19922944 | tf_op jit(solution)/shard_map/mfk,kthd->tfhmd/dot_general | solution.py:116
  187.2 0.0 copy-start.3
  187.2 6.5 %slice_bitcast_fusion.1 = (bf16[8,16,320,64]{2,3,0,1:T(8,128)(2,1)}, bf16[8,16,320,64]{2,3,0,1:T(8,128)(2,1)}) fusion(bf16[2,8,16,320,64]{3,4,1,2,0:T(8,128)(2,1)S(1)} %convert_bitcast_fusion), kind=kLoop, calls=%fused_computation.8 | loop fusion | bytes 20971520 | tf_op jit(solution)/shard_map/squeeze | solution.py:128
  193.7 9.0 %fusion.5 = f32[8,16,64,320]{3,2,1,0:T(8,128)} fusion(bf16[8,16,320,64]{2,3,0,1:T(8,128)(2,1)} %get-tuple-element.12, bf16[1024,3,16,64]{0,3,2,1:T(8,128)(2,1)} %bitcast.94, bf16[64,8,1024,1]{2,0,1,3:T(8,128)(2,1)S(1)} %copy-done.3), kind=kOutput, calls=%fused_computation.12 | convolution fusion | flops 1409810432 | bytes 19922944 | tf_op jit(solution)/shard_map/fhcd,fhmd->fhcm/dot_general | solution.py:119
  202.7 14.4 %fusion.60 = (f32[8,16,64]{2,1,0:T(8,128)S(1)}, f32[8,16,64,320]{3,2,1,0:T(8,128)}) fusion(f32[8,16,64,320]{3,2,1,0:T(8,128)} %fusion.5, pred[320]{0:T(512)(128)(4,1)S(1)} %gt.12), kind=kOutput, calls=%fused_computation.91 | output fusion | flops 15728959 | bytes 21004608 | tf_op jit(solution)/shard_map/sub | solution.py:30
  217.1 6.0 %fusion.38 = bf16[8,16,64,64]{3,2,1,0:T(8,128)(2,1)S(1)} fusion(f32[8,16,64,320]{3,2,1,0:T(8,128)} %get-tuple-element.24, f32[8,16,64]{2,1,0:T(8,128)S(1)} %get-tuple-element.23, bf16[8,16,320,64]{2,3,0,1:T(8,128)(2,1)S(1)} %copy-done.2), kind=kOutput, calls=%fused_computation.56 | convolution fusion | flops 341311488 | bytes 16809984 | tf_op jit(solution)/shard_map/fhcm,fhmd->cfhd/dot_general | solution.py:127
  223.1 0.0 copy-start.6
  223.1 2.4 copy.29
  225.5 7.6 %all-to-all-start.1 = ((bf16[64,8,1024]{2,1,0:T(8,128)(2,1)}), bf16[64,8,1024]{2,1,0:T(8,128)(2,1)}, u32[]{:S(2)}, u32[]{:S(2)}) async-start(bf16[64,8,1024]{2,1,0:T(8,128)(2,1)} %copy.29), calls=%async_computation.1 | async-start | bytes 2097152 | tf_op jit(solution)/shard_map/all_to_all | solution.py:130
  233.2 2.3 slice.66
  235.5 2.3 slice.76
  237.7 26.0 %all-to-all-done.1 = bf16[64,8,1024]{2,1,0:T(8,128)(2,1)} async-done(((bf16[64,8,1024]{2,1,0:T(8,128)(2,1)}), bf16[64,8,1024]{2,1,0:T(8,128)(2,1)}, u32[]{:S(2)}, u32[]{:S(2)}) %all-to-all-start.1) | async-done | bytes 1048608 | tf_op jit(solution)/shard_map/all_to_all | solution.py:130
  263.7 4.9 %fusion.23 = bf16[4,128,1024]{2,1,0:T(8,128)(2,1)} fusion(bf16[4,128,1024]{2,1,0:T(8,128)(2,1)S(1)} %copy-done.6, bf16[1024,512]{1,0:T(8,128)(2,1)} %slice.76, bf16[1024,512]{1,0:T(8,128)(2,1)} %slice.66, pred[]{:T(512)S(6)} %eq.6, bf16[4,16,8,1024]{3,2,0,1:T(8,128)(2,1)} %bitcast.35, f32[1024]{0:T(1024)S(1)} %bitcast.102), kind=kOutput, calls=%fused_computation.39 | convolution fusion | flops 1085276160 | bytes 5246977 | tf_op jit(solution)/shard_map/dot_general | solution.py:137
  (14 shorter events, 0.1 us)
Async XLA Ops:
  6.5 21.4 %copy-start = (bf16[1024,1024]{1,0:T(8,128)(2,1)S(1)}, bf16[1024,1024]{1,0:T(8,128)(2,1)}, u32[]{:S(2)}) copy-start(bf16[1024,1024]{1,0:T(8,128)(2,1)} %param.10) | copy-start | bytes 6291460
  6.5 133.0 %all-gather.2.cloned.1.call-start = ((), (), s32[]{:S(2)}) async-start(), calls=%async_computation.2 | async-start | bytes 4456448 | tf_op jit(solution)/shard_map/all_gather | solution.py:44
  9.2 8.7 %copy-start.7 = (bf16[4,128,1024]{2,1,0:T(8,128)(2,1)S(1)}, bf16[4,128,1024]{2,1,0:T(8,128)(2,1)}, u32[]{:S(2)}) copy-start(bf16[4,128,1024]{2,1,0:T(8,128)(2,1)} %param.7) | copy-start | bytes 3145732
  9.2 9.0 %copy-start.9 = (f32[6,1024]{1,0:T(8,128)S(1)}, f32[6,1024]{1,0:T(8,128)}, u32[]{:S(2)}) copy-start(f32[6,1024]{1,0:T(8,128)} %param.8) | copy-start | bytes 73732
  24.2 3.7 %copy-start.4 = (bf16[3,4,16,128,64]{3,4,2,0,1:T(8,128)(2,1)}, bf16[3,4,16,128,64]{3,4,2,0,1:T(8,128)(2,1)S(1)}, u32[]{:S(2)}) copy-start(bf16[3,4,16,128,64]{3,4,2,0,1:T(8,128)(2,1)S(1)} %convert_bitcast_fusion.1) | copy-start | bytes 9437188
  32.7 43.4 %copy-start.5 = (bf16[4,128,1024]{2,1,0:T(8,128)(2,1)}, bf16[4,128,1024]{2,1,0:T(8,128)(2,1)S(1)}, u32[]{:S(2)}) copy-start(bf16[4,128,1024]{2,1,0:T(8,128)(2,1)S(1)} %get-tuple-element.22) | copy-start | bytes 3145732
  75.8 65.4 %copy-start.10 = (s32[16,4]{0,1:T(4,128)S(1)}, s32[16,4]{0,1:T(4,128)}, u32[]{:S(2)}) copy-start(s32[16,4]{0,1:T(4,128)} %param.13) | copy-start | bytes 772
  77.3 40.3 %collective-permute-start.1 = (bf16[64,8,1024]{2,0,1:T(8,128)(2,1)}, bf16[64,8,1024]{2,0,1:T(8,128)(2,1)S(1)}, u32[]{:S(2)}, u32[]{:S(2)}) collective-permute-start(bf16[64,8,1024]{2,0,1:T(8,128)(2,1)} %all_to_all.27), channel_id=1, source_target_pairs={{224,0},{240,16},{0,32},{16,48},{32,64},{48,80},{64,96},{80,112},{... | collective-permute-start | bytes 3145736 | tf_op jit(solution)/shard_map/ppermute | solution.py:16
  78.5 61.1 %collective-permute-start = (bf16[64,8,1024]{2,0,1:T(8,128)(2,1)}, bf16[64,8,1024]{2,0,1:T(8,128)(2,1)S(1)}, u32[]{:S(2)}, u32[]{:S(2)}) collective-permute-start(bf16[64,8,1024]{2,0,1:T(8,128)(2,1)} %all_to_all.27), channel_id=1, source_target_pairs={{32,0},{48,16},{64,32},{80,48},{96,64},{112,80},{128,96},{144,112}... | collective-permute-start | bytes 3145736 | tf_op jit(solution)/shard_map/ppermute | solution.py:16
  139.5 16.4 %collective-permute-start.2 = (bf16[1024,2048]{1,0:T(8,128)(2,1)}, bf16[1024,2048]{1,0:T(8,128)(2,1)}, u32[]{:S(2)}, u32[]{:S(2)}) collective-permute-start(bf16[1024,2048]{1,0:T(8,128)(2,1)} %all-gather.2.cloned.1.call-done), channel_id=1, source_target_pairs={{0,16},{16,0},{32,48},{48,32},{64,80},{80,64},{96,112},{112,96},{1... | collective-permute-start | bytes 12582920 | tf_op jit(solution)/shard_map/ppermute | solution.py:50
  139.5 9.0 %collective-permute-start.3 = (bf16[64,8,1024]{2,0,1:T(8,128)(2,1)}, bf16[64,8,1024]{2,0,1:T(8,128)(2,1)}, u32[]{:S(2)}, u32[]{:S(2)}) collective-permute-start(bf16[64,8,1024]{2,0,1:T(8,128)(2,1)} %all_to_all.27), channel_id=1, source_target_pairs={{0,16},{16,0},{32,48},{48,32},{64,80},{80,64},{96,112},{112,96},{1... | collective-permute-start | bytes 3145736 | tf_op jit(solution)/shard_map/ppermute | solution.py:100
  141.1 8.9 %collective-permute-start.4 = (bf16[64,8,1024]{2,0,1:T(8,128)(2,1)}, bf16[64,8,1024]{2,0,1:T(8,128)(2,1)}, u32[]{:S(2)}, u32[]{:S(2)}) collective-permute-start(bf16[64,8,1024]{2,0,1:T(8,128)(2,1)} %broadcast_select_fusion), channel_id=1, source_target_pairs={{0,16},{16,0},{32,48},{48,32},{64,80},{80,64},{96,112},{112,96},{1... | collective-permute-start | bytes 3145736 | tf_op jit(solution)/shard_map/ppermute | solution.py:102
  153.5 2.4 copy-start.8
  187.2 6.5 %copy-start.3 = (bf16[64,8,1024,1]{2,0,1,3:T(8,128)(2,1)S(1)}, bf16[64,8,1024,1]{2,0,1,3:T(8,128)(2,1)}, u32[]{:S(2)}) copy-start(bf16[64,8,1024,1]{2,0,1,3:T(8,128)(2,1)} %reshape.70) | copy-start | bytes 3145732
  202.7 14.4 %copy-start.2 = (bf16[8,16,320,64]{2,3,0,1:T(8,128)(2,1)S(1)}, bf16[8,16,320,64]{2,3,0,1:T(8,128)(2,1)}, u32[]{:S(2)}) copy-start(bf16[8,16,320,64]{2,3,0,1:T(8,128)(2,1)} %get-tuple-element.11) | copy-start | bytes 15728644
  223.1 40.7 %copy-start.6 = (bf16[4,128,1024]{2,1,0:T(8,128)(2,1)S(1)}, bf16[4,128,1024]{2,1,0:T(8,128)(2,1)}, u32[]{:S(2)}) copy-start(bf16[4,128,1024]{2,1,0:T(8,128)(2,1)} %copy-done.5) | copy-start | bytes 3145732
  225.5 38.2 %all-to-all-start.1 = ((bf16[64,8,1024]{2,1,0:T(8,128)(2,1)}), bf16[64,8,1024]{2,1,0:T(8,128)(2,1)}, u32[]{:S(2)}, u32[]{:S(2)}) async-start(bf16[64,8,1024]{2,1,0:T(8,128)(2,1)} %copy.29), calls=%async_computation.1 | async-start | bytes 2097152 | tf_op jit(solution)/shard_map/all_to_all | solution.py:130
  263.7 4.9 %copy-start.1 = (bf16[1024,1024]{1,0:T(8,128)(2,1)S(1)}, bf16[1024,1024]{1,0:T(8,128)(2,1)}, u32[]{:S(2)}) copy-start(bf16[1024,1024]{1,0:T(8,128)(2,1)} %param.10) | copy-start | bytes 6291460
Sparse Core Ops, SparseCore 0:
  9.9 125.7 all-gather.1

commit v5 on v4

--- a/solution.py
+++ b/solution.py
@@ -71,10 +71,12 @@
     gathered, halves = gather_half_by_core((w_inter_qkv, w_inter_out), "tm", "grp")
 
     normed = modulate(motion, modulation, 0, 1)
-    t_w = w_temporal_qkv.reshape(feature_width, 3, head_count, HEAD)
-    t_packed = jnp.einsum(
-        "nfk,kshd->snhfd", normed, t_w, preferred_element_type=jnp.float32
+    t_packed = jnp.dot(
+        normed.reshape(own_chars * all_frames, feature_width),
+        w_temporal_qkv,
+        preferred_element_type=jnp.float32,
     ).astype(jnp.bfloat16)
+    t_packed = t_packed.reshape(own_chars, all_frames, 3, head_count, HEAD).transpose(2, 0, 3, 1, 4)
     scores = jnp.einsum(
         "nhfd,nhgd->nhfg", t_packed[0], t_packed[1], preferred_element_type=jnp.float32
     ) * scale
@@ -108,14 +110,19 @@
     inter_qkv, inter_out = swap_halves(gathered, halves, "grp")
     char_count, frame_count, unused_width = frames_own.shape
 
-    i_w = inter_qkv.reshape(feature_width, 3, head_count, HEAD)
-    queries = jnp.einsum(
-        "cfk,khd->fhcd", frames_own, i_w[:, 0], preferred_element_type=jnp.float32
+    queries = jnp.dot(
+        frames_own.reshape(char_count * frame_count, feature_width),
+        inter_qkv[:, :feature_width],
+        preferred_element_type=jnp.float32,
     ).astype(jnp.bfloat16)
+    queries = queries.reshape(char_count, frame_count, head_count, HEAD).transpose(1, 2, 0, 3)
     stacked = jnp.concatenate([frames_own] + others, axis=0)
-    pairs = jnp.einsum(
-        "mfk,kthd->tfhmd", stacked, i_w[:, 1:], preferred_element_type=jnp.float32
+    pairs = jnp.dot(
+        stacked.reshape(-1, feature_width),
+        inter_qkv[:, feature_width:],
+        preferred_element_type=jnp.float32,
     ).astype(jnp.bfloat16)
+    pairs = pairs.reshape(-1, frame_count, 2, head_count, HEAD).transpose(2, 1, 3, 0, 4)
     scores = jnp.einsum(
         "fhcd,fhmd->fhcm", queries, pairs[0], preferred_element_type=jnp.float32
     ) * scale

time: 276 us -> 334 us (1.21)
  local copies, waits for them, and re-layouts: 44.7 us -> 98.9 us
  waiting for transfers between devices: 89.3 us -> 76 us
  matrix products: 48.1 us -> 54.7 us
  blocking collectives: 41.8 us -> 45.7 us
  other arithmetic: 26.9 us -> 30.4 us
    reshape x0 -> x5, local copies, waits for them, and re-layouts: none -> 79.1 us  [the longest x2 61 us: per_device(): pairs.reshape(-1, frame_count, 2, head_count, HEAD).transpose(2, 1, 3, 0, 4)]
    ppermute x2, waiting for transfers between devices: 59.3 us -> 43.6 us  [from_group(): return lax.ppermute(block, axis, route)]
    select_n x1 -> x0, local copies, waits for them, and re-layouts: 8.62 us -> none  [swap_halves(): jnp.where(pair_index == 0, jnp.concatenate([own_part, other_part], axis=1...]
    unnamed x25 -> x22, local copies, waits for them, and re-layouts: 12.5 us -> 5.13 us
    squeeze x1 -> x0, local copies, waits for them, and re-layouts: 6.5 us -> none  [per_device(): pairs[1]]
    all_to_all x1, blocking collectives: 41.8 us -> 45.7 us  [per_device(): lax.all_to_all(normed_inter, 'tm', split_axis=1, concat_axis=0, tiled=True)]
    dot_general x2 -> x3, matrix products: 22.6 us -> 25.7 us  [the longest x1 16.8 us: per_device(): jnp.dot(stacked.reshape(-1, feature_width), inter_qkv[:, feature_width:],...]
  transfers between devices with their start and end apart: 7 -> 7, of which waited for: 5 -> 5; matrix products, arithmetic and copies ran while one was open for 14% -> 16% of each run, Pallas kernels for 0% -> 0%
where the time goes in v5:
time: 334 us; the launch traced here: 332 us
  local copies, waits for them, and re-layouts  98.9 us (30%)
  waiting for transfers between devices  76 us (23%)
  matrix products  54.7 us (16%)
  blocking collectives  45.7 us (14%)
  other arithmetic  30.4 us (9%)
  between operations  13.6 us (4%)
  starting transfers between devices  12.1 us (4%)
    reshape x2, local copies, waits for them, and re-layouts, per_device(): pairs.reshape(-1, frame_count, 2, head_count, HEAD).transpose(2, 1, 3, 0, 4)  61 us
    all_to_all x1, blocking collectives, per_device(): lax.all_to_all(normed_inter, 'tm', split_axis=1, concat_axis=0, tiled=True)  45.7 us
    ppermute x2, waiting for transfers between devices, from_group(): return lax.ppermute(block, axis, route)  43.6 us
    all_to_all x1, waiting for transfers between devices, per_device(): lax.all_to_all(mixed_heads.reshape(char_count, frame_count, feature_width...  26.1 us
    sub x2, other arithmetic, softmax_rows(): weights = jnp.exp(scores - row_top)  17.8 us
    dot_general x1, matrix products, per_device(): jnp.dot(stacked.reshape(-1, feature_width), inter_qkv[:, feature_width:],...  16.8 us
    reshape x2, local copies, waits for them, and re-layouts, per_device(): t_packed.reshape(own_chars, all_frames, 3, head_count, HEAD)  16.8 us
    dot_general x1, matrix products, per_device(): jnp.einsum('fhcd,fhmd->fhcm', queries, pairs[0], preferred_element_type=j...  10.3 us
  transfers between devices with their start and end apart: 7, of which 5 were waited for; matrix products, arithmetic and copies ran while one was open for 16% of the time, Pallas kernels for 0%

profile of v5, /device:TPU:8, one launch (start us, length us, event | category | flops | bytes accessed | tf_op | source)
XLA Modules:
  0.0 331.5 jit_solution(16139807055382789698)
XLA Ops:
  6.5 0.0 copy-start
  6.5 0.0 all-gather.2.cloned.1.call-start
  6.5 1.0 constant_dynamic-slice_fusion
  7.5 0.9 constant_dynamic-slice_fusion.1
  8.5 0.7 pad_maximum_fusion
  9.2 0.0 all-gather.2.cloned.1.call-update
  9.2 1.5 fusion.13
  10.7 1.0 fusion.52
  11.8 1.6 fusion.16
  13.4 7.6 %convolution_convert_fusion.1 = bf16[512,3072]{1,0:T(8,128)(2,1)} fusion(bf16[512,1024]{1,0:T(8,128)(2,1)S(1)} %bitcast.82, bf16[1024,3072]{1,0:T(8,128)(2,1)} %param.9), kind=kOutput, calls=%fused_computation.16 | convolution fusion | flops 3222798336 | bytes 10485760 | tf_op jit(solution)/shard_map/dot_general | solution.py:74
  21.0 8.6 %reshape.82 = bf16[4,128,3,16,64]{4,3,2,1,0:T(8,128)(2,1)} reshape(bf16[512,3072]{1,0:T(8,128)(2,1)} %convolution_convert_fusion.1) | data formatting | bytes 6291456 | tf_op jit(solution)/shard_map/reshape | solution.py:79
  29.6 8.2 %copy.28 = bf16[4,128,3,16,64]{1,4,3,0,2:T(8,128)(2,1)} copy(bf16[4,128,3,16,64]{4,3,2,1,0:T(8,128)(2,1)} %reshape.82) | data formatting | bytes 6291456 | tf_op jit(solution)/shard_map/reshape | solution.py:79
  37.8 2.3 fusion.45
  40.1 0.0 copy-start.3
  40.1 3.0 fusion.53
  43.1 0.0 copy-done
  43.1 0.0 copy-done.3
  43.1 5.5 %fusion.18 = (f32[4,128]{1,0:T(4,128)S(1)}, bf16[4,128,1024]{2,1,0:T(8,128)(2,1)}) fusion(bf16[16,64,1024,1]{2,1,0,3:T(8,128)(2,1)S(1)} %bitcast.68, f32[4,16,128,128]{2,3,1,0:T(8,128)} %get-tuple-element.18, f32[4,16,128]{2,1,0:T(8,128)S(1)} %get-tuple-element.17, bf16[3,4,16,128,64]{3,4,2,1,0:T(8,128)(2,1)} %bitcast.74, f32[1024]{0:T(1024)S(1)} %bitcast.88, ...), kind=kOutput, calls=%fused_computation.33 | convolution fusion | flops 1214250496 | bytes 9476096 | tf_op jit(solution)/shard_map/nhfd,hdo->nfo/dot_general | solution.py:87
  48.6 1.6 fusion.21
  50.2 0.8 copy.30
  51.0 45.7 %all_to_all.33 = bf16[4,128,1024]{2,0,1:T(4,128)(2,1)S(1)} all-to-all(bf16[4,128,1024]{2,0,1:T(4,128)(2,1)S(1)} %copy.30), channel_id=1, replica_groups=mesh['grp'=16,'tm'=16] {'tm'}, dimensions={1} | all-to-all | bytes 2097152 | tf_op jit(solution)/shard_map/all_to_all | solution.py:96
  96.7 0.3 copy.51
  97.0 0.1 copy.32
  97.1 0.7 collective-permute-start.2
  97.8 2.3 collective-permute-start.1
  100.1 24.0 %collective-permute-done.2 = bf16[64,8,1024]{2,1,0:T(8,128)(2,1)S(1)} collective-permute-done((bf16[64,8,1024]{2,1,0:T(8,128)(2,1)S(1)}, bf16[64,8,1024]{2,1,0:T(8,128)(2,1)S(1)}, u32[]{:S(2)}, u32[]{:S(2)}) %collective-permute-start.2) | collective-permute-done | bytes 1048608 | tf_op jit(solution)/shard_map/ppermute | solution.py:16
  124.1 19.6 %collective-permute-done.1 = bf16[64,8,1024]{2,1,0:T(8,128)(2,1)S(1)} collective-permute-done((bf16[64,8,1024]{2,1,0:T(8,128)(2,1)S(1)}, bf16[64,8,1024]{2,1,0:T(8,128)(2,1)S(1)}, u32[]{:S(2)}, u32[]{:S(2)}) %collective-permute-start.1) | collective-permute-done | bytes 1048608 | tf_op jit(solution)/shard_map/ppermute | solution.py:16
  143.7 0.0 collective-permute-start.4
  143.8 0.5 collective-permute-start
  144.3 1.1 broadcast_select_fusion
  145.3 0.0 collective-permute-start.3
  145.3 0.2 dynamic-slice_reduce_fusion
  145.5 0.1 add_compare_fusion
  145.6 0.1 broadcast_in_dim.8
  145.7 0.1 gt.12
  145.8 0.1 constant_dynamic-update-slice_fusion.2
  145.9 2.1 slice.60
  147.9 4.8 %collective-permute-done = bf16[64,8,1024]{2,1,0:T(8,128)(2,1)} collective-permute-done((bf16[64,8,1024]{2,1,0:T(8,128)(2,1)S(1)}, bf16[64,8,1024]{2,1,0:T(8,128)(2,1)}, u32[]{:S(2)}, u32[]{:S(2)}) %collective-permute-start) | collective-permute-done | bytes 1048608 | tf_op jit(solution)/shard_map/ppermute | solution.py:102
  152.7 1.5 collective-permute-done.3
  154.2 1.6 select_dynamic-update-slice_fusion.1
  155.9 0.1 constant_dynamic-update-slice_fusion.1
  156.0 1.6 select_dynamic-update-slice_fusion
  157.6 0.1 constant_dynamic-update-slice_fusion
  157.7 2.4 copy-done.5
  160.0 0.0 collective-permute-done.4
  160.0 2.1 slice.71
  162.1 1.8 maximum_select_fusion
  163.9 2.6 copy-done.2
  166.5 1.3 fusion.40
  167.8 1.3 reshape.77
  169.1 16.8 %convolution_convert_fusion = bf16[2560,2048]{1,0:T(8,128)(2,1)} fusion(bf16[320,8,1024]{2,1,0:T(8,128)(2,1)} %copy-done.5, bf16[1024,3072]{1,0:T(8,128)(2,1)} %copy-done.2), kind=kOutput, calls=%fused_computation.5 | convolution fusion | flops 10742661120 | bytes 19922944 | tf_op jit(solution)/shard_map/dot_general | solution.py:120
  185.9 30.4 %reshape.75 = bf16[320,8,2,16,64]{4,3,2,1,0:T(8,128)(2,1)} reshape(bf16[2560,2048]{1,0:T(8,128)(2,1)} %convolution_convert_fusion) | data formatting | bytes 20971520 | tf_op jit(solution)/shard_map/reshape | solution.py:125
  216.3 30.6 %copy.33 = bf16[320,8,2,16,64]{0,4,3,1,2:T(8,128)(2,1)} copy(bf16[320,8,2,16,64]{4,3,2,1,0:T(8,128)(2,1)} %reshape.75) | data formatting | bytes 20971520 | tf_op jit(solution)/shard_map/reshape | solution.py:125
  247.0 10.3 %fusion.3 = f32[8,16,64,320]{3,2,1,0:T(8,128)} fusion(bf16[2,8,16,320,64]{3,4,2,1,0:T(8,128)(2,1)} %bitcast.69, bf16[64,8,16,64]{3,2,1,0:T(8,128)(2,1)S(1)} %reshape.77), kind=kOutput, calls=%fused_computation.8 | convolution fusion | flops 335544320 | bytes 17825792 | tf_op jit(solution)/shard_map/fhcd,fhmd->fhcm/dot_general | solution.py:126
  257.3 14.8 %fusion.54 = (f32[8,16,64]{2,1,0:T(8,128)S(1)}, f32[8,16,64,320]{3,2,1,0:T(8,128)}) fusion(f32[8,16,64,320]{3,2,1,0:T(8,128)} %fusion.3, pred[320]{0:T(512)(128)(4,1)S(1)} %gt.12), kind=kOutput, calls=%fused_computation.85 | output fusion | flops 15728959 | bytes 21004608 | tf_op jit(solution)/shard_map/sub | solution.py:30
  272.1 0.0 slice-done.2
  272.1 6.0 %fusion.38 = bf16[8,16,64,64]{3,2,1,0:T(8,128)(2,1)S(1)} fusion(f32[8,16,64,320]{3,2,1,0:T(8,128)} %get-tuple-element.22, f32[8,16,64]{2,1,0:T(8,128)S(1)} %get-tuple-element.21, bf16[2,8,16,320,64]{3,4,2,1,0:T(8,128)(2,1)S(1)} %bitcast.72), kind=kOutput, calls=%fused_computation.54 | convolution fusion | flops 341311488 | bytes 17891328 | tf_op jit(solution)/shard_map/fhcm,fhmd->cfhd/dot_general | solution.py:134
  278.1 0.0 copy-start.4
  278.1 2.4 copy.36
  280.5 8.6 %all-to-all-start.1 = ((bf16[64,8,1024]{2,1,0:T(8,128)(2,1)}), bf16[64,8,1024]{2,1,0:T(8,128)(2,1)}, u32[]{:S(2)}, u32[]{:S(2)}) async-start(bf16[64,8,1024]{2,1,0:T(8,128)(2,1)} %copy.36), calls=%async_computation.1 | async-start | bytes 2097152 | tf_op jit(solution)/shard_map/all_to_all | solution.py:137
  289.1 2.3 slice.66
  291.4 2.3 slice.76
  293.7 26.1 %all-to-all-done.1 = bf16[64,8,1024]{2,1,0:T(8,128)(2,1)} async-done(((bf16[64,8,1024]{2,1,0:T(8,128)(2,1)}), bf16[64,8,1024]{2,1,0:T(8,128)(2,1)}, u32[]{:S(2)}, u32[]{:S(2)}) %all-to-all-start.1) | async-done | bytes 1048608 | tf_op jit(solution)/shard_map/all_to_all | solution.py:137
  319.7 4.9 %fusion.22 = bf16[4,128,1024]{2,1,0:T(8,128)(2,1)} fusion(bf16[4,128,1024]{2,1,0:T(8,128)(2,1)S(1)} %copy-done.4, bf16[1024,512]{1,0:T(8,128)(2,1)} %slice.76, bf16[1024,512]{1,0:T(8,128)(2,1)} %slice.66, pred[]{:T(512)S(6)} %eq.6, bf16[4,16,8,1024]{3,2,0,1:T(8,128)(2,1)} %bitcast.28, f32[1024]{0:T(1024)S(1)} %bitcast.87), kind=kOutput, calls=%fused_computation.37 | convolution fusion | flops 1085276160 | bytes 5246977 | tf_op jit(solution)/shard_map/dot_general | solution.py:144
  (16 shorter events, 0.0 us)
Async XLA Ops:
  6.5 36.6 %copy-start = (bf16[1024,1024]{1,0:T(8,128)(2,1)S(1)}, bf16[1024,1024]{1,0:T(8,128)(2,1)}, u32[]{:S(2)}) copy-start(bf16[1024,1024]{1,0:T(8,128)(2,1)} %param.10) | copy-start | bytes 6291460
  6.5 137.2 %all-gather.2.cloned.1.call-start = ((), (), s32[]{:S(2)}) async-start(), calls=%async_computation.2 | async-start | bytes 4456448 | tf_op jit(solution)/shard_map/all_gather | solution.py:44
  40.1 3.0 copy-start.3
  96.7 48.6 %copy-start.6 = (s32[16,4]{0,1:T(4,128)S(1)}, s32[16,4]{0,1:T(4,128)}, u32[]{:S(2)}) copy-start(s32[16,4]{0,1:T(4,128)} %param.13) | copy-start | bytes 772
  97.1 27.0 %collective-permute-start.2 = (bf16[64,8,1024]{2,1,0:T(8,128)(2,1)S(1)}, bf16[64,8,1024]{2,1,0:T(8,128)(2,1)S(1)}, u32[]{:S(2)}, u32[]{:S(2)}) collective-permute-start(bf16[64,8,1024]{2,1,0:T(8,128)(2,1)S(1)} %bitcast.75), channel_id=1, source_target_pairs={{224,0},{240,16},{0,32},{16,48},{32,64},{48,80},{64,96},{80,112},{... | collective-permute-start | bytes 3145736 | tf_op jit(solution)/shard_map/ppermute | solution.py:16
  97.8 45.9 %collective-permute-start.1 = (bf16[64,8,1024]{2,1,0:T(8,128)(2,1)S(1)}, bf16[64,8,1024]{2,1,0:T(8,128)(2,1)S(1)}, u32[]{:S(2)}, u32[]{:S(2)}) collective-permute-start(bf16[64,8,1024]{2,1,0:T(8,128)(2,1)S(1)} %bitcast.76), channel_id=1, source_target_pairs={{32,0},{48,16},{64,32},{80,48},{96,64},{112,80},{128,96},{144,112}... | collective-permute-start | bytes 3145736 | tf_op jit(solution)/shard_map/ppermute | solution.py:16
  143.7 16.3 %collective-permute-start.4 = (bf16[1024,2048]{1,0:T(8,128)(2,1)}, bf16[1024,2048]{1,0:T(8,128)(2,1)}, u32[]{:S(2)}, u32[]{:S(2)}) collective-permute-start(bf16[1024,2048]{1,0:T(8,128)(2,1)} %all-gather.2.cloned.1.call-done), channel_id=1, source_target_pairs={{0,16},{16,0},{32,48},{48,32},{64,80},{80,64},{96,112},{112,96},{1... | collective-permute-start | bytes 12582920 | tf_op jit(solution)/shard_map/ppermute | solution.py:50
  143.8 9.0 %collective-permute-start = (bf16[64,8,1024]{2,1,0:T(8,128)(2,1)S(1)}, bf16[64,8,1024]{2,1,0:T(8,128)(2,1)}, u32[]{:S(2)}, u32[]{:S(2)}) collective-permute-start(bf16[64,8,1024]{2,1,0:T(8,128)(2,1)S(1)} %bitcast.77), channel_id=1, source_target_pairs={{0,16},{16,0},{32,48},{48,32},{64,80},{80,64},{96,112},{112,96},{1... | collective-permute-start | bytes 3145736 | tf_op jit(solution)/shard_map/ppermute | solution.py:102
  145.3 8.9 %collective-permute-start.3 = (bf16[64,8,1024]{2,1,0:T(8,128)(2,1)}, bf16[64,8,1024]{2,1,0:T(8,128)(2,1)}, u32[]{:S(2)}, u32[]{:S(2)}) collective-permute-start(bf16[64,8,1024]{2,1,0:T(8,128)(2,1)} %broadcast_select_fusion), channel_id=1, source_target_pairs={{0,16},{16,0},{32,48},{48,32},{64,80},{80,64},{96,112},{112,96},{1... | collective-permute-start | bytes 3145736 | tf_op jit(solution)/shard_map/ppermute | solution.py:104
  157.7 2.4 copy-start.5
  163.9 2.6 copy-start.2
  247.0 25.1 %slice-start = ((s8[12582912]{0:T(1024)(128)(4,1)}), s8[4194304]{0:T(1024)(128)(4,1)S(1)}, s32[]{:S(2)}) async-start(s8[12582912]{0:T(1024)(128)(4,1)} %bitcast.70), calls=%async_computation.3 | async-start | bytes 8388608
  247.0 25.1 %slice-start.1 = ((s8[12582912]{0:T(1024)(128)(4,1)}), s8[4194304]{0:T(1024)(128)(4,1)S(1)}, s32[]{:S(2)}) async-start(s8[12582912]{0:T(1024)(128)(4,1)} %bitcast.70), calls=%async_computation.4 | async-start | bytes 8388608
  257.3 14.8 %slice-start.2 = ((s8[12582912]{0:T(1024)(128)(4,1)}), s8[4194304]{0:T(1024)(128)(4,1)S(1)}, s32[]{:S(2)}) async-start(s8[12582912]{0:T(1024)(128)(4,1)} %bitcast.70), calls=%async_computation.5 | async-start | bytes 8388608
  278.1 41.6 %copy-start.4 = (bf16[4,128,1024]{2,1,0:T(8,128)(2,1)S(1)}, bf16[4,128,1024]{2,1,0:T(8,128)(2,1)}, u32[]{:S(2)}) copy-start(bf16[4,128,1024]{2,1,0:T(8,128)(2,1)} %get-tuple-element.20) | copy-start | bytes 3145732
  280.5 39.2 %all-to-all-start.1 = ((bf16[64,8,1024]{2,1,0:T(8,128)(2,1)}), bf16[64,8,1024]{2,1,0:T(8,128)(2,1)}, u32[]{:S(2)}, u32[]{:S(2)}) async-start(bf16[64,8,1024]{2,1,0:T(8,128)(2,1)} %copy.36), calls=%async_computation.1 | async-start | bytes 2097152 | tf_op jit(solution)/shard_map/all_to_all | solution.py:137
  319.7 4.9 %copy-start.1 = (bf16[1024,1024]{1,0:T(8,128)(2,1)S(1)}, bf16[1024,1024]{1,0:T(8,128)(2,1)}, u32[]{:S(2)}) copy-start(bf16[1024,1024]{1,0:T(8,128)(2,1)} %param.10) | copy-start | bytes 6291460
Sparse Core Ops, SparseCore 0:
  9.9 117.5 all-gather.1

commit v6 on v4

--- a/solution.py
+++ b/solution.py
@@ -36,12 +36,12 @@
     halves = [shard.shape[1] // 2 for shard in shards]
     mine = jnp.concatenate(
         [
-            lax.dynamic_slice_in_dim(shard, pair_index * half, half, axis=1)
+            lax.dynamic_slice_in_dim(shard, pair_index * half, half, axis=1).T
             for shard, half in zip(shards, halves)
         ],
-        axis=1,
+        axis=0,
     )
-    return lax.all_gather(mine, axis_small, axis=0, tiled=True), halves
+    return lax.all_gather(mine, axis_small, axis=1, tiled=True), halves
 
 
 def swap_halves(gathered, halves, axis_pair):
@@ -51,14 +51,14 @@
     results = []
     start = 0
     for half in halves:
-        own_part = gathered[:, start:start + half]
-        other_part = other[:, start:start + half]
+        own_part = gathered[start:start + half]
+        other_part = other[start:start + half]
         start += half
         results.append(
             jnp.where(
                 pair_index == 0,
-                jnp.concatenate([own_part, other_part], axis=1),
-                jnp.concatenate([other_part, own_part], axis=1),
+                jnp.concatenate([own_part, other_part], axis=0),
+                jnp.concatenate([other_part, own_part], axis=0),
             )
         )
     return results
@@ -108,13 +108,13 @@
     inter_qkv, inter_out = swap_halves(gathered, halves, "grp")
     char_count, frame_count, unused_width = frames_own.shape
 
-    i_w = inter_qkv.reshape(feature_width, 3, head_count, HEAD)
+    i_w = inter_qkv.reshape(3, head_count, HEAD, feature_width)
     queries = jnp.einsum(
-        "cfk,khd->fhcd", frames_own, i_w[:, 0], preferred_element_type=jnp.float32
+        "cfk,hdk->fhcd", frames_own, i_w[0], preferred_element_type=jnp.float32
     ).astype(jnp.bfloat16)
     stacked = jnp.concatenate([frames_own] + others, axis=0)
     pairs = jnp.einsum(
-        "mfk,kthd->tfhmd", stacked, i_w[:, 1:], preferred_element_type=jnp.float32
+        "mfk,thdk->tfhmd", stacked, i_w[1:], preferred_element_type=jnp.float32
     ).astype(jnp.bfloat16)
     scores = jnp.einsum(
         "fhcd,fhmd->fhcm", queries, pairs[0], preferred_element_type=jnp.float32
@@ -134,7 +134,8 @@
         concat_axis=1,
         tiled=True,
     )
-    result = jnp.dot(
+    result = jnp.einsum(
+        "tk,ok->to",
         mixed_chars.reshape(own_chars * all_frames, feature_width),
         inter_out,
         preferred_element_type=jnp.float32,

time: 276 us -> 272 us (0.986)
    select_n x1 -> x0, local copies, waits for them, and re-layouts: 8.62 us -> none  [swap_halves(): jnp.where(pair_index == 0, jnp.concatenate([own_part, other_part], axis=1...]
    optimization_barrier x0 -> x1, local copies, waits for them, and re-layouts: none -> 6.41 us  [per_device(): lax.optimization_barrier((gathered, ahead_two, behind_two))]
    slice x4 -> x7, local copies, waits for them, and re-layouts: 8.77 us -> 9.45 us  [the longest x2 4.52 us: swap_halves(): own_part = gathered[start:start + half]]
where the time goes in v6:
time: 272 us; the launch traced here: 271 us
  waiting for transfers between devices  88.4 us (32%)
  matrix products  45.5 us (17%)
  local copies, waits for them, and re-layouts  42.8 us (16%)
  blocking collectives  42.3 us (16%)
  other arithmetic  26.7 us (10%)
  between operations  13.6 us (5%)
  starting transfers between devices  11.3 us (4%)
    ppermute x2, waiting for transfers between devices, from_group(): return lax.ppermute(block, axis, route)  58.6 us
    all_to_all x1, blocking collectives, per_device(): lax.all_to_all(normed_inter, 'tm', split_axis=1, concat_axis=0, tiled=True)  42.3 us
    all_to_all x1, waiting for transfers between devices, per_device(): lax.all_to_all(mixed_heads.reshape(char_count, frame_count, feature_width...  26 us
    sub x2, other arithmetic, softmax_rows(): weights = jnp.exp(scores - row_top)  17.3 us
    dot_general x1, matrix products, per_device(): jnp.einsum('mfk,thdk->tfhmd', stacked, i_w[1:], preferred_element_type=jn...  14.4 us
    unnamed x25, local copies, waits for them, and re-layouts  12.3 us
    dot_general x1, matrix products, per_device(): jnp.einsum('fhcd,fhmd->fhcm', queries, pairs[0], preferred_element_type=j...  8.77 us
    all_to_all x1, starting transfers between devices, per_device(): lax.all_to_all(mixed_heads.reshape(char_count, frame_count, feature_width...  7.9 us
  transfers between devices with their start and end apart: 7, of which 5 were waited for; matrix products, arithmetic and copies ran while one was open for 14% of the time, Pallas kernels for 0%

profile of v6, /device:TPU:8, one launch (start us, length us, event | category | flops | bytes accessed | tf_op | source)
XLA Modules:
  0.0 270.7 jit_solution(3672145151106790419)
XLA Ops:
  6.5 0.0 copy-start
  6.5 0.0 all-gather.2.cloned.1.call-start
  6.5 1.0 dynamic-slice_bitcast_fusion.1
  7.5 0.9 dynamic-slice_bitcast_fusion
  8.5 0.7 pad_maximum_fusion
  9.2 0.0 all-gather.2.cloned.1.call-update
  9.2 0.0 copy-start.8
  9.2 0.0 copy-start.9
  9.2 8.7 %copy.23 = bf16[1024,3072]{0,1:T(8,128)(2,1)} copy(bf16[1024,3072]{1,0:T(8,128)(2,1)} %param.9) | data formatting | bytes 12582912 | tf_op args[2]
  18.0 0.0 copy-done.8
  18.0 0.3 fusion.14
  18.2 0.0 copy-done.9
  18.3 5.9 %convert_bitcast_fusion.1 = bf16[3,4,16,128,64]{3,4,2,0,1:T(8,128)(2,1)S(1)} fusion(bf16[1024,3,16,64,1]{0,3,2,1,4:T(8,128)(2,1)} %bitcast.96, bf16[4,128,1024]{2,1,0:T(8,128)(2,1)S(1)} %copy-done.8, f32[1024]{0:T(1024)S(1)} %bitcast.104, f32[1024]{0:T(1024)S(1)} %bitcast.105, f32[4,128]{1,0:T(4,128)S(1)} %add_rsqrt_fusion.1), kind=kOutput, calls=%fused_computation.25 | convolution fusion | flops 3225419776 | bytes 10496000 | tf_op jit(solution)/shard_map/nfk,kshd->snhfd/dot_general | solution.py:75
  24.2 0.0 copy-start.5
  24.2 0.8 fusion.47
  25.0 2.9 %fusion.60 = (f32[4,16,128]{2,1,0:T(8,128)S(1)}, f32[4,16,128,128]{2,3,1,0:T(8,128)}) fusion(f32[4,16,128,128]{2,3,1,0:T(8,128)S(1)} %fusion.47), kind=kOutput, calls=%fused_computation.88 | output fusion | flops 4194431 | bytes 8421376 | tf_op jit(solution)/shard_map/sub | solution.py:30
  27.9 0.0 copy-done.5
  27.9 4.8 %fusion.19 = (f32[4,128]{1,0:T(4,128)S(1)}, bf16[4,128,1024]{2,1,0:T(8,128)(2,1)S(1)}) fusion(bf16[16,64,1024,1]{2,1,0,3:T(8,128)(2,1)S(1)} %bitcast.92, f32[4,16,128,128]{2,3,1,0:T(8,128)} %get-tuple-element.20, f32[4,16,128]{2,1,0:T(8,128)S(1)} %get-tuple-element.19, bf16[3,4,16,128,64]{3,4,2,0,1:T(8,128)(2,1)} %copy-done.5, f32[1024]{0:T(1024)S(1)} %bitcast.103, ...), kind=kOutput, calls=%fused_computation.34 | convolution fusion | flops 1214250496 | bytes 9476096 | tf_op jit(solution)/shard_map/nhfd,hdo->nfo/dot_general | solution.py:85
  32.7 0.0 copy-start.6
  32.7 0.4 fusion.22
  33.1 0.8 copy.25
  33.9 42.3 %all_to_all.33 = bf16[4,128,1024]{2,0,1:T(4,128)(2,1)S(1)} all-to-all(bf16[4,128,1024]{2,0,1:T(4,128)(2,1)S(1)} %copy.25), channel_id=1, replica_groups=mesh['grp'=16,'tm'=16] {'tm'}, dimensions={1} | all-to-all | bytes 2097152 | tf_op jit(solution)/shard_map/all_to_all | solution.py:94
  76.3 0.4 copy.53
  76.7 1.1 all_to_all.27
  77.8 1.3 collective-permute-start.1
  79.1 1.6 collective-permute-start
  80.7 36.9 %collective-permute-done.1 = bf16[64,8,1024]{2,0,1:T(8,128)(2,1)S(1)} collective-permute-done((bf16[64,8,1024]{2,0,1:T(8,128)(2,1)}, bf16[64,8,1024]{2,0,1:T(8,128)(2,1)S(1)}, u32[]{:S(2)}, u32[]{:S(2)}) %collective-permute-start.1) | collective-permute-done | bytes 1048608 | tf_op jit(solution)/shard_map/ppermute | solution.py:16
  117.6 21.7 %collective-permute-done = bf16[64,8,1024]{2,0,1:T(8,128)(2,1)S(1)} collective-permute-done((bf16[64,8,1024]{2,0,1:T(8,128)(2,1)}, bf16[64,8,1024]{2,0,1:T(8,128)(2,1)S(1)}, u32[]{:S(2)}, u32[]{:S(2)}) %collective-permute-start) | collective-permute-done | bytes 1048608 | tf_op jit(solution)/shard_map/ppermute | solution.py:16
  139.3 6.4 %copy.27 = bf16[2048,1024]{1,0:T(8,128)(2,1)} copy(bf16[2048,1024]{0,1:T(8,128)(2,1)} %all-gather.2.cloned.1.call-done) | data formatting | bytes 8388608 | tf_op jit(solution)/shard_map/optimization_barrier | solution.py:101
  145.7 0.0 collective-permute-start.2
  145.7 0.5 collective-permute-start.3
  146.2 1.1 broadcast_select_fusion
  147.3 0.0 collective-permute-start.4
  147.3 0.2 dynamic-slice_reduce_fusion
  147.5 0.1 add_compare_fusion
  147.6 0.1 broadcast_in_dim.8
  147.7 0.1 gt.12
  147.7 1.2 reshape.69
  148.9 1.3 constant_dynamic-update-slice_fusion.2
  150.2 2.2 slice.76
  152.4 2.3 collective-permute-done.3
  154.7 1.5 collective-permute-done.4
  156.2 1.6 select_dynamic-update-slice_fusion.1
  157.8 0.1 constant_dynamic-update-slice_fusion.1
  157.9 1.6 select_dynamic-update-slice_fusion
  159.6 0.1 constant_dynamic-update-slice_fusion
  159.6 0.0 collective-permute-done.2
  159.7 2.2 slice.77
  161.9 3.6 %maximum_select_fusion = bf16[3072,1024]{1,0:T(8,128)(2,1)S(1)} fusion(bf16[1536,1024]{1,0:T(8,128)(2,1)S(1)} %slice.77, bf16[1536,1024]{1,0:T(8,128)(2,1)S(1)} %slice.76, pred[]{:T(512)S(6)} %eq.6), kind=kLoop, calls=%fused_computation.9 | loop fusion | flops 28311552 | bytes 12582913 | tf_op jit(solution)/shard_map/jit(_where)/select_n | solution.py:58
  165.4 0.5 slice.78
  165.9 2.1 copy-done.2
  168.0 14.4 %convert_bitcast_fusion = bf16[2,8,16,320,64]{3,4,1,2,0:T(8,128)(2,1)S(1)} fusion(bf16[2,16,64,1024,1]{3,2,4,1,0:T(8,128)(2,1)S(1)} %bitcast.97, bf16[320,8,1024]{2,0,1:T(8,128)(2,1)S(1)} %constant_dynamic-update-slice_fusion), kind=kOutput, calls=%fused_computation.5 | convolution fusion | flops 10742661120 | bytes 19922944 | tf_op jit(solution)/shard_map/mfk,thdk->tfhmd/dot_general | solution.py:116
  182.4 0.0 slice-start
  182.5 6.4 %slice_bitcast_fusion.1 = (bf16[8,16,320,64]{2,3,0,1:T(8,128)(2,1)}, bf16[8,16,320,64]{2,3,0,1:T(8,128)(2,1)}) fusion(bf16[2,8,16,320,64]{3,4,1,2,0:T(8,128)(2,1)S(1)} %convert_bitcast_fusion), kind=kLoop, calls=%fused_computation.8 | loop fusion | bytes 20971520 | tf_op jit(solution)/shard_map/squeeze | solution.py:128
  188.9 8.8 %fusion.5 = f32[8,16,64,320]{3,2,1,0:T(8,128)} fusion(bf16[8,16,320,64]{2,3,0,1:T(8,128)(2,1)} %get-tuple-element.12, bf16[16,64,1024,1]{2,1,0,3:T(8,128)(2,1)S(1)} %bitcast.93, bf16[64,8,1024,1]{2,0,1,3:T(8,128)(2,1)S(1)} %copy-done.4), kind=kOutput, calls=%fused_computation.12 | convolution fusion | flops 1409810432 | bytes 18874368 | tf_op jit(solution)/shard_map/fhcd,fhmd->fhcm/dot_general | solution.py:119
  197.6 14.4 %fusion.61 = (f32[8,16,64]{2,1,0:T(8,128)S(1)}, f32[8,16,64,320]{3,2,1,0:T(8,128)}) fusion(f32[8,16,64,320]{3,2,1,0:T(8,128)} %fusion.5, pred[320]{0:T(512)(128)(4,1)S(1)} %gt.12), kind=kOutput, calls=%fused_computation.89 | output fusion | flops 15728959 | bytes 21004608 | tf_op jit(solution)/shard_map/sub | solution.py:30
  212.0 6.0 %fusion.39 = bf16[8,16,64,64]{3,2,1,0:T(8,128)(2,1)S(1)} fusion(f32[8,16,64,320]{3,2,1,0:T(8,128)} %get-tuple-element.24, f32[8,16,64]{2,1,0:T(8,128)S(1)} %get-tuple-element.23, bf16[8,16,320,64]{2,3,0,1:T(8,128)(2,1)S(1)} %copy-done.3), kind=kOutput, calls=%fused_computation.54 | convolution fusion | flops 341311488 | bytes 16809984 | tf_op jit(solution)/shard_map/fhcm,fhmd->cfhd/dot_general | solution.py:127
  218.0 0.0 copy-start.7
  218.0 2.4 copy.32
  220.4 7.9 %all-to-all-start.1 = ((bf16[64,8,1024]{2,1,0:T(8,128)(2,1)}), bf16[64,8,1024]{2,1,0:T(8,128)(2,1)}, u32[]{:S(2)}, u32[]{:S(2)}) async-start(bf16[64,8,1024]{2,1,0:T(8,128)(2,1)} %copy.32), calls=%async_computation.1 | async-start | bytes 2097152 | tf_op jit(solution)/shard_map/all_to_all | solution.py:130
  228.4 2.3 slice.82
  230.7 2.3 slice.83
  233.0 26.0 %all-to-all-done.1 = bf16[64,8,1024]{2,1,0:T(8,128)(2,1)} async-done(((bf16[64,8,1024]{2,1,0:T(8,128)(2,1)}), bf16[64,8,1024]{2,1,0:T(8,128)(2,1)}, u32[]{:S(2)}, u32[]{:S(2)}) %all-to-all-start.1) | async-done | bytes 1048608 | tf_op jit(solution)/shard_map/all_to_all | solution.py:130
  259.0 4.9 %fusion.23 = bf16[4,128,1024]{2,1,0:T(8,128)(2,1)} fusion(bf16[4,128,1024]{2,1,0:T(8,128)(2,1)S(1)} %copy-done.7, bf16[512,1024]{1,0:T(8,128)(2,1)} %slice.83, bf16[512,1024]{1,0:T(8,128)(2,1)} %slice.82, pred[]{:T(512)S(6)} %eq.6, bf16[4,16,8,1024]{3,2,0,1:T(8,128)(2,1)} %bitcast.37, f32[1024]{0:T(1024)S(1)} %bitcast.102), kind=kOutput, calls=%fused_computation.38 | convolution fusion | flops 1085276160 | bytes 5246977 | tf_op jit(solution)/shard_map/tk,ok->to/dot_general | solution.py:137
  (17 shorter events, 0.1 us)
Async XLA Ops:
  6.5 21.4 %copy-start = (bf16[1024,1024]{1,0:T(8,128)(2,1)S(1)}, bf16[1024,1024]{1,0:T(8,128)(2,1)}, u32[]{:S(2)}) copy-start(bf16[1024,1024]{1,0:T(8,128)(2,1)} %param.10) | copy-start | bytes 6291460
  6.5 132.8 %all-gather.2.cloned.1.call-start = ((), (), s32[]{:S(2)}) async-start(), calls=%async_computation.2 | async-start | bytes 4456448 | tf_op jit(solution)/shard_map/all_gather | solution.py:44
  9.2 8.7 %copy-start.8 = (bf16[4,128,1024]{2,1,0:T(8,128)(2,1)S(1)}, bf16[4,128,1024]{2,1,0:T(8,128)(2,1)}, u32[]{:S(2)}) copy-start(bf16[4,128,1024]{2,1,0:T(8,128)(2,1)} %param.7) | copy-start | bytes 3145732
  9.2 9.0 %copy-start.9 = (f32[6,1024]{1,0:T(8,128)S(1)}, f32[6,1024]{1,0:T(8,128)}, u32[]{:S(2)}) copy-start(f32[6,1024]{1,0:T(8,128)} %param.8) | copy-start | bytes 73732
  24.2 3.7 %copy-start.5 = (bf16[3,4,16,128,64]{3,4,2,0,1:T(8,128)(2,1)}, bf16[3,4,16,128,64]{3,4,2,0,1:T(8,128)(2,1)S(1)}, u32[]{:S(2)}) copy-start(bf16[3,4,16,128,64]{3,4,2,0,1:T(8,128)(2,1)S(1)} %convert_bitcast_fusion.1) | copy-start | bytes 9437188
  32.7 43.9 %copy-start.6 = (bf16[4,128,1024]{2,1,0:T(8,128)(2,1)}, bf16[4,128,1024]{2,1,0:T(8,128)(2,1)S(1)}, u32[]{:S(2)}) copy-start(bf16[4,128,1024]{2,1,0:T(8,128)(2,1)S(1)} %get-tuple-element.22) | copy-start | bytes 3145732
  77.8 69.5 %copy-start.10 = (s32[16,4]{0,1:T(4,128)S(1)}, s32[16,4]{0,1:T(4,128)}, u32[]{:S(2)}) copy-start(s32[16,4]{0,1:T(4,128)} %param.13) | copy-start | bytes 772
  77.8 39.8 %collective-permute-start.1 = (bf16[64,8,1024]{2,0,1:T(8,128)(2,1)}, bf16[64,8,1024]{2,0,1:T(8,128)(2,1)S(1)}, u32[]{:S(2)}, u32[]{:S(2)}) collective-permute-start(bf16[64,8,1024]{2,0,1:T(8,128)(2,1)} %all_to_all.27), channel_id=1, source_target_pairs={{224,0},{240,16},{0,32},{16,48},{32,64},{48,80},{64,96},{80,112},{... | collective-permute-start | bytes 3145736 | tf_op jit(solution)/shard_map/ppermute | solution.py:16
  79.1 60.2 %collective-permute-start = (bf16[64,8,1024]{2,0,1:T(8,128)(2,1)}, bf16[64,8,1024]{2,0,1:T(8,128)(2,1)S(1)}, u32[]{:S(2)}, u32[]{:S(2)}) collective-permute-start(bf16[64,8,1024]{2,0,1:T(8,128)(2,1)} %all_to_all.27), channel_id=1, source_target_pairs={{32,0},{48,16},{64,32},{80,48},{96,64},{112,80},{128,96},{144,112}... | collective-permute-start | bytes 3145736 | tf_op jit(solution)/shard_map/ppermute | solution.py:16
  145.7 13.9 %collective-permute-start.2 = (bf16[2048,1024]{1,0:T(8,128)(2,1)}, bf16[2048,1024]{1,0:T(8,128)(2,1)}, u32[]{:S(2)}, u32[]{:S(2)}) collective-permute-start(bf16[2048,1024]{1,0:T(8,128)(2,1)} %copy.27), channel_id=1, source_target_pairs={{0,16},{16,0},{32,48},{48,32},{64,80},{80,64},{96,112},{112,96},{1... | collective-permute-start | bytes 12582920 | tf_op jit(solution)/shard_map/ppermute | solution.py:50
  145.7 9.0 %collective-permute-start.3 = (bf16[64,8,1024]{2,0,1:T(8,128)(2,1)}, bf16[64,8,1024]{2,0,1:T(8,128)(2,1)}, u32[]{:S(2)}, u32[]{:S(2)}) collective-permute-start(bf16[64,8,1024]{2,0,1:T(8,128)(2,1)} %all_to_all.27), channel_id=1, source_target_pairs={{0,16},{16,0},{32,48},{48,32},{64,80},{80,64},{96,112},{112,96},{1... | collective-permute-start | bytes 3145736 | tf_op jit(solution)/shard_map/ppermute | solution.py:100
  147.3 8.9 %collective-permute-start.4 = (bf16[64,8,1024]{2,0,1:T(8,128)(2,1)}, bf16[64,8,1024]{2,0,1:T(8,128)(2,1)}, u32[]{:S(2)}, u32[]{:S(2)}) collective-permute-start(bf16[64,8,1024]{2,0,1:T(8,128)(2,1)} %broadcast_select_fusion), channel_id=1, source_target_pairs={{0,16},{16,0},{32,48},{48,32},{64,80},{80,64},{96,112},{112,96},{1... | collective-permute-start | bytes 3145736 | tf_op jit(solution)/shard_map/ppermute | solution.py:102
  165.4 2.6 copy-start.2
  182.4 6.4 %slice-start = ((bf16[3072,1024]{1,0:T(8,128)(2,1)}), bf16[1024,1024]{1,0:T(8,128)(2,1)S(1)}, s32[]{:S(2)}) async-start(bf16[3072,1024]{1,0:T(8,128)(2,1)} %copy-done.2), calls=%async_computation.3 | async-start | bytes 4194304 | tf_op jit(solution)/shard_map/slice | solution.py:113
  182.4 6.4 %copy-start.4 = (bf16[64,8,1024,1]{2,0,1,3:T(8,128)(2,1)S(1)}, bf16[64,8,1024,1]{2,0,1,3:T(8,128)(2,1)}, u32[]{:S(2)}) copy-start(bf16[64,8,1024,1]{2,0,1,3:T(8,128)(2,1)} %reshape.69) | copy-start | bytes 3145732
  197.6 14.4 %copy-start.3 = (bf16[8,16,320,64]{2,3,0,1:T(8,128)(2,1)S(1)}, bf16[8,16,320,64]{2,3,0,1:T(8,128)(2,1)}, u32[]{:S(2)}) copy-start(bf16[8,16,320,64]{2,3,0,1:T(8,128)(2,1)} %get-tuple-element.11) | copy-start | bytes 15728644
  218.0 40.9 %copy-start.7 = (bf16[4,128,1024]{2,1,0:T(8,128)(2,1)S(1)}, bf16[4,128,1024]{2,1,0:T(8,128)(2,1)}, u32[]{:S(2)}) copy-start(bf16[4,128,1024]{2,1,0:T(8,128)(2,1)} %copy-done.6) | copy-start | bytes 3145732
  220.4 38.5 %all-to-all-start.1 = ((bf16[64,8,1024]{2,1,0:T(8,128)(2,1)}), bf16[64,8,1024]{2,1,0:T(8,128)(2,1)}, u32[]{:S(2)}, u32[]{:S(2)}) async-start(bf16[64,8,1024]{2,1,0:T(8,128)(2,1)} %copy.32), calls=%async_computation.1 | async-start | bytes 2097152 | tf_op jit(solution)/shard_map/all_to_all | solution.py:130
  258.9 4.9 %copy-start.1 = (bf16[1024,1024]{1,0:T(8,128)(2,1)S(1)}, bf16[1024,1024]{1,0:T(8,128)(2,1)}, u32[]{:S(2)}) copy-start(bf16[1024,1024]{1,0:T(8,128)(2,1)} %param.10) | copy-start | bytes 6291460
Sparse Core Ops, SparseCore 0:
  9.9 125.6 all-gather.1

commit v7 on v6

--- a/solution.py
+++ b/solution.py
@@ -47,12 +47,11 @@
 def swap_halves(gathered, halves, axis_pair):
     pair_index = lax.axis_index(axis_pair) % 2
     count = lax.axis_size(axis_pair)
-    other = lax.ppermute(gathered, axis_pair, [(i, i ^ 1) for i in range(count)])
     results = []
     start = 0
     for half in halves:
         own_part = gathered[start:start + half]
-        other_part = other[start:start + half]
+        other_part = lax.ppermute(own_part, axis_pair, [(i, i ^ 1) for i in range(count)])
         start += half
         results.append(
             jnp.where(

time: 272 us -> 274 us (level)
  other arithmetic: 26.7 us -> 29.5 us
    slice x2 -> x0, local copies, waits for them, and re-layouts: 4.47 us -> none  [swap_halves(): other_part = other[start:start + half]]
    ppermute x1 -> x2, waiting for transfers between devices: 0.01 us -> 2.79 us  [swap_halves(): lax.ppermute(own_part, axis_pair, [(i, i ^ 1) for i in range(count)])]
    unnamed x25 -> x31, local copies, waits for them, and re-layouts: 12.3 us -> 14.5 us
  transfers between devices with their start and end apart: 7 -> 8, of which waited for: 5 -> 6; matrix products, arithmetic and copies ran while one was open for 14% -> 14% of each run, Pallas kernels for 0% -> 0%
where the time goes in v7:
time: 274 us; the launch traced here: 273 us
  waiting for transfers between devices  90.1 us (33%)
  matrix products  45.6 us (17%)
  blocking collectives  41.8 us (15%)
  local copies, waits for them, and re-layouts  41.1 us (15%)
  other arithmetic  29.5 us (11%)
  between operations  13.7 us (5%)
  starting transfers between devices  11.5 us (4%)
    ppermute x2, waiting for transfers between devices, from_group(): return lax.ppermute(block, axis, route)  59.9 us
    all_to_all x1, blocking collectives, per_device(): lax.all_to_all(normed_inter, 'tm', split_axis=1, concat_axis=0, tiled=True)  41.8 us
    all_to_all x1, waiting for transfers between devices, per_device(): lax.all_to_all(mixed_heads.reshape(char_count, frame_count, feature_width...  25.5 us
    sub x2, other arithmetic, softmax_rows(): weights = jnp.exp(scores - row_top)  17.5 us
    unnamed x31, local copies, waits for them, and re-layouts  14.5 us
    dot_general x1, matrix products, per_device(): jnp.einsum('mfk,thdk->tfhmd', stacked, i_w[1:], preferred_element_type=jn...  14.4 us
    dot_general x1, matrix products, per_device(): jnp.einsum('fhcd,fhmd->fhcm', queries, pairs[0], preferred_element_type=j...  8.8 us
    all_to_all x1, starting transfers between devices, per_device(): lax.all_to_all(mixed_heads.reshape(char_count, frame_count, feature_width...  7.84 us
  transfers between devices with their start and end apart: 8, of which 6 were waited for; matrix products, arithmetic and copies ran while one was open for 14% of the time, Pallas kernels for 0%

profile of v7, /device:TPU:8, one launch (start us, length us, event | category | flops | bytes accessed | tf_op | source)
XLA Modules:
  0.0 273.4 jit_solution(1198356105639413888)
XLA Ops:
  6.5 0.0 all-gather.2.cloned.1.call-start
  6.5 1.0 dynamic-slice_bitcast_fusion.1
  7.5 0.9 dynamic-slice_bitcast_fusion
  8.5 0.7 pad_maximum_fusion
  9.2 0.0 all-gather.2.cloned.1.call-update
  9.2 0.0 copy-start.10
  9.3 0.0 copy-start.12
  9.3 8.7 %copy.23 = bf16[1024,3072]{0,1:T(8,128)(2,1)} copy(bf16[1024,3072]{1,0:T(8,128)(2,1)} %param.9) | data formatting | bytes 12582912 | tf_op args[2]
  18.0 0.0 copy-done.10
  18.0 0.3 fusion.14
  18.3 5.9 %convert_bitcast_fusion.1 = bf16[3,4,16,128,64]{3,4,2,0,1:T(8,128)(2,1)S(1)} fusion(bf16[1024,3,16,64,1]{0,3,2,1,4:T(8,128)(2,1)} %bitcast.96, bf16[4,128,1024]{2,1,0:T(8,128)(2,1)S(1)} %copy-done.10, f32[1024]{0:T(1024)S(1)} %bitcast.104, f32[1024]{0:T(1024)S(1)} %bitcast.105, f32[4,128]{1,0:T(4,128)S(1)} %add_rsqrt_fusion.1), kind=kOutput, calls=%fused_computation.25 | convolution fusion | flops 3225419776 | bytes 10496000 | tf_op jit(solution)/shard_map/nfk,kshd->snhfd/dot_general | solution.py:74
  24.2 0.0 copy-start.7
  24.2 0.8 fusion.47
  25.0 3.0 %fusion.60 = (f32[4,16,128]{2,1,0:T(8,128)S(1)}, f32[4,16,128,128]{2,3,1,0:T(8,128)}) fusion(f32[4,16,128,128]{2,3,1,0:T(8,128)S(1)} %fusion.47), kind=kOutput, calls=%fused_computation.88 | output fusion | flops 4194431 | bytes 8421376 | tf_op jit(solution)/shard_map/sub | solution.py:30
  28.0 0.0 copy-done
  28.0 4.8 %fusion.19 = (f32[4,128]{1,0:T(4,128)S(1)}, bf16[4,128,1024]{2,1,0:T(8,128)(2,1)S(1)}) fusion(bf16[16,64,1024,1]{2,1,0,3:T(8,128)(2,1)S(1)} %bitcast.92, f32[4,16,128,128]{2,3,1,0:T(8,128)} %get-tuple-element.20, f32[4,16,128]{2,1,0:T(8,128)S(1)} %get-tuple-element.19, bf16[3,4,16,128,64]{3,4,2,0,1:T(8,128)(2,1)} %copy-done.7, f32[1024]{0:T(1024)S(1)} %bitcast.103, ...), kind=kOutput, calls=%fused_computation.34 | convolution fusion | flops 1214250496 | bytes 9476096 | tf_op jit(solution)/shard_map/nhfd,hdo->nfo/dot_general | solution.py:84
  32.8 0.0 copy-start.8
  32.8 0.4 fusion.22
  33.2 0.8 copy.25
  34.0 41.8 %all_to_all.33 = bf16[4,128,1024]{2,0,1:T(4,128)(2,1)S(1)} all-to-all(bf16[4,128,1024]{2,0,1:T(4,128)(2,1)S(1)} %copy.25), channel_id=1, replica_groups=mesh['grp'=16,'tm'=16] {'tm'}, dimensions={1} | all-to-all | bytes 2097152 | tf_op jit(solution)/shard_map/all_to_all | solution.py:93
  75.8 0.4 copy.54
  76.2 0.0 copy-done.8
  76.2 0.3 all_to_all.27
  76.5 1.9 collective-permute-start.1
  78.5 1.1 collective-permute-start
  79.5 38.0 %collective-permute-done.1 = bf16[64,8,1024]{2,0,1:T(8,128)(2,1)} collective-permute-done((bf16[64,8,1024]{2,0,1:T(8,128)(2,1)S(1)}, bf16[64,8,1024]{2,0,1:T(8,128)(2,1)}, u32[]{:S(2)}, u32[]{:S(2)}) %collective-permute-start.1) | collective-permute-done | bytes 1048608 | tf_op jit(solution)/shard_map/ppermute | solution.py:16
  117.5 21.9 %collective-permute-done = bf16[64,8,1024]{2,0,1:T(8,128)(2,1)} collective-permute-done((bf16[64,8,1024]{2,0,1:T(8,128)(2,1)S(1)}, bf16[64,8,1024]{2,0,1:T(8,128)(2,1)}, u32[]{:S(2)}, u32[]{:S(2)}) %collective-permute-start) | collective-permute-done | bytes 1048608 | tf_op jit(solution)/shard_map/ppermute | solution.py:16
  139.4 6.4 %copy.27 = bf16[2048,1024]{1,0:T(8,128)(2,1)} copy(bf16[2048,1024]{0,1:T(8,128)(2,1)} %all-gather.2.cloned.1.call-done) | data formatting | bytes 8388608 | tf_op jit(solution)/shard_map/optimization_barrier | solution.py:100
  145.8 2.2 slice.68
  148.0 0.1 collective-permute-start.2
  148.1 0.5 collective-permute-start.3
  148.6 2.3 broadcast_select_fusion
  150.9 0.1 collective-permute-start.4
  151.1 0.2 dynamic-slice_reduce_fusion
  151.2 0.1 add_compare_fusion
  151.3 0.1 broadcast_in_dim.8
  151.4 0.1 gt.12
  151.5 2.2 reshape.69
  153.7 1.3 constant_dynamic-update-slice_fusion.2
  154.9 0.5 collective-permute-done.3
  155.4 1.5 collective-permute-done.4
  156.9 1.6 select_dynamic-update-slice_fusion.1
  158.5 1.3 constant_dynamic-update-slice_fusion.1
  159.8 1.6 select_dynamic-update-slice_fusion
  161.5 1.3 constant_dynamic-update-slice_fusion
  162.8 0.0 collective-permute-done.2
  162.8 5.0 %maximum_select_fusion = bf16[3072,1024]{1,0:T(8,128)(2,1)S(1)} fusion(bf16[1536,1024]{1,0:T(8,128)(2,1)} %collective-permute-done.2, bf16[1536,1024]{1,0:T(8,128)(2,1)S(1)} %slice.68, pred[]{:T(512)S(6)} %eq.6), kind=kLoop, calls=%fused_computation.9 | loop fusion | flops 28311552 | bytes 12582913 | tf_op jit(solution)/shard_map/jit(_where)/select_n | solution.py:57
  167.8 0.5 slice.69
  168.2 2.1 copy-done.2
  170.4 14.4 %convert_bitcast_fusion = bf16[2,8,16,320,64]{3,4,1,2,0:T(8,128)(2,1)S(1)} fusion(bf16[2,16,64,1024,1]{3,2,4,1,0:T(8,128)(2,1)S(1)} %bitcast.97, bf16[320,8,1024]{2,0,1:T(8,128)(2,1)S(1)} %constant_dynamic-update-slice_fusion), kind=kOutput, calls=%fused_computation.5 | convolution fusion | flops 10742661120 | bytes 19922944 | tf_op jit(solution)/shard_map/mfk,thdk->tfhmd/dot_general | solution.py:115
  184.8 0.0 slice-start
  184.8 6.6 %slice_bitcast_fusion.1 = (bf16[8,16,320,64]{2,3,0,1:T(8,128)(2,1)}, bf16[8,16,320,64]{2,3,0,1:T(8,128)(2,1)}) fusion(bf16[2,8,16,320,64]{3,4,1,2,0:T(8,128)(2,1)S(1)} %convert_bitcast_fusion), kind=kLoop, calls=%fused_computation.8 | loop fusion | bytes 20971520 | tf_op jit(solution)/shard_map/squeeze | solution.py:127
  191.4 8.8 %fusion.5 = f32[8,16,64,320]{3,2,1,0:T(8,128)} fusion(bf16[8,16,320,64]{2,3,0,1:T(8,128)(2,1)} %get-tuple-element.12, bf16[16,64,1024,1]{2,1,0,3:T(8,128)(2,1)S(1)} %bitcast.93, bf16[64,8,1024,1]{2,0,1,3:T(8,128)(2,1)S(1)} %copy-done.6), kind=kOutput, calls=%fused_computation.12 | convolution fusion | flops 1409810432 | bytes 18874368 | tf_op jit(solution)/shard_map/fhcd,fhmd->fhcm/dot_general | solution.py:118
  200.2 14.5 %fusion.61 = (f32[8,16,64]{2,1,0:T(8,128)S(1)}, f32[8,16,64,320]{3,2,1,0:T(8,128)}) fusion(f32[8,16,64,320]{3,2,1,0:T(8,128)} %fusion.5, pred[320]{0:T(512)(128)(4,1)S(1)} %gt.12), kind=kOutput, calls=%fused_computation.89 | output fusion | flops 15728959 | bytes 21004608 | tf_op jit(solution)/shard_map/sub | solution.py:30
  214.7 6.0 %fusion.39 = bf16[8,16,64,64]{3,2,1,0:T(8,128)(2,1)S(1)} fusion(f32[8,16,64,320]{3,2,1,0:T(8,128)} %get-tuple-element.24, f32[8,16,64]{2,1,0:T(8,128)S(1)} %get-tuple-element.23, bf16[8,16,320,64]{2,3,0,1:T(8,128)(2,1)S(1)} %copy-done.4), kind=kOutput, calls=%fused_computation.54 | convolution fusion | flops 341311488 | bytes 16809984 | tf_op jit(solution)/shard_map/fhcm,fhmd->cfhd/dot_general | solution.py:126
  220.7 0.0 copy-start.9
  220.7 2.4 copy.31
  223.1 7.8 %all-to-all-start.1 = ((bf16[64,8,1024]{2,1,0:T(8,128)(2,1)}), bf16[64,8,1024]{2,1,0:T(8,128)(2,1)}, u32[]{:S(2)}, u32[]{:S(2)}) async-start(bf16[64,8,1024]{2,1,0:T(8,128)(2,1)} %copy.31), calls=%async_computation.1 | async-start | bytes 2097152 | tf_op jit(solution)/shard_map/all_to_all | solution.py:129
  231.0 1.3 slice.64
  232.3 1.0 copy-done.11
  233.3 0.0 collective-permute-start.5
  233.3 2.8 %collective-permute-done.5 = bf16[512,1024]{0,1:T(8,128)(2,1)} collective-permute-done((bf16[512,1024]{0,1:T(8,128)(2,1)S(1)}, bf16[512,1024]{0,1:T(8,128)(2,1)}, u32[]{:S(2)}, u32[]{:S(2)}) %collective-permute-start.5) | collective-permute-done | bytes 1048608 | tf_op jit(solution)/shard_map/ppermute | solution.py:54
  236.1 25.5 %all-to-all-done.1 = bf16[64,8,1024]{2,1,0:T(8,128)(2,1)} async-done(((bf16[64,8,1024]{2,1,0:T(8,128)(2,1)}), bf16[64,8,1024]{2,1,0:T(8,128)(2,1)}, u32[]{:S(2)}, u32[]{:S(2)}) %all-to-all-start.1) | async-done | bytes 1048608 | tf_op jit(solution)/shard_map/all_to_all | solution.py:129
  261.6 4.9 %fusion.23 = bf16[4,128,1024]{2,1,0:T(8,128)(2,1)} fusion(bf16[4,128,1024]{2,1,0:T(8,128)(2,1)S(1)} %copy-done.9, bf16[512,1024]{0,1:T(8,128)(2,1)} %collective-permute-done.5, bf16[512,1024]{0,1:T(8,128)(2,1)} %copy-done.11, pred[]{:T(512)S(6)} %eq.6, bf16[4,16,8,1024]{3,2,0,1:T(8,128)(2,1)} %bitcast.37, f32[1024]{0:T(1024)S(1)} %bitcast.102), kind=kOutput, calls=%fused_computation.38 | convolution fusion | flops 1085276160 | bytes 5246977 | tf_op jit(solution)/shard_map/tk,ok->to/dot_general | solution.py:136
  (23 shorter events, 0.1 us)
Async XLA Ops:
  6.5 21.4 %copy-start = (bf16[1024,1024]{1,0:T(8,128)(2,1)S(1)}, bf16[1024,1024]{1,0:T(8,128)(2,1)}, u32[]{:S(2)}) copy-start(bf16[1024,1024]{1,0:T(8,128)(2,1)} %param.10) | copy-start | bytes 6291460
  6.5 132.9 %all-gather.2.cloned.1.call-start = ((), (), s32[]{:S(2)}) async-start(), calls=%async_computation.2 | async-start | bytes 4456448 | tf_op jit(solution)/shard_map/all_gather | solution.py:44
  9.2 8.8 %copy-start.10 = (bf16[4,128,1024]{2,1,0:T(8,128)(2,1)S(1)}, bf16[4,128,1024]{2,1,0:T(8,128)(2,1)}, u32[]{:S(2)}) copy-start(bf16[4,128,1024]{2,1,0:T(8,128)(2,1)} %param.7) | copy-start | bytes 3145732
  9.3 9.0 %copy-start.12 = (f32[6,1024]{1,0:T(8,128)S(1)}, f32[6,1024]{1,0:T(8,128)}, u32[]{:S(2)}) copy-start(f32[6,1024]{1,0:T(8,128)} %param.8) | copy-start | bytes 73732
  24.2 3.7 %copy-start.7 = (bf16[3,4,16,128,64]{3,4,2,0,1:T(8,128)(2,1)}, bf16[3,4,16,128,64]{3,4,2,0,1:T(8,128)(2,1)S(1)}, u32[]{:S(2)}) copy-start(bf16[3,4,16,128,64]{3,4,2,0,1:T(8,128)(2,1)S(1)} %convert_bitcast_fusion.1) | copy-start | bytes 9437188
  32.8 43.4 %copy-start.8 = (bf16[4,128,1024]{2,1,0:T(8,128)(2,1)}, bf16[4,128,1024]{2,1,0:T(8,128)(2,1)S(1)}, u32[]{:S(2)}) copy-start(bf16[4,128,1024]{2,1,0:T(8,128)(2,1)S(1)} %get-tuple-element.22) | copy-start | bytes 3145732
  76.2 63.2 %copy-start.3 = (bf16[4,16,8,1024]{3,0,1,2:T(4,128)(2,1)}, bf16[4,16,8,1024]{3,0,1,2:T(4,128)(2,1)S(1)}, u32[]{:S(2)}) copy-start(bf16[4,16,8,1024]{3,0,1,2:T(4,128)(2,1)S(1)} %copy.54) | copy-start | bytes 3145732
  76.5 62.9 %copy-start.5 = (bf16[64,8,1024]{2,0,1:T(8,128)(2,1)}, bf16[64,8,1024]{2,0,1:T(8,128)(2,1)S(1)}, u32[]{:S(2)}) copy-start(bf16[64,8,1024]{2,0,1:T(8,128)(2,1)S(1)} %all_to_all.27) | copy-start | bytes 3145732
  76.5 41.0 %collective-permute-start.1 = (bf16[64,8,1024]{2,0,1:T(8,128)(2,1)S(1)}, bf16[64,8,1024]{2,0,1:T(8,128)(2,1)}, u32[]{:S(2)}, u32[]{:S(2)}) collective-permute-start(bf16[64,8,1024]{2,0,1:T(8,128)(2,1)S(1)} %all_to_all.27), channel_id=1, source_target_pairs={{224,0},{240,16},{0,32},{16,48},{32,64},{48,80},{64,96},{80,112},{... | collective-permute-start | bytes 3145736 | tf_op jit(solution)/shard_map/ppermute | solution.py:16
  78.5 60.9 %collective-permute-start = (bf16[64,8,1024]{2,0,1:T(8,128)(2,1)S(1)}, bf16[64,8,1024]{2,0,1:T(8,128)(2,1)}, u32[]{:S(2)}, u32[]{:S(2)}) collective-permute-start(bf16[64,8,1024]{2,0,1:T(8,128)(2,1)S(1)} %all_to_all.27), channel_id=1, source_target_pairs={{32,0},{48,16},{64,32},{80,48},{96,64},{112,80},{128,96},{144,112}... | collective-permute-start | bytes 3145736 | tf_op jit(solution)/shard_map/ppermute | solution.py:16
  145.8 5.2 %copy-start.13 = (s32[16,4]{0,1:T(4,128)S(1)}, s32[16,4]{0,1:T(4,128)}, u32[]{:S(2)}) copy-start(s32[16,4]{0,1:T(4,128)} %param.13) | copy-start | bytes 772
  148.0 14.7 %collective-permute-start.2 = (bf16[1536,1024]{1,0:T(8,128)(2,1)S(1)}, bf16[1536,1024]{1,0:T(8,128)(2,1)}, u32[]{:S(2)}, u32[]{:S(2)}) collective-permute-start(bf16[1536,1024]{1,0:T(8,128)(2,1)S(1)} %slice.68), channel_id=1, source_target_pairs={{0,16},{16,0},{32,48},{48,32},{64,80},{80,64},{96,112},{112,96},{1... | collective-permute-start | bytes 9437192 | tf_op jit(solution)/shard_map/ppermute | solution.py:54
  148.1 7.3 %collective-permute-start.3 = (bf16[64,8,1024]{2,0,1:T(8,128)(2,1)}, bf16[64,8,1024]{2,0,1:T(8,128)(2,1)}, u32[]{:S(2)}, u32[]{:S(2)}) collective-permute-start(bf16[64,8,1024]{2,0,1:T(8,128)(2,1)} %copy-done.5), channel_id=1, source_target_pairs={{0,16},{16,0},{32,48},{48,32},{64,80},{80,64},{96,112},{112,96},{1... | collective-permute-start | bytes 3145736 | tf_op jit(solution)/shard_map/ppermute | solution.py:99
  150.9 6.0 %collective-permute-start.4 = (bf16[64,8,1024]{2,0,1:T(8,128)(2,1)}, bf16[64,8,1024]{2,0,1:T(8,128)(2,1)}, u32[]{:S(2)}, u32[]{:S(2)}) collective-permute-start(bf16[64,8,1024]{2,0,1:T(8,128)(2,1)} %broadcast_select_fusion), channel_id=1, source_target_pairs={{0,16},{16,0},{32,48},{48,32},{64,80},{80,64},{96,112},{112,96},{1... | collective-permute-start | bytes 3145736 | tf_op jit(solution)/shard_map/ppermute | solution.py:101
  167.8 2.6 copy-start.2
  184.8 6.7 %slice-start = ((bf16[3072,1024]{1,0:T(8,128)(2,1)}), bf16[1024,1024]{1,0:T(8,128)(2,1)S(1)}, s32[]{:S(2)}) async-start(bf16[3072,1024]{1,0:T(8,128)(2,1)} %copy-done.2), calls=%async_computation.3 | async-start | bytes 4194304 | tf_op jit(solution)/shard_map/slice | solution.py:112
  184.8 6.6 %copy-start.6 = (bf16[64,8,1024,1]{2,0,1,3:T(8,128)(2,1)S(1)}, bf16[64,8,1024,1]{2,0,1,3:T(8,128)(2,1)}, u32[]{:S(2)}) copy-start(bf16[64,8,1024,1]{2,0,1,3:T(8,128)(2,1)} %reshape.69) | copy-start | bytes 3145732
  200.2 14.5 %copy-start.4 = (bf16[8,16,320,64]{2,3,0,1:T(8,128)(2,1)S(1)}, bf16[8,16,320,64]{2,3,0,1:T(8,128)(2,1)}, u32[]{:S(2)}) copy-start(bf16[8,16,320,64]{2,3,0,1:T(8,128)(2,1)} %get-tuple-element.11) | copy-start | bytes 15728644
  220.7 40.9 %copy-start.9 = (bf16[4,128,1024]{2,1,0:T(8,128)(2,1)S(1)}, bf16[4,128,1024]{2,1,0:T(8,128)(2,1)}, u32[]{:S(2)}) copy-start(bf16[4,128,1024]{2,1,0:T(8,128)(2,1)} %copy-done.8) | copy-start | bytes 3145732
  223.1 38.4 %all-to-all-start.1 = ((bf16[64,8,1024]{2,1,0:T(8,128)(2,1)}), bf16[64,8,1024]{2,1,0:T(8,128)(2,1)}, u32[]{:S(2)}, u32[]{:S(2)}) async-start(bf16[64,8,1024]{2,1,0:T(8,128)(2,1)} %copy.31), calls=%async_computation.1 | async-start | bytes 2097152 | tf_op jit(solution)/shard_map/all_to_all | solution.py:129
  232.3 1.0 copy-start.11
  233.3 2.8 %collective-permute-start.5 = (bf16[512,1024]{0,1:T(8,128)(2,1)S(1)}, bf16[512,1024]{0,1:T(8,128)(2,1)}, u32[]{:S(2)}, u32[]{:S(2)}) collective-permute-start(bf16[512,1024]{0,1:T(8,128)(2,1)S(1)} %slice.64), channel_id=1, source_target_pairs={{0,16},{16,0},{32,48},{48,32},{64,80},{80,64},{96,112},{112,96},{1... | collective-permute-start | bytes 3145736 | tf_op jit(solution)/shard_map/ppermute | solution.py:54
  261.6 4.9 %copy-start.1 = (bf16[1024,1024]{1,0:T(8,128)(2,1)S(1)}, bf16[1024,1024]{1,0:T(8,128)(2,1)}, u32[]{:S(2)}) copy-start(bf16[1024,1024]{1,0:T(8,128)(2,1)} %param.10) | copy-start | bytes 6291460
Sparse Core Ops, SparseCore 0:
  9.9 125.7 all-gather.1

commit v8 on v6

--- a/solution.py
+++ b/solution.py
@@ -113,9 +113,12 @@
         "cfk,hdk->fhcd", frames_own, i_w[0], preferred_element_type=jnp.float32
     ).astype(jnp.bfloat16)
     stacked = jnp.concatenate([frames_own] + others, axis=0)
-    pairs = jnp.einsum(
-        "mfk,thdk->tfhmd", stacked, i_w[1:], preferred_element_type=jnp.float32
-    ).astype(jnp.bfloat16)
+    pairs = [
+        jnp.einsum(
+            "mfk,hdk->fhmd", stacked, i_w[part], preferred_element_type=jnp.float32
+        ).astype(jnp.bfloat16)
+        for part in (1, 2)
+    ]
     scores = jnp.einsum(
         "fhcd,fhmd->fhcm", queries, pairs[0], preferred_element_type=jnp.float32
     ) * scale

time: 272 us -> 271 us (level)
  local copies, waits for them, and re-layouts: 42.8 us -> 36.5 us
    dot_general x1, matrix products: 14.4 us -> 3.74 us  [per_device(): jnp.einsum('cfk,hdk->fhcd', frames_own, i_w[0], preferred_element_type=jn...]
    dot_general x1, matrix products: 5.97 us -> 13.3 us  [per_device(): jnp.einsum('fhcm,fhmd->cfhd', weights, pairs[1], preferred_element_type=j...]
    squeeze x1 -> x0, local copies, waits for them, and re-layouts: 6.41 us -> none  [per_device(): pairs[1]]
    dot_general x1, matrix products: 8.77 us -> 13.9 us  [per_device(): jnp.einsum('fhcd,fhmd->fhcm', queries, pairs[0], preferred_element_type=j...]
    unnamed x25 -> x21, local copies, waits for them, and re-layouts: 12.3 us -> 11.4 us
  transfers between devices with their start and end apart: 7 -> 7, of which waited for: 5 -> 5; matrix products, arithmetic and copies ran while one was open for 14% -> 16% of each run, Pallas kernels for 0% -> 0%
where the time goes in v8:
time: 271 us; the launch traced here: 270 us
  waiting for transfers between devices  90.5 us (33%)
  matrix products  47.4 us (17%)
  blocking collectives  42.1 us (16%)
  local copies, waits for them, and re-layouts  36.5 us (13%)
  other arithmetic  28.8 us (11%)
  between operations  13.6 us (5%)
  starting transfers between devices  11.4 us (4%)
    ppermute x2, waiting for transfers between devices, from_group(): return lax.ppermute(block, axis, route)  58.3 us
    all_to_all x1, blocking collectives, per_device(): lax.all_to_all(normed_inter, 'tm', split_axis=1, concat_axis=0, tiled=True)  42.1 us
    all_to_all x1, waiting for transfers between devices, per_device(): lax.all_to_all(mixed_heads.reshape(char_count, frame_count, feature_width...  26 us
    sub x2, other arithmetic, softmax_rows(): weights = jnp.exp(scores - row_top)  17.4 us
    dot_general x1, matrix products, per_device(): jnp.einsum('fhcd,fhmd->fhcm', queries, pairs[0], preferred_element_type=j...  13.9 us
    dot_general x1, matrix products, per_device(): jnp.einsum('fhcm,fhmd->cfhd', weights, pairs[1], preferred_element_type=j...  13.3 us
    unnamed x21, local copies, waits for them, and re-layouts  11.4 us
    all_to_all x1, starting transfers between devices, per_device(): lax.all_to_all(mixed_heads.reshape(char_count, frame_count, feature_width...  7.95 us
  transfers between devices with their start and end apart: 7, of which 5 were waited for; matrix products, arithmetic and copies ran while one was open for 16% of the time, Pallas kernels for 0%

profile of v8, /device:TPU:8, one launch (start us, length us, event | category | flops | bytes accessed | tf_op | source)
XLA Modules:
  0.0 270.3 jit_solution(1083922397730545098)
XLA Ops:
  6.5 0.0 copy-start
  6.5 0.0 all-gather.2.cloned.1.call-start
  6.5 1.0 dynamic-slice_bitcast_fusion.1
  7.5 0.9 dynamic-slice_bitcast_fusion
  8.5 0.7 pad_maximum_fusion
  9.2 0.0 all-gather.2.cloned.1.call-update
  9.2 0.0 copy-start.6
  9.2 0.0 copy-start.7
  9.2 8.7 %copy.31 = bf16[1024,3072]{0,1:T(8,128)(2,1)} copy(bf16[1024,3072]{1,0:T(8,128)(2,1)} %param.9) | data formatting | bytes 12582912 | tf_op args[2]
  18.0 0.0 copy-done.6
  18.0 0.3 fusion.23
  18.3 0.0 copy-done.7
  18.3 5.9 %convert_bitcast_fusion = bf16[3,4,16,128,64]{3,4,2,0,1:T(8,128)(2,1)S(1)} fusion(bf16[1024,3,16,64,1]{0,3,2,1,4:T(8,128)(2,1)} %bitcast.99, bf16[4,128,1024]{2,1,0:T(8,128)(2,1)S(1)} %copy-done.6, f32[1024]{0:T(1024)S(1)} %bitcast.111, f32[1024]{0:T(1024)S(1)} %bitcast.112, f32[4,128]{1,0:T(4,128)S(1)} %add_rsqrt_fusion.1), kind=kOutput, calls=%fused_computation.27 | convolution fusion | flops 3225419776 | bytes 10496000 | tf_op jit(solution)/shard_map/nfk,kshd->snhfd/dot_general | solution.py:75
  24.2 0.0 copy-start.2
  24.2 0.8 fusion.56
  25.0 2.9 %fusion.70 = (f32[4,16,128]{2,1,0:T(8,128)S(1)}, f32[4,16,128,128]{2,3,1,0:T(8,128)}) fusion(f32[4,16,128,128]{2,3,1,0:T(8,128)S(1)} %fusion.56), kind=kOutput, calls=%fused_computation.91 | output fusion | flops 4194431 | bytes 8421376 | tf_op jit(solution)/shard_map/sub | solution.py:30
  27.9 0.0 copy-done.2
  27.9 0.0 copy-done
  27.9 4.8 %fusion.28 = (f32[4,128]{1,0:T(4,128)S(1)}, bf16[4,128,1024]{2,1,0:T(8,128)(2,1)S(1)}) fusion(bf16[16,64,1024,1]{2,1,0,3:T(8,128)(2,1)S(1)} %bitcast.98, f32[4,16,128,128]{2,3,1,0:T(8,128)} %get-tuple-element.23, f32[4,16,128]{2,1,0:T(8,128)S(1)} %get-tuple-element.22, bf16[3,4,16,128,64]{3,4,2,0,1:T(8,128)(2,1)} %copy-done.2, f32[1024]{0:T(1024)S(1)} %bitcast.110, ...), kind=kOutput, calls=%fused_computation.36 | convolution fusion | flops 1214250496 | bytes 9476096 | tf_op jit(solution)/shard_map/nhfd,hdo->nfo/dot_general | solution.py:85
  32.7 0.0 copy-start.4
  32.8 0.4 fusion.31
  33.1 0.8 copy.33
  34.0 42.1 %all_to_all.33 = bf16[4,128,1024]{2,0,1:T(4,128)(2,1)S(1)} all-to-all(bf16[4,128,1024]{2,0,1:T(4,128)(2,1)S(1)} %copy.33), channel_id=1, replica_groups=mesh['grp'=16,'tm'=16] {'tm'}, dimensions={1} | all-to-all | bytes 2097152 | tf_op jit(solution)/shard_map/all_to_all | solution.py:94
  76.0 0.3 copy.64
  76.4 0.0 copy-done.4
  76.4 0.1 copy.35
  76.5 1.6 constant_dynamic-update-slice_fusion.2
  78.1 1.6 collective-permute-start.1
  79.6 1.3 collective-permute-start
  81.0 36.5 %collective-permute-done.1 = bf16[64,8,1024]{2,0,1:T(8,128)(2,1)S(1)} collective-permute-done((bf16[64,8,1024]{2,0,1:T(8,128)(2,1)S(1)}, bf16[64,8,1024]{2,0,1:T(8,128)(2,1)S(1)}, u32[]{:S(2)}, u32[]{:S(2)}) %collective-permute-start.1) | collective-permute-done | bytes 1048608 | tf_op jit(solution)/shard_map/ppermute | solution.py:16
  117.5 0.0 copy-done.3
  117.5 21.7 %collective-permute-done = bf16[64,8,1024]{2,0,1:T(8,128)(2,1)S(1)} collective-permute-done((bf16[64,8,1024]{2,0,1:T(8,128)(2,1)S(1)}, bf16[64,8,1024]{2,0,1:T(8,128)(2,1)S(1)}, u32[]{:S(2)}, u32[]{:S(2)}) %collective-permute-start) | collective-permute-done | bytes 1048608 | tf_op jit(solution)/shard_map/ppermute | solution.py:16
  139.2 6.4 %copy.38 = bf16[2048,1024]{1,0:T(8,128)(2,1)} copy(bf16[2048,1024]{0,1:T(8,128)(2,1)} %all-gather.2.cloned.1.call-done) | data formatting | bytes 8388608 | tf_op jit(solution)/shard_map/optimization_barrier | solution.py:101
  145.6 0.0 collective-permute-start.2
  145.6 0.5 collective-permute-start.3
  146.2 1.1 broadcast_select_fusion
  147.2 0.0 collective-permute-start.4
  147.3 0.0 copy-done.8
  147.3 0.2 dynamic-slice_reduce_fusion
  147.4 0.1 add_compare_fusion
  147.5 0.1 broadcast_in_dim.8
  147.6 0.1 gt.12
  147.7 2.2 slice.70
  149.9 4.8 %collective-permute-done.3 = bf16[64,8,1024]{2,0,1:T(8,128)(2,1)} collective-permute-done((bf16[64,8,1024]{2,0,1:T(8,128)(2,1)}, bf16[64,8,1024]{2,0,1:T(8,128)(2,1)}, u32[]{:S(2)}, u32[]{:S(2)}) %collective-permute-start.3) | collective-permute-done | bytes 1048608 | tf_op jit(solution)/shard_map/ppermute | solution.py:100
  154.6 1.5 collective-permute-done.4
  156.1 2.7 select_dynamic-update-slice_fusion.1
  158.8 1.1 constant_dynamic-update-slice_fusion.1
  159.9 2.6 select_dynamic-update-slice_fusion
  162.6 1.0 constant_dynamic-update-slice_fusion
  163.6 0.0 collective-permute-done.2
  163.6 2.2 slice.71
  165.8 3.6 %maximum_select_fusion = bf16[3072,1024]{1,0:T(8,128)(2,1)S(1)} fusion(bf16[1536,1024]{1,0:T(8,128)(2,1)S(1)} %slice.71, bf16[1536,1024]{1,0:T(8,128)(2,1)S(1)} %slice.70, pred[]{:T(512)S(6)} %eq.6), kind=kLoop, calls=%fused_computation.6 | loop fusion | flops 28311552 | bytes 12582913 | tf_op jit(solution)/shard_map/jit(_where)/select_n | solution.py:58
  169.4 2.7 %fusion.68 = (bf16[1024,1024]{1,0:T(8,128)(2,1)}, bf16[1024,1024]{1,0:T(8,128)(2,1)}, bf16[1024,1024]{1,0:T(8,128)(2,1)S(1)}) fusion(bf16[3072,1024]{1,0:T(8,128)(2,1)S(1)} %maximum_select_fusion), kind=kLoop, calls=%fused_computation.89 | loop fusion | bytes 12582912 | tf_op jit(solution)/shard_map/slice | solution.py:118
  172.1 3.7 %fusion.58 = bf16[16,64,64,8]{2,1,0,3:T(8,128)(2,1)} fusion(bf16[16,64,1024,1]{2,1,0,3:T(8,128)(2,1)S(1)} %bitcast.106, bf16[64,8,1024,1]{2,1,0,3:T(8,128)(2,1)S(1)} %bitcast.101), kind=kOutput, calls=%fused_computation.63 | convolution fusion | flops 1073741824 | bytes 4194304 | tf_op jit(solution)/shard_map/cfk,hdk->fhcd/dot_general | solution.py:112
  175.9 13.9 %fusion.3 = f32[8,16,64,320]{3,2,1,0:T(8,128)} fusion(bf16[16,64,1024,1]{2,1,0,3:T(8,128)(2,1)} %bitcast.105, bf16[320,8,1024]{2,0,1:T(8,128)(2,1)} %constant_dynamic-update-slice_fusion, bf16[16,64,64,8]{2,1,0,3:T(8,128)(2,1)} %fusion.58), kind=kOutput, calls=%fused_computation.7 | convolution fusion | flops 5706874880 | bytes 18874368 | tf_op jit(solution)/shard_map/fhcd,fhmd->fhcm/dot_general | solution.py:122
  189.8 14.4 %fusion.71 = (f32[8,16,64]{2,1,0:T(8,128)S(1)}, f32[8,16,64,320]{3,2,1,0:T(8,128)}) fusion(f32[8,16,64,320]{3,2,1,0:T(8,128)} %fusion.3, pred[320]{0:T(512)(128)(4,1)S(1)} %gt.12), kind=kOutput, calls=%fused_computation.92 | output fusion | flops 15728959 | bytes 21004608 | tf_op jit(solution)/shard_map/sub | solution.py:30
  204.2 13.3 %fusion.46 = bf16[8,16,64,64]{3,2,1,0:T(8,128)(2,1)S(1)} fusion(f32[8,16,64,320]{3,2,1,0:T(8,128)} %get-tuple-element.27, f32[8,16,64]{2,1,0:T(8,128)S(1)} %get-tuple-element.26, bf16[16,64,1024,1]{2,1,0,3:T(8,128)(2,1)} %bitcast.104, bf16[320,8,1024]{2,0,1:T(8,128)(2,1)} %constant_dynamic-update-slice_fusion), kind=kOutput, calls=%fused_computation.55 | convolution fusion | flops 5712642048 | bytes 18907136 | tf_op jit(solution)/shard_map/fhcm,fhmd->cfhd/dot_general | solution.py:130
  217.5 0.0 copy-start.5
  217.5 2.4 copy.44
  220.0 7.9 %all-to-all-start.1 = ((bf16[64,8,1024]{2,1,0:T(8,128)(2,1)}), bf16[64,8,1024]{2,1,0:T(8,128)(2,1)}, u32[]{:S(2)}, u32[]{:S(2)}) async-start(bf16[64,8,1024]{2,1,0:T(8,128)(2,1)} %copy.44), calls=%async_computation.1 | async-start | bytes 2097152 | tf_op jit(solution)/shard_map/all_to_all | solution.py:133
  227.9 2.3 slice.75
  230.2 2.3 slice.76
  232.5 26.0 %all-to-all-done.1 = bf16[64,8,1024]{2,1,0:T(8,128)(2,1)} async-done(((bf16[64,8,1024]{2,1,0:T(8,128)(2,1)}), bf16[64,8,1024]{2,1,0:T(8,128)(2,1)}, u32[]{:S(2)}, u32[]{:S(2)}) %all-to-all-start.1) | async-done | bytes 1048608 | tf_op jit(solution)/shard_map/all_to_all | solution.py:133
  258.5 4.9 %fusion.32 = bf16[4,128,1024]{2,1,0:T(8,128)(2,1)} fusion(bf16[4,128,1024]{2,1,0:T(8,128)(2,1)S(1)} %copy-done.5, bf16[512,1024]{1,0:T(8,128)(2,1)} %slice.76, bf16[512,1024]{1,0:T(8,128)(2,1)} %slice.75, pred[]{:T(512)S(6)} %eq.6, bf16[4,16,8,1024]{3,2,0,1:T(8,128)(2,1)} %bitcast.39, f32[1024]{0:T(1024)S(1)} %bitcast.109), kind=kOutput, calls=%fused_computation.40 | convolution fusion | flops 1085276160 | bytes 5246977 | tf_op jit(solution)/shard_map/tk,ok->to/dot_general | solution.py:140
  (9 shorter events, 0.0 us)
Async XLA Ops:
  6.5 21.4 %copy-start = (bf16[1024,1024]{1,0:T(8,128)(2,1)S(1)}, bf16[1024,1024]{1,0:T(8,128)(2,1)}, u32[]{:S(2)}) copy-start(bf16[1024,1024]{1,0:T(8,128)(2,1)} %param.10) | copy-start | bytes 6291460
  6.5 132.7 %all-gather.2.cloned.1.call-start = ((), (), s32[]{:S(2)}) async-start(), calls=%async_computation.2 | async-start | bytes 4456448 | tf_op jit(solution)/shard_map/all_gather | solution.py:44
  9.2 8.8 %copy-start.6 = (bf16[4,128,1024]{2,1,0:T(8,128)(2,1)S(1)}, bf16[4,128,1024]{2,1,0:T(8,128)(2,1)}, u32[]{:S(2)}) copy-start(bf16[4,128,1024]{2,1,0:T(8,128)(2,1)} %param.7) | copy-start | bytes 3145732
  9.2 9.0 %copy-start.7 = (f32[6,1024]{1,0:T(8,128)S(1)}, f32[6,1024]{1,0:T(8,128)}, u32[]{:S(2)}) copy-start(f32[6,1024]{1,0:T(8,128)} %param.8) | copy-start | bytes 73732
  24.2 3.7 %copy-start.2 = (bf16[3,4,16,128,64]{3,4,2,0,1:T(8,128)(2,1)}, bf16[3,4,16,128,64]{3,4,2,0,1:T(8,128)(2,1)S(1)}, u32[]{:S(2)}) copy-start(bf16[3,4,16,128,64]{3,4,2,0,1:T(8,128)(2,1)S(1)} %convert_bitcast_fusion) | copy-start | bytes 9437188
  32.7 43.6 %copy-start.4 = (bf16[4,128,1024]{2,1,0:T(8,128)(2,1)}, bf16[4,128,1024]{2,1,0:T(8,128)(2,1)S(1)}, u32[]{:S(2)}) copy-start(bf16[4,128,1024]{2,1,0:T(8,128)(2,1)S(1)} %get-tuple-element.25) | copy-start | bytes 3145732
  78.0 39.5 %copy-start.3 = (bf16[64,8,1024]{2,0,1:T(8,128)(2,1)}, bf16[64,8,1024]{2,0,1:T(8,128)(2,1)S(1)}, u32[]{:S(2)}) copy-start(bf16[64,8,1024]{2,0,1:T(8,128)(2,1)S(1)} %get-tuple-element.15) | copy-start | bytes 3145732
  78.1 69.2 %copy-start.8 = (s32[16,4]{0,1:T(4,128)S(1)}, s32[16,4]{0,1:T(4,128)}, u32[]{:S(2)}) copy-start(s32[16,4]{0,1:T(4,128)} %param.13) | copy-start | bytes 772
  78.1 39.4 %collective-permute-start.1 = (bf16[64,8,1024]{2,0,1:T(8,128)(2,1)S(1)}, bf16[64,8,1024]{2,0,1:T(8,128)(2,1)S(1)}, u32[]{:S(2)}, u32[]{:S(2)}) collective-permute-start(bf16[64,8,1024]{2,0,1:T(8,128)(2,1)S(1)} %get-tuple-element.15), channel_id=1, source_target_pairs={{224,0},{240,16},{0,32},{16,48},{32,64},{48,80},{64,96},{80,112},{... | collective-permute-start | bytes 3145736 | tf_op jit(solution)/shard_map/ppermute | solution.py:16
  79.6 59.6 %collective-permute-start = (bf16[64,8,1024]{2,0,1:T(8,128)(2,1)S(1)}, bf16[64,8,1024]{2,0,1:T(8,128)(2,1)S(1)}, u32[]{:S(2)}, u32[]{:S(2)}) collective-permute-start(bf16[64,8,1024]{2,0,1:T(8,128)(2,1)S(1)} %get-tuple-element.15), channel_id=1, source_target_pairs={{32,0},{48,16},{64,32},{80,48},{96,64},{112,80},{128,96},{144,112}... | collective-permute-start | bytes 3145736 | tf_op jit(solution)/shard_map/ppermute | solution.py:16
  145.6 18.0 %collective-permute-start.2 = (bf16[2048,1024]{1,0:T(8,128)(2,1)}, bf16[2048,1024]{1,0:T(8,128)(2,1)}, u32[]{:S(2)}, u32[]{:S(2)}) collective-permute-start(bf16[2048,1024]{1,0:T(8,128)(2,1)} %copy.38), channel_id=1, source_target_pairs={{0,16},{16,0},{32,48},{48,32},{64,80},{80,64},{96,112},{112,96},{1... | collective-permute-start | bytes 12582920 | tf_op jit(solution)/shard_map/ppermute | solution.py:50
  145.6 9.0 %collective-permute-start.3 = (bf16[64,8,1024]{2,0,1:T(8,128)(2,1)}, bf16[64,8,1024]{2,0,1:T(8,128)(2,1)}, u32[]{:S(2)}, u32[]{:S(2)}) collective-permute-start(bf16[64,8,1024]{2,0,1:T(8,128)(2,1)} %copy-done.3), channel_id=1, source_target_pairs={{0,16},{16,0},{32,48},{48,32},{64,80},{80,64},{96,112},{112,96},{1... | collective-permute-start | bytes 3145736 | tf_op jit(solution)/shard_map/ppermute | solution.py:100
  147.2 8.9 %collective-permute-start.4 = (bf16[64,8,1024]{2,0,1:T(8,128)(2,1)}, bf16[64,8,1024]{2,0,1:T(8,128)(2,1)}, u32[]{:S(2)}, u32[]{:S(2)}) collective-permute-start(bf16[64,8,1024]{2,0,1:T(8,128)(2,1)} %broadcast_select_fusion), channel_id=1, source_target_pairs={{0,16},{16,0},{32,48},{48,32},{64,80},{80,64},{96,112},{112,96},{1... | collective-permute-start | bytes 3145736 | tf_op jit(solution)/shard_map/ppermute | solution.py:102
  217.5 41.0 %copy-start.5 = (bf16[4,128,1024]{2,1,0:T(8,128)(2,1)S(1)}, bf16[4,128,1024]{2,1,0:T(8,128)(2,1)}, u32[]{:S(2)}) copy-start(bf16[4,128,1024]{2,1,0:T(8,128)(2,1)} %copy-done.4) | copy-start | bytes 3145732
  220.0 38.5 %all-to-all-start.1 = ((bf16[64,8,1024]{2,1,0:T(8,128)(2,1)}), bf16[64,8,1024]{2,1,0:T(8,128)(2,1)}, u32[]{:S(2)}, u32[]{:S(2)}) async-start(bf16[64,8,1024]{2,1,0:T(8,128)(2,1)} %copy.44), calls=%async_computation.1 | async-start | bytes 2097152 | tf_op jit(solution)/shard_map/all_to_all | solution.py:133
  258.5 4.9 %copy-start.1 = (bf16[1024,1024]{1,0:T(8,128)(2,1)S(1)}, bf16[1024,1024]{1,0:T(8,128)(2,1)}, u32[]{:S(2)}) copy-start(bf16[1024,1024]{1,0:T(8,128)(2,1)} %param.10) | copy-start | bytes 6291460
Sparse Core Ops, SparseCore 0:
  9.9 125.4 all-gather.1

commit v9 on v8

--- a/solution.py
+++ b/solution.py
@@ -31,44 +31,48 @@
     return (weights / jnp.sum(weights, axis=-1, keepdims=True)).astype(jnp.bfloat16)
 
 
-def gather_half_by_core(shards, axis_small, axis_pair):
+def gather_half_by_core(w_qkv, w_out, axis_small, axis_pair):
     pair_index = lax.axis_index(axis_pair) % 2
-    halves = [shard.shape[1] // 2 for shard in shards]
-    mine = jnp.concatenate(
+    width = w_out.shape[1]
+    half = width // 2
+    pieces = [
+        lax.dynamic_slice_in_dim(w_qkv, part * width + pair_index * half, half, axis=1).T
+        for part in range(3)
+    ]
+    pieces.append(lax.dynamic_slice_in_dim(w_out, pair_index * half, half, axis=1).T)
+    return lax.all_gather(jnp.concatenate(pieces, axis=0), axis_small, axis=1, tiled=True)
+
+
+def assemble_halves(gathered, axis_pair):
+    pair_index = lax.axis_index(axis_pair) % 2
+    count = lax.axis_size(axis_pair)
+    other = lax.ppermute(gathered, axis_pair, [(i, i ^ 1) for i in range(count)])
+    half = gathered.shape[0] // 4
+    qkv = jnp.stack(
         [
-            lax.dynamic_slice_in_dim(shard, pair_index * half, half, axis=1).T
-            for shard, half in zip(shards, halves)
+            jnp.concatenate(
+                [gathered[part * half:(part + 1) * half], other[part * half:(part + 1) * half]],
+                axis=0,
+            )
+            for part in range(3)
         ],
         axis=0,
     )
-    return lax.all_gather(mine, axis_small, axis=1, tiled=True), halves
-
-
-def swap_halves(gathered, halves, axis_pair):
-    pair_index = lax.axis_index(axis_pair) % 2
-    count = lax.axis_size(axis_pair)
-    other = lax.ppermute(gathered, axis_pair, [(i, i ^ 1) for i in range(count)])
-    results = []
-    start = 0
-    for half in halves:
-        own_part = gathered[start:start + half]
-        other_part = other[start:start + half]
-        start += half
-        results.append(
-            jnp.where(
-                pair_index == 0,
-                jnp.concatenate([own_part, other_part], axis=0),
-                jnp.concatenate([other_part, own_part], axis=0),
-            )
-        )
-    return results
+    own_out = gathered[3 * half:]
+    other_out = other[3 * half:]
+    out = jnp.where(
+        pair_index == 0,
+        jnp.concatenate([own_out, other_out], axis=0),
+        jnp.concatenate([other_out, own_out], axis=0),
+    )
+    return qkv, out
 
 
 def per_device(motion, modulation, w_temporal_qkv, w_temporal_out, w_inter_qkv, w_inter_out, links):
     own_chars, all_frames, feature_width = motion.shape
     head_count = feature_width // HEAD
     scale = HEAD ** (-0.5)
-    gathered, halves = gather_half_by_core((w_inter_qkv, w_inter_out), "tm", "grp")
+    gathered = gather_half_by_core(w_inter_qkv, w_inter_out, "tm", "grp")
 
     normed = modulate(motion, modulation, 0, 1)
     t_w = w_temporal_qkv.reshape(feature_width, 3, head_count, HEAD)
@@ -105,7 +109,7 @@
     ahead_one = jnp.where(pair_index == 0, pair_own, relayed)
     behind_one = jnp.where(pair_index == 0, relayed, pair_own)
     others = [ahead_one, ahead_two, behind_one, behind_two]
-    inter_qkv, inter_out = swap_halves(gathered, halves, "grp")
+    inter_qkv, inter_out = assemble_halves(gathered, "grp")
     char_count, frame_count, unused_width = frames_own.shape
 
     i_w = inter_qkv.reshape(3, head_count, HEAD, feature_width)
@@ -130,6 +134,9 @@
     mixed_heads = jnp.einsum(
         "fhcm,fhmd->cfhd", weights, pairs[1], preferred_element_type=jnp.float32
     ).astype(jnp.bfloat16)
+    mixed_heads = jnp.where(
+        pair_index == 0, mixed_heads, jnp.roll(mixed_heads, head_count // 2, axis=2)
+    )
     mixed_chars = lax.all_to_all(
         mixed_heads.reshape(char_count, frame_count, feature_width),
         "tm",

time: 271 us -> 271 us (level)
  blocking collectives: 42.1 us -> 79.9 us
  waiting for transfers between devices: 90.5 us -> 64.1 us
  starting transfers between devices: 11.4 us -> 3.44 us
  local copies, waits for them, and re-layouts: 36.5 us -> 31.7 us
    all_to_all x0 -> x1, blocking collectives: none -> 37.8 us  [per_device(): lax.all_to_all(mixed_heads.reshape(char_count, frame_count, feature_width...]
    all_to_all x1 -> x0, waiting for transfers between devices: 26 us -> none  [per_device(): lax.all_to_all(mixed_heads.reshape(char_count, frame_count, feature_width...]
    all_to_all x1 -> x0, starting transfers between devices: 7.95 us -> none  [per_device(): lax.all_to_all(mixed_heads.reshape(char_count, frame_count, feature_width...]
    slice x5 -> x3, local copies, waits for them, and re-layouts: 11.7 us -> 7.41 us  [the longest x1 3.6 us: assemble_halves(): gathered[part * half:(part + 1) * half]]
    concatenate x1 -> x4, other arithmetic: 0.72 us -> 3.88 us  [the longest x3 3.16 us: assemble_halves(): jnp.concatenate([gathered[part * half:(part + 1) * half], other[part * ha...]
  transfers between devices with their start and end apart: 7 -> 6, of which waited for: 5 -> 4; matrix products, arithmetic and copies ran while one was open for 16% -> 15% of each run, Pallas kernels for 0% -> 0%
where the time goes in v9:
time: 271 us; the launch traced here: 270 us
  blocking collectives  79.9 us (29%)
  waiting for transfers between devices  64.1 us (24%)
  matrix products  47.3 us (17%)
  local copies, waits for them, and re-layouts  31.7 us (12%)
  other arithmetic  30.2 us (11%)
  between operations  13.5 us (5%)
  starting transfers between devices  3.44 us (1%)
    ppermute x2, waiting for transfers between devices, from_group(): return lax.ppermute(block, axis, route)  59.3 us
    all_to_all x1, blocking collectives, per_device(): lax.all_to_all(normed_inter, 'tm', split_axis=1, concat_axis=0, tiled=True)  42.1 us
    all_to_all x1, blocking collectives, per_device(): lax.all_to_all(mixed_heads.reshape(char_count, frame_count, feature_width...  37.8 us
    sub x2, other arithmetic, softmax_rows(): weights = jnp.exp(scores - row_top)  17.3 us
    dot_general x1, matrix products, per_device(): jnp.einsum('fhcd,fhmd->fhcm', queries, pairs[0], preferred_element_type=j...  13.9 us
    dot_general x1, matrix products, per_device(): jnp.einsum('fhcm,fhmd->cfhd', weights, pairs[1], preferred_element_type=j...  13.3 us
    unnamed x21, local copies, waits for them, and re-layouts  11.4 us
    optimization_barrier x1, local copies, waits for them, and re-layouts, per_device(): lax.optimization_barrier((gathered, ahead_two, behind_two))  6.39 us
  transfers between devices with their start and end apart: 6, of which 4 were waited for; matrix products, arithmetic and copies ran while one was open for 15% of the time, Pallas kernels for 0%

profile of v9, /device:TPU:8, one launch (start us, length us, event | category | flops | bytes accessed | tf_op | source)
XLA Modules:
  0.0 270.2 jit_solution(14494505834269978078)
XLA Ops:
  6.5 0.0 copy-start
  6.5 0.0 all-gather.2.cloned.1.call-start
  6.5 1.1 dynamic-slice_bitcast_fusion.3
  7.6 0.7 pad_maximum_fusion.3
  8.4 0.0 all-gather.2.cloned.1.call-update
  8.4 0.0 copy-start.6
  8.4 0.0 copy-start.7
  8.4 8.7 %copy.35 = bf16[1024,3072]{0,1:T(8,128)(2,1)} copy(bf16[1024,3072]{1,0:T(8,128)(2,1)} %param.9) | data formatting | bytes 12582912 | tf_op args[2]
  17.1 0.0 copy-done.6
  17.1 0.3 fusion.23
  17.4 0.0 copy-done.7
  17.4 5.9 %convert_bitcast_fusion = bf16[3,4,16,128,64]{3,4,2,0,1:T(8,128)(2,1)S(1)} fusion(bf16[1024,3,16,64,1]{0,3,2,1,4:T(8,128)(2,1)} %bitcast.104, bf16[4,128,1024]{2,1,0:T(8,128)(2,1)S(1)} %copy-done.6, f32[1024]{0:T(1024)S(1)} %bitcast.116, f32[1024]{0:T(1024)S(1)} %bitcast.117, f32[4,128]{1,0:T(4,128)S(1)} %add_rsqrt_fusion.1), kind=kOutput, calls=%fused_computation.26 | convolution fusion | flops 3225419776 | bytes 10496000 | tf_op jit(solution)/shard_map/nfk,kshd->snhfd/dot_general | solution.py:79
  23.4 0.0 copy-start.2
  23.4 0.8 fusion.55
  24.1 2.9 %fusion.71 = (f32[4,16,128]{2,1,0:T(8,128)S(1)}, f32[4,16,128,128]{2,3,1,0:T(8,128)}) fusion(f32[4,16,128,128]{2,3,1,0:T(8,128)S(1)} %fusion.55), kind=kOutput, calls=%fused_computation.98 | output fusion | flops 4194431 | bytes 8421376 | tf_op jit(solution)/shard_map/sub | solution.py:30
  27.1 0.0 copy-done.2
  27.1 0.0 copy-done
  27.1 4.8 %fusion.28 = (f32[4,128]{1,0:T(4,128)S(1)}, bf16[4,128,1024]{2,1,0:T(8,128)(2,1)S(1)}) fusion(bf16[16,64,1024,1]{2,1,0,3:T(8,128)(2,1)S(1)} %bitcast.102, f32[4,16,128,128]{2,3,1,0:T(8,128)} %get-tuple-element.33, f32[4,16,128]{2,1,0:T(8,128)S(1)} %get-tuple-element.32, bf16[3,4,16,128,64]{3,4,2,0,1:T(8,128)(2,1)} %copy-done.2, f32[1024]{0:T(1024)S(1)} %bitcast.115, ...), kind=kOutput, calls=%fused_computation.35 | convolution fusion | flops 1214250496 | bytes 9476096 | tf_op jit(solution)/shard_map/nhfd,hdo->nfo/dot_general | solution.py:89
  31.9 0.0 copy-start.4
  31.9 0.4 fusion.31
  32.3 0.8 copy.37
  33.1 42.1 %all_to_all.33 = bf16[4,128,1024]{2,0,1:T(4,128)(2,1)S(1)} all-to-all(bf16[4,128,1024]{2,0,1:T(4,128)(2,1)S(1)} %copy.37), channel_id=1, replica_groups=mesh['grp'=16,'tm'=16] {'tm'}, dimensions={1} | all-to-all | bytes 2097152 | tf_op jit(solution)/shard_map/all_to_all | solution.py:98
  75.2 0.3 copy.70
  75.5 0.0 copy-done.4
  75.5 0.1 copy.39
  75.6 1.6 constant_dynamic-update-slice_fusion.2
  77.2 0.9 collective-permute-start.1
  78.1 2.0 collective-permute-start
  80.2 37.5 %collective-permute-done.1 = bf16[64,8,1024]{2,0,1:T(8,128)(2,1)S(1)} collective-permute-done((bf16[64,8,1024]{2,0,1:T(8,128)(2,1)S(1)}, bf16[64,8,1024]{2,0,1:T(8,128)(2,1)S(1)}, u32[]{:S(2)}, u32[]{:S(2)}) %collective-permute-start.1) | collective-permute-done | bytes 1048608 | tf_op jit(solution)/shard_map/ppermute | solution.py:16
  117.6 0.0 copy-done.3
  117.6 21.8 %collective-permute-done = bf16[64,8,1024]{2,0,1:T(8,128)(2,1)S(1)} collective-permute-done((bf16[64,8,1024]{2,0,1:T(8,128)(2,1)S(1)}, bf16[64,8,1024]{2,0,1:T(8,128)(2,1)S(1)}, u32[]{:S(2)}, u32[]{:S(2)}) %collective-permute-start) | collective-permute-done | bytes 1048608 | tf_op jit(solution)/shard_map/ppermute | solution.py:16
  139.5 6.4 %copy.42 = bf16[2048,1024]{1,0:T(8,128)(2,1)} copy(bf16[2048,1024]{0,1:T(8,128)(2,1)} %all-gather.2.cloned.1.call-done) | data formatting | bytes 8388608 | tf_op jit(solution)/shard_map/optimization_barrier | solution.py:105
  145.9 0.0 collective-permute-start.2
  145.9 0.5 collective-permute-start.3
  146.4 1.1 broadcast_select_fusion
  147.5 0.0 collective-permute-start.4
  147.5 0.0 copy-done.8
  147.5 0.2 dynamic-slice_reduce_fusion
  147.7 0.1 add_compare_fusion
  147.8 0.1 broadcast_in_dim.8
  147.9 0.1 gt.12
  148.0 3.6 %fusion.67 = (bf16[512,1024]{1,0:T(8,128)(2,1)S(1)}, bf16[512,1024]{1,0:T(8,128)(2,1)}, bf16[512,1024]{1,0:T(8,128)(2,1)S(1)}, bf16[512,1024]{1,0:T(8,128)(2,1)S(1)}) fusion(bf16[2048,1024]{1,0:T(8,128)(2,1)} %copy.42), kind=kLoop, calls=%fused_computation.94 | loop fusion | bytes 8388608 | tf_op jit(solution)/shard_map/slice | solution.py:54
  151.6 3.3 %collective-permute-done.3 = bf16[64,8,1024]{2,0,1:T(8,128)(2,1)} collective-permute-done((bf16[64,8,1024]{2,0,1:T(8,128)(2,1)}, bf16[64,8,1024]{2,0,1:T(8,128)(2,1)}, u32[]{:S(2)}, u32[]{:S(2)}) %collective-permute-start.3) | collective-permute-done | bytes 1048608 | tf_op jit(solution)/shard_map/ppermute | solution.py:104
  154.9 1.5 collective-permute-done.4
  156.4 2.6 select_dynamic-update-slice_fusion.1
  159.0 1.1 constant_dynamic-update-slice_fusion.1
  160.1 2.6 select_dynamic-update-slice_fusion
  162.7 1.1 constant_dynamic-update-slice_fusion
  163.8 0.0 collective-permute-done.2
  163.8 3.6 %fusion.68 = (bf16[512,1024]{1,0:T(8,128)(2,1)S(1)}, bf16[512,1024]{1,0:T(8,128)(2,1)}, bf16[512,1024]{1,0:T(8,128)(2,1)S(1)}, bf16[512,1024]{1,0:T(8,128)(2,1)S(1)}) fusion(bf16[2048,1024]{1,0:T(8,128)(2,1)} %collective-permute-done.2), kind=kLoop, calls=%fused_computation.95 | loop fusion | bytes 8388608 | tf_op jit(solution)/shard_map/slice | solution.py:54
  167.4 1.5 pad_maximum_fusion
  168.9 1.5 pad_maximum_fusion.2
  170.4 0.2 pad_maximum_fusion.1
  170.6 4.0 %fusion.57 = bf16[16,64,64,8]{2,1,0,3:T(8,128)(2,1)} fusion(bf16[16,64,1024,1]{2,1,0,3:T(8,128)(2,1)S(1)} %bitcast.110, bf16[64,8,1024,1]{2,1,0,3:T(8,128)(2,1)S(1)} %bitcast.106), kind=kOutput, calls=%fused_computation.66 | convolution fusion | flops 1073741824 | bytes 4194304 | tf_op jit(solution)/shard_map/cfk,hdk->fhcd/dot_general | solution.py:116
  174.6 13.9 %fusion.3 = f32[8,16,64,320]{3,2,1,0:T(8,128)} fusion(bf16[16,64,1024,1]{2,1,0,3:T(8,128)(2,1)} %bitcast.109, bf16[320,8,1024]{2,0,1:T(8,128)(2,1)} %constant_dynamic-update-slice_fusion, bf16[16,64,64,8]{2,1,0,3:T(8,128)(2,1)} %fusion.57), kind=kOutput, calls=%fused_computation.6 | convolution fusion | flops 5706874880 | bytes 18874368 | tf_op jit(solution)/shard_map/fhcd,fhmd->fhcm/dot_general | solution.py:126
  188.5 14.4 %fusion.72 = (f32[8,16,64]{2,1,0:T(8,128)S(1)}, f32[8,16,64,320]{3,2,1,0:T(8,128)}) fusion(f32[8,16,64,320]{3,2,1,0:T(8,128)} %fusion.3, pred[320]{0:T(512)(128)(4,1)S(1)} %gt.12), kind=kOutput, calls=%fused_computation.99 | output fusion | flops 15728959 | bytes 21004608 | tf_op jit(solution)/shard_map/sub | solution.py:30
  202.9 13.3 %convert_bitcast_fusion.1 = bf16[64,8,16,64]{0,3,2,1:T(8,128)(2,1)S(1)} fusion(f32[8,16,64,320]{3,2,1,0:T(8,128)} %get-tuple-element.37, f32[8,16,64]{2,1,0:T(8,128)S(1)} %get-tuple-element.36, bf16[16,64,1024,1]{2,1,0,3:T(8,128)(2,1)} %bitcast.108, bf16[320,8,1024]{2,0,1:T(8,128)(2,1)} %constant_dynamic-update-slice_fusion), kind=kOutput, calls=%fused_computation.54 | convolution fusion | flops 5712642048 | bytes 18907136 | tf_op jit(solution)/shard_map/fhcm,fhmd->cfhd/dot_general | solution.py:134
  216.2 0.2 fusion.69
  216.4 1.8 maximum_select_fusion
  218.2 2.8 %copy.50 = bf16[64,8,1024]{2,1,0:T(8,128)(2,1)S(1)} copy(bf16[64,8,1024]{0,2,1:T(8,128)(2,1)} %bitcast.103) | data formatting | bytes 2097152 | tf_op jit(solution)/shard_map/reshape | solution.py:141
  221.0 37.8 %all_to_all.34 = bf16[64,8,1024]{2,1,0:T(8,128)(2,1)S(1)} all-to-all(bf16[64,8,1024]{2,1,0:T(8,128)(2,1)S(1)} %copy.50), channel_id=1, replica_groups=mesh['grp'=16,'tm'=16] {'tm'}, dimensions={0} | all-to-all | bytes 2097152 | tf_op jit(solution)/shard_map/all_to_all | solution.py:140
  258.8 0.0 copy-done.5
  258.8 4.6 %fusion.32 = bf16[4,128,1024]{2,1,0:T(8,128)(2,1)} fusion(bf16[4,128,1024]{2,1,0:T(8,128)(2,1)S(1)} %copy-done.5, bf16[512,1024]{1,0:T(8,128)(2,1)} %get-tuple-element.16, bf16[512,1024]{1,0:T(8,128)(2,1)} %get-tuple-element.12, pred[]{:T(512)S(6)} %eq.6, bf16[4,16,8,1024]{3,2,0,1:T(8,128)(2,1)S(1)} %bitcast.111, f32[1024]{0:T(1024)S(1)} %bitcast.114), kind=kOutput, calls=%fused_computation.39 | convolution fusion | flops 1085276160 | bytes 5246977 | tf_op jit(solution)/shard_map/tk,ok->to/dot_general | solution.py:147
  263.4 0.0 copy-done.1
  (8 shorter events, 0.0 us)
Async XLA Ops:
  6.5 20.5 %copy-start = (bf16[1024,1024]{1,0:T(8,128)(2,1)S(1)}, bf16[1024,1024]{1,0:T(8,128)(2,1)}, u32[]{:S(2)}) copy-start(bf16[1024,1024]{1,0:T(8,128)(2,1)} %param.10) | copy-start | bytes 6291460
  6.5 132.9 %all-gather.2.cloned.1.call-start = ((), (), s32[]{:S(2)}) async-start(), calls=%async_computation.2 | async-start | bytes 4456448 | tf_op jit(solution)/shard_map/all_gather | solution.py:43
  8.4 8.7 %copy-start.6 = (bf16[4,128,1024]{2,1,0:T(8,128)(2,1)S(1)}, bf16[4,128,1024]{2,1,0:T(8,128)(2,1)}, u32[]{:S(2)}) copy-start(bf16[4,128,1024]{2,1,0:T(8,128)(2,1)} %param.7) | copy-start | bytes 3145732
  8.4 9.0 %copy-start.7 = (f32[6,1024]{1,0:T(8,128)S(1)}, f32[6,1024]{1,0:T(8,128)}, u32[]{:S(2)}) copy-start(f32[6,1024]{1,0:T(8,128)} %param.8) | copy-start | bytes 73732
  23.4 3.7 %copy-start.2 = (bf16[3,4,16,128,64]{3,4,2,0,1:T(8,128)(2,1)}, bf16[3,4,16,128,64]{3,4,2,0,1:T(8,128)(2,1)S(1)}, u32[]{:S(2)}) copy-start(bf16[3,4,16,128,64]{3,4,2,0,1:T(8,128)(2,1)S(1)} %convert_bitcast_fusion) | copy-start | bytes 9437188
  31.9 43.7 %copy-start.4 = (bf16[4,128,1024]{2,1,0:T(8,128)(2,1)}, bf16[4,128,1024]{2,1,0:T(8,128)(2,1)S(1)}, u32[]{:S(2)}) copy-start(bf16[4,128,1024]{2,1,0:T(8,128)(2,1)S(1)} %get-tuple-element.35) | copy-start | bytes 3145732
  77.2 40.4 %copy-start.3 = (bf16[64,8,1024]{2,0,1:T(8,128)(2,1)}, bf16[64,8,1024]{2,0,1:T(8,128)(2,1)S(1)}, u32[]{:S(2)}) copy-start(bf16[64,8,1024]{2,0,1:T(8,128)(2,1)S(1)} %get-tuple-element.22) | copy-start | bytes 3145732
  77.2 70.3 %copy-start.8 = (s32[16,4]{0,1:T(4,128)S(1)}, s32[16,4]{0,1:T(4,128)}, u32[]{:S(2)}) copy-start(s32[16,4]{0,1:T(4,128)} %param.13) | copy-start | bytes 772
  77.2 40.4 %collective-permute-start.1 = (bf16[64,8,1024]{2,0,1:T(8,128)(2,1)S(1)}, bf16[64,8,1024]{2,0,1:T(8,128)(2,1)S(1)}, u32[]{:S(2)}, u32[]{:S(2)}) collective-permute-start(bf16[64,8,1024]{2,0,1:T(8,128)(2,1)S(1)} %get-tuple-element.22), channel_id=1, source_target_pairs={{224,0},{240,16},{0,32},{16,48},{32,64},{48,80},{64,96},{80,112},{... | collective-permute-start | bytes 3145736 | tf_op jit(solution)/shard_map/ppermute | solution.py:16
  78.1 61.3 %collective-permute-start = (bf16[64,8,1024]{2,0,1:T(8,128)(2,1)S(1)}, bf16[64,8,1024]{2,0,1:T(8,128)(2,1)S(1)}, u32[]{:S(2)}, u32[]{:S(2)}) collective-permute-start(bf16[64,8,1024]{2,0,1:T(8,128)(2,1)S(1)} %get-tuple-element.22), channel_id=1, source_target_pairs={{32,0},{48,16},{64,32},{80,48},{96,64},{112,80},{128,96},{144,112}... | collective-permute-start | bytes 3145736 | tf_op jit(solution)/shard_map/ppermute | solution.py:16
  145.9 17.9 %collective-permute-start.2 = (bf16[2048,1024]{1,0:T(8,128)(2,1)}, bf16[2048,1024]{1,0:T(8,128)(2,1)}, u32[]{:S(2)}, u32[]{:S(2)}) collective-permute-start(bf16[2048,1024]{1,0:T(8,128)(2,1)} %copy.42), channel_id=1, source_target_pairs={{0,16},{16,0},{32,48},{48,32},{64,80},{80,64},{96,112},{112,96},{1... | collective-permute-start | bytes 12582920 | tf_op jit(solution)/shard_map/ppermute | solution.py:49
  145.9 9.0 %collective-permute-start.3 = (bf16[64,8,1024]{2,0,1:T(8,128)(2,1)}, bf16[64,8,1024]{2,0,1:T(8,128)(2,1)}, u32[]{:S(2)}, u32[]{:S(2)}) collective-permute-start(bf16[64,8,1024]{2,0,1:T(8,128)(2,1)} %copy-done.3), channel_id=1, source_target_pairs={{0,16},{16,0},{32,48},{48,32},{64,80},{80,64},{96,112},{112,96},{1... | collective-permute-start | bytes 3145736 | tf_op jit(solution)/shard_map/ppermute | solution.py:104
  147.5 8.8 %collective-permute-start.4 = (bf16[64,8,1024]{2,0,1:T(8,128)(2,1)}, bf16[64,8,1024]{2,0,1:T(8,128)(2,1)}, u32[]{:S(2)}, u32[]{:S(2)}) collective-permute-start(bf16[64,8,1024]{2,0,1:T(8,128)(2,1)} %broadcast_select_fusion), channel_id=1, source_target_pairs={{0,16},{16,0},{32,48},{48,32},{64,80},{80,64},{96,112},{112,96},{1... | collective-permute-start | bytes 3145736 | tf_op jit(solution)/shard_map/ppermute | solution.py:106
  218.2 40.5 %copy-start.5 = (bf16[4,128,1024]{2,1,0:T(8,128)(2,1)S(1)}, bf16[4,128,1024]{2,1,0:T(8,128)(2,1)}, u32[]{:S(2)}) copy-start(bf16[4,128,1024]{2,1,0:T(8,128)(2,1)} %copy-done.4) | copy-start | bytes 3145732
  258.8 4.6 %copy-start.1 = (bf16[1024,1024]{1,0:T(8,128)(2,1)S(1)}, bf16[1024,1024]{1,0:T(8,128)(2,1)}, u32[]{:S(2)}) copy-start(bf16[1024,1024]{1,0:T(8,128)(2,1)} %param.10) | copy-start | bytes 6291460
Sparse Core Ops, SparseCore 0:
  9.9 124.7 all-gather.1

commit v10 on v9

--- a/solution.py
+++ b/solution.py
@@ -102,7 +102,9 @@
     ahead_two = from_group(frames_own, "grp", 2)
     behind_two = from_group(frames_own, "grp", -2)
     pair_own = lax.ppermute(frames_own, "grp", pair_route)
-    gathered, ahead_two, behind_two = lax.optimization_barrier((gathered, ahead_two, behind_two))
+    gathered, ahead_two, behind_two, pair_own = lax.optimization_barrier(
+        (gathered, ahead_two, behind_two, pair_own)
+    )
     relayed = lax.ppermute(
         jnp.where(pair_index == 0, ahead_two, behind_two), "grp", pair_route
     )

time: 271 us -> 269 us (level)
    ppermute x1, waiting for transfers between devices: 3.3 us -> 0.01 us  [per_device(): pair_own = lax.ppermute(frames_own, 'grp', pair_route)]
    unnamed x21 -> x19, local copies, waits for them, and re-layouts: 11.4 us -> 12.6 us
  transfers between devices with their start and end apart: 6 -> 6, of which waited for: 4 -> 3; matrix products, arithmetic and copies ran while one was open for 15% -> 15% of each run, Pallas kernels for 0% -> 0%
where the time goes in v10:
time: 269 us
  blocking collectives  79.9 us (30%)
  waiting for transfers between devices  62 us (23%)
  matrix products  47.3 us (18%)
  local copies, waits for them, and re-layouts  32.9 us (12%)
  other arithmetic  30.3 us (11%)
  between operations  13.5 us (5%)
  starting transfers between devices  2.94 us (1%)
    ppermute x2, waiting for transfers between devices, from_group(): return lax.ppermute(block, axis, route)  59.4 us
    all_to_all x1, blocking collectives, per_device(): lax.all_to_all(normed_inter, 'tm', split_axis=1, concat_axis=0, tiled=True)  42.1 us
    all_to_all x1, blocking collectives, per_device(): lax.all_to_all(mixed_heads.reshape(char_count, frame_count, feature_width...  37.8 us
    sub x2, other arithmetic, softmax_rows(): weights = jnp.exp(scores - row_top)  17.4 us
    dot_general x1, matrix products, per_device(): jnp.einsum('fhcd,fhmd->fhcm', queries, pairs[0], preferred_element_type=j...  13.9 us
    dot_general x1, matrix products, per_device(): jnp.einsum('fhcm,fhmd->cfhd', weights, pairs[1], preferred_element_type=j...  13.3 us
    unnamed x19, local copies, waits for them, and re-layouts  12.6 us
    optimization_barrier x1, local copies, waits for them, and re-layouts, per_device(): lax.optimization_barrier((gathered, ahead_two, behind_two, pair_own))  6.39 us
  transfers between devices with their start and end apart: 6, of which 3 were waited for; matrix products, arithmetic and copies ran while one was open for 15% of the time, Pallas kernels for 0%

profile of v10, /device:TPU:8, one launch (start us, length us, event | category | flops | bytes accessed | tf_op | source)
XLA Modules:
  0.0 268.9 jit_solution(17767761403840563705)
XLA Ops:
  6.5 0.0 copy-start
  6.5 0.0 all-gather.2.cloned.1.call-start
  6.5 1.1 dynamic-slice_bitcast_fusion.3
  7.6 0.7 pad_maximum_fusion.3
  8.4 0.0 all-gather.2.cloned.1.call-update
  8.4 0.0 copy-start.5
  8.4 0.0 copy-start.6
  8.4 8.7 %copy.35 = bf16[1024,3072]{0,1:T(8,128)(2,1)} copy(bf16[1024,3072]{1,0:T(8,128)(2,1)} %param.9) | data formatting | bytes 12582912 | tf_op args[2]
  17.1 0.0 copy-done.5
  17.1 0.3 fusion.23
  17.4 0.0 copy-done.6
  17.5 5.9 %convert_bitcast_fusion = bf16[3,4,16,128,64]{3,4,2,0,1:T(8,128)(2,1)S(1)} fusion(bf16[1024,3,16,64,1]{0,3,2,1,4:T(8,128)(2,1)} %bitcast.104, bf16[4,128,1024]{2,1,0:T(8,128)(2,1)S(1)} %copy-done.5, f32[1024]{0:T(1024)S(1)} %bitcast.116, f32[1024]{0:T(1024)S(1)} %bitcast.117, f32[4,128]{1,0:T(4,128)S(1)} %add_rsqrt_fusion.1), kind=kOutput, calls=%fused_computation.26 | convolution fusion | flops 3225419776 | bytes 10496000 | tf_op jit(solution)/shard_map/nfk,kshd->snhfd/dot_general | solution.py:79
  23.4 0.0 copy-start.2
  23.4 0.8 fusion.55
  24.2 2.9 %fusion.71 = (f32[4,16,128]{2,1,0:T(8,128)S(1)}, f32[4,16,128,128]{2,3,1,0:T(8,128)}) fusion(f32[4,16,128,128]{2,3,1,0:T(8,128)S(1)} %fusion.55), kind=kOutput, calls=%fused_computation.98 | output fusion | flops 4194431 | bytes 8421376 | tf_op jit(solution)/shard_map/sub | solution.py:30
  27.1 0.0 copy-done.2
  27.1 0.0 copy-done
  27.1 4.8 %fusion.28 = (f32[4,128]{1,0:T(4,128)S(1)}, bf16[4,128,1024]{2,1,0:T(8,128)(2,1)S(1)}) fusion(bf16[16,64,1024,1]{2,1,0,3:T(8,128)(2,1)S(1)} %bitcast.102, f32[4,16,128,128]{2,3,1,0:T(8,128)} %get-tuple-element.35, f32[4,16,128]{2,1,0:T(8,128)S(1)} %get-tuple-element.34, bf16[3,4,16,128,64]{3,4,2,0,1:T(8,128)(2,1)} %copy-done.2, f32[1024]{0:T(1024)S(1)} %bitcast.115, ...), kind=kOutput, calls=%fused_computation.35 | convolution fusion | flops 1214250496 | bytes 9476096 | tf_op jit(solution)/shard_map/nhfd,hdo->nfo/dot_general | solution.py:89
  31.9 0.0 copy-start.3
  31.9 0.4 fusion.31
  32.3 0.8 copy.37
  33.1 42.1 %all_to_all.33 = bf16[4,128,1024]{2,0,1:T(4,128)(2,1)S(1)} all-to-all(bf16[4,128,1024]{2,0,1:T(4,128)(2,1)S(1)} %copy.37), channel_id=1, replica_groups=mesh['grp'=16,'tm'=16] {'tm'}, dimensions={1} | all-to-all | bytes 2097152 | tf_op jit(solution)/shard_map/all_to_all | solution.py:98
  75.2 0.3 copy.70
  75.5 0.0 copy-done.3
  75.5 0.1 copy.39
  75.6 1.6 constant_dynamic-update-slice_fusion.2
  77.2 0.0 copy-start.7
  77.2 0.0 collective-permute-start.2
  77.2 0.9 collective-permute-start.1
  78.1 2.0 collective-permute-start
  80.2 0.0 collective-permute-done.2
  80.2 36.9 %collective-permute-done.1 = bf16[64,8,1024]{2,0,1:T(8,128)(2,1)S(1)} collective-permute-done((bf16[64,8,1024]{2,0,1:T(8,128)(2,1)S(1)}, bf16[64,8,1024]{2,0,1:T(8,128)(2,1)S(1)}, u32[]{:S(2)}, u32[]{:S(2)}) %collective-permute-start.1) | collective-permute-done | bytes 1048608 | tf_op jit(solution)/shard_map/ppermute | solution.py:16
  117.1 22.5 %collective-permute-done = bf16[64,8,1024]{2,0,1:T(8,128)(2,1)} collective-permute-done((bf16[64,8,1024]{2,0,1:T(8,128)(2,1)S(1)}, bf16[64,8,1024]{2,0,1:T(8,128)(2,1)}, u32[]{:S(2)}, u32[]{:S(2)}) %collective-permute-start) | collective-permute-done | bytes 1048608 | tf_op jit(solution)/shard_map/ppermute | solution.py:16
  139.6 6.4 %copy.43 = bf16[2048,1024]{1,0:T(8,128)(2,1)} copy(bf16[2048,1024]{0,1:T(8,128)(2,1)} %all-gather.2.cloned.1.call-done) | data formatting | bytes 8388608 | tf_op jit(solution)/shard_map/optimization_barrier | solution.py:105
  146.0 0.0 collective-permute-start.3
  146.0 2.4 broadcast_select_fusion
  148.3 0.0 collective-permute-start.4
  148.3 0.0 copy-done.7
  148.3 0.2 dynamic-slice_reduce_fusion
  148.5 0.1 add_compare_fusion
  148.6 0.1 broadcast_in_dim.8
  148.7 0.1 gt.12
  148.8 3.6 %fusion.67 = (bf16[512,1024]{1,0:T(8,128)(2,1)S(1)}, bf16[512,1024]{1,0:T(8,128)(2,1)}, bf16[512,1024]{1,0:T(8,128)(2,1)S(1)}, bf16[512,1024]{1,0:T(8,128)(2,1)S(1)}) fusion(bf16[2048,1024]{1,0:T(8,128)(2,1)} %copy.43), kind=kLoop, calls=%fused_computation.94 | loop fusion | bytes 8388608 | tf_op jit(solution)/shard_map/slice | solution.py:54
  152.4 2.6 collective-permute-done.4
  155.0 1.5 select_dynamic-update-slice_fusion.1
  156.4 2.3 constant_dynamic-update-slice_fusion.1
  158.7 2.6 select_dynamic-update-slice_fusion
  161.3 1.1 constant_dynamic-update-slice_fusion
  162.4 0.0 collective-permute-done.3
  162.4 3.6 %fusion.68 = (bf16[512,1024]{1,0:T(8,128)(2,1)S(1)}, bf16[512,1024]{1,0:T(8,128)(2,1)}, bf16[512,1024]{1,0:T(8,128)(2,1)S(1)}, bf16[512,1024]{1,0:T(8,128)(2,1)S(1)}) fusion(bf16[2048,1024]{1,0:T(8,128)(2,1)} %collective-permute-done.3), kind=kLoop, calls=%fused_computation.95 | loop fusion | bytes 8388608 | tf_op jit(solution)/shard_map/slice | solution.py:54
  166.0 1.5 pad_maximum_fusion
  167.5 1.5 pad_maximum_fusion.2
  169.0 0.2 pad_maximum_fusion.1
  169.1 4.0 %fusion.57 = bf16[16,64,64,8]{2,1,0,3:T(8,128)(2,1)} fusion(bf16[16,64,1024,1]{2,1,0,3:T(8,128)(2,1)S(1)} %bitcast.110, bf16[64,8,1024,1]{2,1,0,3:T(8,128)(2,1)S(1)} %bitcast.106), kind=kOutput, calls=%fused_computation.66 | convolution fusion | flops 1073741824 | bytes 4194304 | tf_op jit(solution)/shard_map/cfk,hdk->fhcd/dot_general | solution.py:118
  173.2 13.9 %fusion.3 = f32[8,16,64,320]{3,2,1,0:T(8,128)} fusion(bf16[16,64,1024,1]{2,1,0,3:T(8,128)(2,1)} %bitcast.109, bf16[320,8,1024]{2,0,1:T(8,128)(2,1)} %constant_dynamic-update-slice_fusion, bf16[16,64,64,8]{2,1,0,3:T(8,128)(2,1)} %fusion.57), kind=kOutput, calls=%fused_computation.6 | convolution fusion | flops 5706874880 | bytes 18874368 | tf_op jit(solution)/shard_map/fhcd,fhmd->fhcm/dot_general | solution.py:128
  187.1 14.4 %fusion.72 = (f32[8,16,64]{2,1,0:T(8,128)S(1)}, f32[8,16,64,320]{3,2,1,0:T(8,128)}) fusion(f32[8,16,64,320]{3,2,1,0:T(8,128)} %fusion.3, pred[320]{0:T(512)(128)(4,1)S(1)} %gt.12), kind=kOutput, calls=%fused_computation.99 | output fusion | flops 15728959 | bytes 21004608 | tf_op jit(solution)/shard_map/sub | solution.py:30
  201.5 13.3 %convert_bitcast_fusion.1 = bf16[64,8,16,64]{0,3,2,1:T(8,128)(2,1)S(1)} fusion(f32[8,16,64,320]{3,2,1,0:T(8,128)} %get-tuple-element.39, f32[8,16,64]{2,1,0:T(8,128)S(1)} %get-tuple-element.38, bf16[16,64,1024,1]{2,1,0,3:T(8,128)(2,1)} %bitcast.108, bf16[320,8,1024]{2,0,1:T(8,128)(2,1)} %constant_dynamic-update-slice_fusion), kind=kOutput, calls=%fused_computation.54 | convolution fusion | flops 5712642048 | bytes 18907136 | tf_op jit(solution)/shard_map/fhcm,fhmd->cfhd/dot_general | solution.py:136
  214.8 0.2 fusion.69
  215.1 1.8 maximum_select_fusion
  216.9 2.8 %copy.50 = bf16[64,8,1024]{2,1,0:T(8,128)(2,1)S(1)} copy(bf16[64,8,1024]{0,2,1:T(8,128)(2,1)} %bitcast.103) | data formatting | bytes 2097152 | tf_op jit(solution)/shard_map/reshape | solution.py:143
  219.6 37.8 %all_to_all.34 = bf16[64,8,1024]{2,1,0:T(8,128)(2,1)S(1)} all-to-all(bf16[64,8,1024]{2,1,0:T(8,128)(2,1)S(1)} %copy.50), channel_id=1, replica_groups=mesh['grp'=16,'tm'=16] {'tm'}, dimensions={0} | all-to-all | bytes 2097152 | tf_op jit(solution)/shard_map/all_to_all | solution.py:142
  257.4 0.0 copy-done.4
  257.4 4.6 %fusion.32 = bf16[4,128,1024]{2,1,0:T(8,128)(2,1)} fusion(bf16[4,128,1024]{2,1,0:T(8,128)(2,1)S(1)} %copy-done.4, bf16[512,1024]{1,0:T(8,128)(2,1)} %get-tuple-element.18, bf16[512,1024]{1,0:T(8,128)(2,1)} %get-tuple-element.14, pred[]{:T(512)S(6)} %eq.6, bf16[4,16,8,1024]{3,2,0,1:T(8,128)(2,1)S(1)} %bitcast.111, f32[1024]{0:T(1024)S(1)} %bitcast.114), kind=kOutput, calls=%fused_computation.39 | convolution fusion | flops 1085276160 | bytes 5246977 | tf_op jit(solution)/shard_map/tk,ok->to/dot_general | solution.py:149
  262.0 0.0 copy-done.1
  (6 shorter events, 0.0 us)
Async XLA Ops:
  6.5 20.6 %copy-start = (bf16[1024,1024]{1,0:T(8,128)(2,1)S(1)}, bf16[1024,1024]{1,0:T(8,128)(2,1)}, u32[]{:S(2)}) copy-start(bf16[1024,1024]{1,0:T(8,128)(2,1)} %param.10) | copy-start | bytes 6291460
  6.5 133.0 %all-gather.2.cloned.1.call-start = ((), (), s32[]{:S(2)}) async-start(), calls=%async_computation.2 | async-start | bytes 4456448 | tf_op jit(solution)/shard_map/all_gather | solution.py:43
  8.4 8.8 %copy-start.5 = (bf16[4,128,1024]{2,1,0:T(8,128)(2,1)S(1)}, bf16[4,128,1024]{2,1,0:T(8,128)(2,1)}, u32[]{:S(2)}) copy-start(bf16[4,128,1024]{2,1,0:T(8,128)(2,1)} %param.7) | copy-start | bytes 3145732
  8.4 9.0 %copy-start.6 = (f32[6,1024]{1,0:T(8,128)S(1)}, f32[6,1024]{1,0:T(8,128)}, u32[]{:S(2)}) copy-start(f32[6,1024]{1,0:T(8,128)} %param.8) | copy-start | bytes 73732
  23.4 3.7 %copy-start.2 = (bf16[3,4,16,128,64]{3,4,2,0,1:T(8,128)(2,1)}, bf16[3,4,16,128,64]{3,4,2,0,1:T(8,128)(2,1)S(1)}, u32[]{:S(2)}) copy-start(bf16[3,4,16,128,64]{3,4,2,0,1:T(8,128)(2,1)S(1)} %convert_bitcast_fusion) | copy-start | bytes 9437188
  31.9 43.6 %copy-start.3 = (bf16[4,128,1024]{2,1,0:T(8,128)(2,1)}, bf16[4,128,1024]{2,1,0:T(8,128)(2,1)S(1)}, u32[]{:S(2)}) copy-start(bf16[4,128,1024]{2,1,0:T(8,128)(2,1)S(1)} %get-tuple-element.37) | copy-start | bytes 3145732
  77.2 71.1 %copy-start.7 = (s32[16,4]{0,1:T(4,128)S(1)}, s32[16,4]{0,1:T(4,128)}, u32[]{:S(2)}) copy-start(s32[16,4]{0,1:T(4,128)} %param.13) | copy-start | bytes 772
  77.2 2.9 %collective-permute-start.2 = (bf16[64,8,1024]{2,0,1:T(8,128)(2,1)S(1)}, bf16[64,8,1024]{2,0,1:T(8,128)(2,1)S(1)}, u32[]{:S(2)}, u32[]{:S(2)}) collective-permute-start(bf16[64,8,1024]{2,0,1:T(8,128)(2,1)S(1)} %get-tuple-element.24), channel_id=1, source_target_pairs={{0,16},{16,0},{32,48},{48,32},{64,80},{80,64},{96,112},{112,96},{1... | collective-permute-start | bytes 3145736 | tf_op jit(solution)/shard_map/ppermute | solution.py:104
  77.2 39.8 %collective-permute-start.1 = (bf16[64,8,1024]{2,0,1:T(8,128)(2,1)S(1)}, bf16[64,8,1024]{2,0,1:T(8,128)(2,1)S(1)}, u32[]{:S(2)}, u32[]{:S(2)}) collective-permute-start(bf16[64,8,1024]{2,0,1:T(8,128)(2,1)S(1)} %get-tuple-element.24), channel_id=1, source_target_pairs={{224,0},{240,16},{0,32},{16,48},{32,64},{48,80},{64,96},{80,112},{... | collective-permute-start | bytes 3145736 | tf_op jit(solution)/shard_map/ppermute | solution.py:16
  78.1 61.5 %collective-permute-start = (bf16[64,8,1024]{2,0,1:T(8,128)(2,1)S(1)}, bf16[64,8,1024]{2,0,1:T(8,128)(2,1)}, u32[]{:S(2)}, u32[]{:S(2)}) collective-permute-start(bf16[64,8,1024]{2,0,1:T(8,128)(2,1)S(1)} %get-tuple-element.24), channel_id=1, source_target_pairs={{32,0},{48,16},{64,32},{80,48},{96,64},{112,80},{128,96},{144,112}... | collective-permute-start | bytes 3145736 | tf_op jit(solution)/shard_map/ppermute | solution.py:16
  146.0 16.4 %collective-permute-start.3 = (bf16[2048,1024]{1,0:T(8,128)(2,1)}, bf16[2048,1024]{1,0:T(8,128)(2,1)}, u32[]{:S(2)}, u32[]{:S(2)}) collective-permute-start(bf16[2048,1024]{1,0:T(8,128)(2,1)} %copy.43), channel_id=1, source_target_pairs={{0,16},{16,0},{32,48},{48,32},{64,80},{80,64},{96,112},{112,96},{1... | collective-permute-start | bytes 12582920 | tf_op jit(solution)/shard_map/ppermute | solution.py:49
  148.3 6.6 %collective-permute-start.4 = (bf16[64,8,1024]{2,0,1:T(8,128)(2,1)}, bf16[64,8,1024]{2,0,1:T(8,128)(2,1)}, u32[]{:S(2)}, u32[]{:S(2)}) collective-permute-start(bf16[64,8,1024]{2,0,1:T(8,128)(2,1)} %broadcast_select_fusion), channel_id=1, source_target_pairs={{0,16},{16,0},{32,48},{48,32},{64,80},{80,64},{96,112},{112,96},{1... | collective-permute-start | bytes 3145736 | tf_op jit(solution)/shard_map/ppermute | solution.py:108
  216.9 40.6 %copy-start.4 = (bf16[4,128,1024]{2,1,0:T(8,128)(2,1)S(1)}, bf16[4,128,1024]{2,1,0:T(8,128)(2,1)}, u32[]{:S(2)}) copy-start(bf16[4,128,1024]{2,1,0:T(8,128)(2,1)} %copy-done.3) | copy-start | bytes 3145732
  257.4 4.6 %copy-start.1 = (bf16[1024,1024]{1,0:T(8,128)(2,1)S(1)}, bf16[1024,1024]{1,0:T(8,128)(2,1)}, u32[]{:S(2)}) copy-start(bf16[1024,1024]{1,0:T(8,128)(2,1)} %param.10) | copy-start | bytes 6291460
Sparse Core Ops, SparseCore 0:
  9.9 124.3 all-gather.1

commit v11 on v10

--- a/solution.py
+++ b/solution.py
@@ -108,9 +108,7 @@
     relayed = lax.ppermute(
         jnp.where(pair_index == 0, ahead_two, behind_two), "grp", pair_route
     )
-    ahead_one = jnp.where(pair_index == 0, pair_own, relayed)
-    behind_one = jnp.where(pair_index == 0, relayed, pair_own)
-    others = [ahead_one, ahead_two, behind_one, behind_two]
+    others = [pair_own, ahead_two, relayed, behind_two]
     inter_qkv, inter_out = assemble_halves(gathered, "grp")
     char_count, frame_count, unused_width = frames_own.shape
 
@@ -129,6 +127,7 @@
         "fhcd,fhmd->fhcm", queries, pairs[0], preferred_element_type=jnp.float32
     ) * scale
     own_links = lax.dynamic_index_in_dim(links, lax.axis_index("grp"), axis=0, keepdims=False)
+    own_links = jnp.where(pair_index == 0, own_links, own_links[jnp.array([2, 1, 0, 3])])
     allowed = jnp.concatenate([jnp.ones((1,), jnp.int32), own_links])
     key_mask = jnp.repeat(allowed, char_count) > 0
     scores = jnp.where(key_mask, scores, -jnp.inf)

time: 269 us -> 267 us (level)
  other arithmetic: 30.3 us -> 26.9 us
  local copies, waits for them, and re-layouts: 32.9 us -> 35.9 us
    unnamed x2 -> x0, other arithmetic: 4.1 us -> none
    unnamed x19 -> x24, local copies, waits for them, and re-layouts: 12.6 us -> 14.9 us
  transfers between devices with their start and end apart: 6 -> 6, of which waited for: 3 -> 2; matrix products, arithmetic and copies ran while one was open for 15% -> 15% of each run, Pallas kernels for 0% -> 0%
where the time goes in v11:
time: 267 us; the launch traced here: 266 us
  blocking collectives  79.8 us (30%)
  waiting for transfers between devices  59.4 us (22%)
  matrix products  47.1 us (18%)
  local copies, waits for them, and re-layouts  35.9 us (13%)
  other arithmetic  26.9 us (10%)
  between operations  13.6 us (5%)
  starting transfers between devices  3.42 us (1%)
    ppermute x2, waiting for transfers between devices, from_group(): return lax.ppermute(block, axis, route)  59.4 us
    all_to_all x1, blocking collectives, per_device(): lax.all_to_all(normed_inter, 'tm', split_axis=1, concat_axis=0, tiled=True)  42.1 us
    all_to_all x1, blocking collectives, per_device(): lax.all_to_all(mixed_heads.reshape(char_count, frame_count, feature_width...  37.7 us
    sub x2, other arithmetic, softmax_rows(): weights = jnp.exp(scores - row_top)  17.3 us
    unnamed x24, local copies, waits for them, and re-layouts  14.9 us
    dot_general x1, matrix products, per_device(): jnp.einsum('fhcd,fhmd->fhcm', queries, pairs[0], preferred_element_type=j...  13.9 us
    dot_general x1, matrix products, per_device(): jnp.einsum('fhcm,fhmd->cfhd', weights, pairs[1], preferred_element_type=j...  13.3 us
    optimization_barrier x1, local copies, waits for them, and re-layouts, per_device(): lax.optimization_barrier((gathered, ahead_two, behind_two, pair_own))  6.39 us
  transfers between devices with their start and end apart: 6, of which 2 were waited for; matrix products, arithmetic and copies ran while one was open for 15% of the time, Pallas kernels for 0%

profile of v11, /device:TPU:8, one launch (start us, length us, event | category | flops | bytes accessed | tf_op | source)
XLA Modules:
  0.0 266.1 jit_solution(10045898747222203768)
XLA Ops:
  6.5 0.0 copy-start
  6.5 0.0 all-gather.2.cloned.1.call-start
  6.5 1.1 dynamic-slice_bitcast_fusion.3
  7.6 0.7 pad_maximum_fusion.3
  8.4 0.0 all-gather.2.cloned.1.call-update
  8.4 0.0 copy-start.5
  8.4 0.0 copy-start.7
  8.4 8.7 %copy.36 = bf16[1024,3072]{0,1:T(8,128)(2,1)} copy(bf16[1024,3072]{1,0:T(8,128)(2,1)} %param.10) | data formatting | bytes 12582912 | tf_op args[2]
  17.1 0.0 copy-done.5
  17.1 0.3 fusion.23
  17.4 0.0 copy-done.7
  17.5 5.9 %convert_bitcast_fusion = bf16[3,4,16,128,64]{3,4,2,0,1:T(8,128)(2,1)S(1)} fusion(bf16[1024,3,16,64,1]{0,3,2,1,4:T(8,128)(2,1)} %bitcast.104, bf16[4,128,1024]{2,1,0:T(8,128)(2,1)S(1)} %copy-done.5, f32[1024]{0:T(1024)S(1)} %bitcast.116, f32[1024]{0:T(1024)S(1)} %bitcast.117, f32[4,128]{1,0:T(4,128)S(1)} %add_rsqrt_fusion.1), kind=kOutput, calls=%fused_computation.27 | convolution fusion | flops 3225419776 | bytes 10496000 | tf_op jit(solution)/shard_map/nfk,kshd->snhfd/dot_general | solution.py:79
  23.4 0.0 copy-start.2
  23.4 0.8 fusion.55
  24.2 2.9 %fusion.71 = (f32[4,16,128]{2,1,0:T(8,128)S(1)}, f32[4,16,128,128]{2,3,1,0:T(8,128)}) fusion(f32[4,16,128,128]{2,3,1,0:T(8,128)S(1)} %fusion.55), kind=kOutput, calls=%fused_computation.101 | output fusion | flops 4194431 | bytes 8421376 | tf_op jit(solution)/shard_map/sub | solution.py:30
  27.1 0.0 copy-done.2
  27.1 0.0 copy-done
  27.1 4.8 %fusion.28 = (f32[4,128]{1,0:T(4,128)S(1)}, bf16[4,128,1024]{2,1,0:T(8,128)(2,1)S(1)}) fusion(bf16[16,64,1024,1]{2,1,0,3:T(8,128)(2,1)S(1)} %bitcast.102, f32[4,16,128,128]{2,3,1,0:T(8,128)} %get-tuple-element.37, f32[4,16,128]{2,1,0:T(8,128)S(1)} %get-tuple-element.36, bf16[3,4,16,128,64]{3,4,2,0,1:T(8,128)(2,1)} %copy-done.2, f32[1024]{0:T(1024)S(1)} %bitcast.115, ...), kind=kOutput, calls=%fused_computation.36 | convolution fusion | flops 1214250496 | bytes 9476096 | tf_op jit(solution)/shard_map/nhfd,hdo->nfo/dot_general | solution.py:89
  31.9 0.0 copy-start.3
  31.9 0.4 fusion.31
  32.3 0.8 copy.38
  33.1 42.1 %all_to_all.33 = bf16[4,128,1024]{2,0,1:T(4,128)(2,1)S(1)} all-to-all(bf16[4,128,1024]{2,0,1:T(4,128)(2,1)S(1)} %copy.38), channel_id=1, replica_groups=mesh['grp'=16,'tm'=16] {'tm'}, dimensions={1} | all-to-all | bytes 2097152 | tf_op jit(solution)/shard_map/all_to_all | solution.py:98
  75.2 0.3 copy.71
  75.6 0.0 copy-done.3
  75.6 0.1 copy.40
  75.7 1.6 constant_dynamic-update-slice_fusion.4
  77.3 0.0 collective-permute-start.2
  77.3 0.8 collective-permute-start.1
  78.1 2.1 collective-permute-start
  80.2 0.0 collective-permute-done.2
  80.2 36.9 %collective-permute-done.1 = bf16[64,8,1024]{2,0,1:T(8,128)(2,1)S(1)} collective-permute-done((bf16[64,8,1024]{2,0,1:T(8,128)(2,1)S(1)}, bf16[64,8,1024]{2,0,1:T(8,128)(2,1)S(1)}, u32[]{:S(2)}, u32[]{:S(2)}) %collective-permute-start.1) | collective-permute-done | bytes 1048608 | tf_op jit(solution)/shard_map/ppermute | solution.py:16
  117.1 0.0 copy-done.6
  117.1 22.5 %collective-permute-done = bf16[64,8,1024]{2,0,1:T(8,128)(2,1)} collective-permute-done((bf16[64,8,1024]{2,0,1:T(8,128)(2,1)S(1)}, bf16[64,8,1024]{2,0,1:T(8,128)(2,1)}, u32[]{:S(2)}, u32[]{:S(2)}) %collective-permute-start) | collective-permute-done | bytes 1048608 | tf_op jit(solution)/shard_map/ppermute | solution.py:16
  139.6 6.4 %copy.44 = bf16[2048,1024]{1,0:T(8,128)(2,1)} copy(bf16[2048,1024]{0,1:T(8,128)(2,1)} %all-gather.2.cloned.1.call-done) | data formatting | bytes 8388608 | tf_op jit(solution)/shard_map/optimization_barrier | solution.py:105
  146.0 0.0 collective-permute-start.3
  146.0 2.3 constant_dynamic-update-slice_fusion.3
  148.3 3.1 %broadcast_select_fusion = (bf16[64,8,1024]{2,0,1:T(8,128)(2,1)}, bf16[320,8,1024]{2,0,1:T(8,128)(2,1)}) fusion(bf16[64,8,1024]{2,0,1:T(8,128)(2,1)} %collective-permute-done, bf16[64,8,1024]{2,0,1:T(8,128)(2,1)S(1)} %collective-permute-done.1, pred[]{:T(512)S(6)} %eq.10, bf16[320,8,1024]{2,0,1:T(8,128)(2,1)} %constant_dynamic-update-slice_fusion.3), kind=kLoop, calls=%fused_computation.74 | loop fusion | flops 524288 | bytes 4194305 | tf_op jit(solution)/shard_map/jit(_where)/select_n | solution.py:109
  151.4 0.5 collective-permute-start.4
  151.9 0.0 copy-done.8
  151.9 0.2 dynamic-slice_reduce_fusion
  152.1 0.0 copy-done.9
  152.1 0.6 gather_fusion
  152.7 0.1 add_compare_fusion
  152.8 0.1 broadcast_in_dim.13
  152.9 0.1 gt.12
  153.0 3.6 %fusion.67 = (bf16[512,1024]{1,0:T(8,128)(2,1)S(1)}, bf16[512,1024]{1,0:T(8,128)(2,1)}, bf16[512,1024]{1,0:T(8,128)(2,1)S(1)}, bf16[512,1024]{1,0:T(8,128)(2,1)S(1)}) fusion(bf16[2048,1024]{1,0:T(8,128)(2,1)} %copy.44), kind=kLoop, calls=%fused_computation.97 | loop fusion | bytes 8388608 | tf_op jit(solution)/shard_map/slice | solution.py:54
  156.6 0.0 collective-permute-done.4
  156.6 2.3 constant_dynamic-update-slice_fusion.1
  158.9 1.1 constant_dynamic-update-slice_fusion
  160.0 0.0 collective-permute-done.3
  160.0 3.6 %fusion.68 = (bf16[512,1024]{1,0:T(8,128)(2,1)S(1)}, bf16[512,1024]{1,0:T(8,128)(2,1)}, bf16[512,1024]{1,0:T(8,128)(2,1)S(1)}, bf16[512,1024]{1,0:T(8,128)(2,1)S(1)}) fusion(bf16[2048,1024]{1,0:T(8,128)(2,1)} %collective-permute-done.3), kind=kLoop, calls=%fused_computation.98 | loop fusion | bytes 8388608 | tf_op jit(solution)/shard_map/slice | solution.py:54
  163.6 1.5 pad_maximum_fusion
  165.0 1.5 pad_maximum_fusion.2
  166.5 0.2 pad_maximum_fusion.1
  166.7 3.8 %fusion.57 = bf16[16,64,64,8]{2,1,0,3:T(8,128)(2,1)} fusion(bf16[16,64,1024,1]{2,1,0,3:T(8,128)(2,1)S(1)} %bitcast.110, bf16[64,8,1024,1]{2,1,0,3:T(8,128)(2,1)S(1)} %bitcast.106), kind=kOutput, calls=%fused_computation.67 | convolution fusion | flops 1073741824 | bytes 4194304 | tf_op jit(solution)/shard_map/cfk,hdk->fhcd/dot_general | solution.py:116
  170.5 13.9 %fusion.3 = f32[8,16,64,320]{3,2,1,0:T(8,128)} fusion(bf16[16,64,1024,1]{2,1,0,3:T(8,128)(2,1)} %bitcast.109, bf16[320,8,1024]{2,0,1:T(8,128)(2,1)} %constant_dynamic-update-slice_fusion, bf16[16,64,64,8]{2,1,0,3:T(8,128)(2,1)} %fusion.57), kind=kOutput, calls=%fused_computation.7 | convolution fusion | flops 5706874880 | bytes 18874368 | tf_op jit(solution)/shard_map/fhcd,fhmd->fhcm/dot_general | solution.py:126
  184.4 14.4 %fusion.72 = (f32[8,16,64]{2,1,0:T(8,128)S(1)}, f32[8,16,64,320]{3,2,1,0:T(8,128)}) fusion(f32[8,16,64,320]{3,2,1,0:T(8,128)} %fusion.3, pred[320]{0:T(512)(128)(4,1)S(1)} %gt.12), kind=kOutput, calls=%fused_computation.102 | output fusion | flops 15728959 | bytes 21004608 | tf_op jit(solution)/shard_map/sub | solution.py:30
  198.8 13.3 %convert_bitcast_fusion.1 = bf16[64,8,16,64]{0,3,2,1:T(8,128)(2,1)S(1)} fusion(f32[8,16,64,320]{3,2,1,0:T(8,128)} %get-tuple-element.41, f32[8,16,64]{2,1,0:T(8,128)S(1)} %get-tuple-element.40, bf16[16,64,1024,1]{2,1,0,3:T(8,128)(2,1)} %bitcast.108, bf16[320,8,1024]{2,0,1:T(8,128)(2,1)} %constant_dynamic-update-slice_fusion), kind=kOutput, calls=%fused_computation.55 | convolution fusion | flops 5712642048 | bytes 18907136 | tf_op jit(solution)/shard_map/fhcm,fhmd->cfhd/dot_general | solution.py:135
  212.1 0.2 fusion.69
  212.3 1.8 maximum_select_fusion
  214.2 2.8 %copy.51 = bf16[64,8,1024]{2,1,0:T(8,128)(2,1)S(1)} copy(bf16[64,8,1024]{0,2,1:T(8,128)(2,1)} %bitcast.103) | data formatting | bytes 2097152 | tf_op jit(solution)/shard_map/reshape | solution.py:142
  216.9 37.7 %all_to_all.34 = bf16[64,8,1024]{2,1,0:T(8,128)(2,1)S(1)} all-to-all(bf16[64,8,1024]{2,1,0:T(8,128)(2,1)S(1)} %copy.51), channel_id=1, replica_groups=mesh['grp'=16,'tm'=16] {'tm'}, dimensions={0} | all-to-all | bytes 2097152 | tf_op jit(solution)/shard_map/all_to_all | solution.py:141
  254.6 4.6 %fusion.32 = bf16[4,128,1024]{2,1,0:T(8,128)(2,1)} fusion(bf16[4,128,1024]{2,1,0:T(8,128)(2,1)S(1)} %copy-done.4, bf16[512,1024]{1,0:T(8,128)(2,1)} %get-tuple-element.18, bf16[512,1024]{1,0:T(8,128)(2,1)} %get-tuple-element.14, pred[]{:T(512)S(6)} %eq.10, bf16[4,16,8,1024]{3,2,0,1:T(8,128)(2,1)S(1)} %bitcast.111, f32[1024]{0:T(1024)S(1)} %bitcast.114), kind=kOutput, calls=%fused_computation.40 | convolution fusion | flops 1085276160 | bytes 5246977 | tf_op jit(solution)/shard_map/tk,ok->to/dot_general | solution.py:148
  259.2 0.0 copy-done.1
  (12 shorter events, 0.1 us)
Async XLA Ops:
  6.5 20.6 %copy-start = (bf16[1024,1024]{1,0:T(8,128)(2,1)S(1)}, bf16[1024,1024]{1,0:T(8,128)(2,1)}, u32[]{:S(2)}) copy-start(bf16[1024,1024]{1,0:T(8,128)(2,1)} %param.11) | copy-start | bytes 6291460
  6.5 133.0 %all-gather.2.cloned.1.call-start = ((), (), s32[]{:S(2)}) async-start(), calls=%async_computation.2 | async-start | bytes 4456448 | tf_op jit(solution)/shard_map/all_gather | solution.py:43
  8.4 8.7 %copy-start.5 = (bf16[4,128,1024]{2,1,0:T(8,128)(2,1)S(1)}, bf16[4,128,1024]{2,1,0:T(8,128)(2,1)}, u32[]{:S(2)}) copy-start(bf16[4,128,1024]{2,1,0:T(8,128)(2,1)} %param.8) | copy-start | bytes 3145732
  8.4 9.0 %copy-start.7 = (f32[6,1024]{1,0:T(8,128)S(1)}, f32[6,1024]{1,0:T(8,128)}, u32[]{:S(2)}) copy-start(f32[6,1024]{1,0:T(8,128)} %param.9) | copy-start | bytes 73732
  23.4 3.7 %copy-start.2 = (bf16[3,4,16,128,64]{3,4,2,0,1:T(8,128)(2,1)}, bf16[3,4,16,128,64]{3,4,2,0,1:T(8,128)(2,1)S(1)}, u32[]{:S(2)}) copy-start(bf16[3,4,16,128,64]{3,4,2,0,1:T(8,128)(2,1)S(1)} %convert_bitcast_fusion) | copy-start | bytes 9437188
  31.9 43.7 %copy-start.3 = (bf16[4,128,1024]{2,1,0:T(8,128)(2,1)}, bf16[4,128,1024]{2,1,0:T(8,128)(2,1)S(1)}, u32[]{:S(2)}) copy-start(bf16[4,128,1024]{2,1,0:T(8,128)(2,1)S(1)} %get-tuple-element.39) | copy-start | bytes 3145732
  77.3 2.9 %collective-permute-start.2 = (bf16[64,8,1024]{2,0,1:T(8,128)(2,1)S(1)}, bf16[64,8,1024]{2,0,1:T(8,128)(2,1)S(1)}, u32[]{:S(2)}, u32[]{:S(2)}) collective-permute-start(bf16[64,8,1024]{2,0,1:T(8,128)(2,1)S(1)} %get-tuple-element.26), channel_id=1, source_target_pairs={{0,16},{16,0},{32,48},{48,32},{64,80},{80,64},{96,112},{112,96},{1... | collective-permute-start | bytes 3145736 | tf_op jit(solution)/shard_map/ppermute | solution.py:104
  77.3 39.8 %collective-permute-start.1 = (bf16[64,8,1024]{2,0,1:T(8,128)(2,1)S(1)}, bf16[64,8,1024]{2,0,1:T(8,128)(2,1)S(1)}, u32[]{:S(2)}, u32[]{:S(2)}) collective-permute-start(bf16[64,8,1024]{2,0,1:T(8,128)(2,1)S(1)} %get-tuple-element.26), channel_id=1, source_target_pairs={{224,0},{240,16},{0,32},{16,48},{32,64},{48,80},{64,96},{80,112},{... | collective-permute-start | bytes 3145736 | tf_op jit(solution)/shard_map/ppermute | solution.py:16
  78.1 61.5 %collective-permute-start = (bf16[64,8,1024]{2,0,1:T(8,128)(2,1)S(1)}, bf16[64,8,1024]{2,0,1:T(8,128)(2,1)}, u32[]{:S(2)}, u32[]{:S(2)}) collective-permute-start(bf16[64,8,1024]{2,0,1:T(8,128)(2,1)S(1)} %get-tuple-element.26), channel_id=1, source_target_pairs={{32,0},{48,16},{64,32},{80,48},{96,64},{112,80},{128,96},{144,112}... | collective-permute-start | bytes 3145736 | tf_op jit(solution)/shard_map/ppermute | solution.py:16
  80.2 36.9 %copy-start.6 = (bf16[64,8,1024]{2,0,1:T(8,128)(2,1)}, bf16[64,8,1024]{2,0,1:T(8,128)(2,1)S(1)}, u32[]{:S(2)}) copy-start(bf16[64,8,1024]{2,0,1:T(8,128)(2,1)S(1)} %collective-permute-done.2) | copy-start | bytes 3145732
  146.0 5.9 %copy-start.8 = (s32[16,4]{0,1:T(4,128)S(1)}, s32[16,4]{0,1:T(4,128)}, u32[]{:S(2)}) copy-start(s32[16,4]{0,1:T(4,128)} %param.14) | copy-start | bytes 772
  146.0 6.1 %copy-start.9 = (s32[4]{0:T(128)S(1)}, s32[4]{0:T(128)}, u32[]{:S(2)}) copy-start(s32[4]{0:T(128)} %constant.69) | copy-start | bytes 52
  146.0 14.0 %collective-permute-start.3 = (bf16[2048,1024]{1,0:T(8,128)(2,1)}, bf16[2048,1024]{1,0:T(8,128)(2,1)}, u32[]{:S(2)}, u32[]{:S(2)}) collective-permute-start(bf16[2048,1024]{1,0:T(8,128)(2,1)} %copy.44), channel_id=1, source_target_pairs={{0,16},{16,0},{32,48},{48,32},{64,80},{80,64},{96,112},{112,96},{1... | collective-permute-start | bytes 12582920 | tf_op jit(solution)/shard_map/ppermute | solution.py:49
  151.4 5.2 %collective-permute-start.4 = (bf16[64,8,1024]{2,0,1:T(8,128)(2,1)}, bf16[64,8,1024]{2,0,1:T(8,128)(2,1)}, u32[]{:S(2)}, u32[]{:S(2)}) collective-permute-start(bf16[64,8,1024]{2,0,1:T(8,128)(2,1)} %get-tuple-element.23), channel_id=1, source_target_pairs={{0,16},{16,0},{32,48},{48,32},{64,80},{80,64},{96,112},{112,96},{1... | collective-permute-start | bytes 3145736 | tf_op jit(solution)/shard_map/ppermute | solution.py:108
  214.2 40.4 %copy-start.4 = (bf16[4,128,1024]{2,1,0:T(8,128)(2,1)S(1)}, bf16[4,128,1024]{2,1,0:T(8,128)(2,1)}, u32[]{:S(2)}) copy-start(bf16[4,128,1024]{2,1,0:T(8,128)(2,1)} %copy-done.3) | copy-start | bytes 3145732
  254.6 4.6 %copy-start.1 = (bf16[1024,1024]{1,0:T(8,128)(2,1)S(1)}, bf16[1024,1024]{1,0:T(8,128)(2,1)}, u32[]{:S(2)}) copy-start(bf16[1024,1024]{1,0:T(8,128)(2,1)} %param.11) | copy-start | bytes 6291460
Sparse Core Ops, SparseCore 0:
  9.9 124.2 all-gather.1
